TPU v7x, 256 devices: a whole 4x4x8 slice. The times are simulated.
256 devices in a mesh: req: 32 (over y, z), tp: 8 (over x, core).
Axes of the slice: x: 4, y: 4, z: 8, core: 2. Of those that a mesh axis runs over, the one named last changes fastest.
Arguments:
- tokens: bfloat16 [32768, 1792], P(('req', 'tp')), may hold values from -6 to 6
- norm_gain: float32 [1792], replicated, may hold values from 0.25 to 1.75
- ffn_gain: float32 [1792], replicated, may hold values from 0.25 to 1.75
- mix_weight: bfloat16 [1792, 4, 1792], P('req', None, 'tp'), may hold values from -0.125 to 0.125
- out_weight: bfloat16 [1792, 1792], P('tp', 'req'), may hold values from -0.125 to 0.125
- ffn_weight: bfloat16 [1792, 2, 7168], P('req', None, 'tp'), may hold values from -0.125 to 0.125
- down_weight: bfloat16 [7168, 1792], P('tp', 'req'), may hold values from -0.0625 to 0.0625
- conv_taps: float32 [3, 1792], P(None, 'tp'), may hold values from -3 to 3
- past_cache: bfloat16 [32, 2, 64, 1792], P('req', None, None, 'tp'), may hold values from -210 to 210
- cached_len: int32 [32], P('req'), may hold values from 0 to 8192, as said below
Outputs:
- layer_out: bfloat16 [32768, 1792], P(('req', 'tp'))
- new_cache: bfloat16 [32, 2, 64, 1792], P('req', None, None, 'tp')
Inputs may be any that keep to these rules, and one draw needn't show every extreme that they name: `cached_len`: one request has exactly 8192 cached positions and another fewer than 64.
All inputs are finite; a program needn't handle non-finite values.
Results may differ from a plain program's by a relative error of at most 0.02.
Values may be sent and summed in bfloat16 or wider, within the bound.
No kernel may reach another device: no remote copies, remote signals or barrier semaphores. Data moves between devices by JAX's collectives and lax.ppermute only.
A program may use at most 64 MiB of HBM per device.

v0:
```python
import math

import jax
import jax.numpy as jnp
from jax import lax
from jax.sharding import PartitionSpec as P

HD = 112
WIN = 64


def normed(row_vals, gain):
    floats = row_vals.astype(jnp.float32)
    scaled = floats * lax.rsqrt(jnp.mean(floats * floats, axis=-1, keepdims=True) + 1e-05)
    return (scaled * gain).astype(jnp.bfloat16)


def window_attend(queries, key_rows, value_rows, length, window):
    row_count, head_count, head_size = queries.shape
    block_rows = min(512, row_count)
    score_scale = 1.0 / math.sqrt(head_size)

    def one_block(block_index):
        begin_row = block_index * block_rows
        query_block = lax.dynamic_slice_in_dim(queries, begin_row, block_rows, 0)
        key_block = lax.dynamic_slice_in_dim(key_rows, begin_row, block_rows + window, 0)
        value_block = lax.dynamic_slice_in_dim(value_rows, begin_row, block_rows + window, 0)
        scores = (
            jnp.einsum("qhd,khd->hqk", query_block, key_block, preferred_element_type=jnp.float32)
            * score_scale
        )
        row_ids = begin_row + jnp.arange(block_rows, dtype=jnp.int32)[:, None]
        col_ids = begin_row + jnp.arange(block_rows + window, dtype=jnp.int32)[None, :]
        usable = (col_ids > row_ids) & (col_ids <= row_ids + window) & (col_ids >= window - length)
        scores = jnp.where(usable[None], scores, -1e30)
        row_max = jnp.max(scores, axis=-1, keepdims=True)
        exponent = jnp.exp(scores - row_max)
        weights = (exponent / jnp.sum(exponent, axis=-1, keepdims=True)).astype(jnp.bfloat16)
        return jnp.einsum("hqk,khd->qhd", weights, value_block, preferred_element_type=jnp.float32)

    blocks = lax.map(one_block, jnp.arange(row_count // block_rows, dtype=jnp.int32))
    return blocks.reshape(row_count, head_count, head_size)


def mix_request(projected, cache_rows, length, tap_table, window, head_size):
    row_count, feat_width = (projected.shape[0], projected.shape[2])
    time_order = (length + jnp.arange(window, dtype=jnp.int32)) % window
    earlier = cache_rows[:, time_order]
    key_rows = jnp.concatenate([earlier[0], projected[:, 1]], axis=0)
    value_rows = jnp.concatenate([earlier[1], projected[:, 2]], axis=0)
    head_count = feat_width // head_size
    attended = window_attend(
        projected[:, 0].reshape(row_count, head_count, head_size),
        key_rows.reshape(-1, head_count, head_size),
        value_rows.reshape(-1, head_count, head_size),
        length,
        window,
    ).reshape(row_count, feat_width)
    positions = jnp.arange(window + row_count, dtype=jnp.int32)
    alive_mask = (positions >= window - length)[:, None]
    masked_values = jnp.where(alive_mask, value_rows.astype(jnp.float32), jnp.float32(0.0))
    tap_count = tap_table.shape[0]
    convolved = jnp.zeros((row_count, feat_width), jnp.float32)
    for tap_index in range(tap_count):
        begin_row = window - (tap_count - 1) + tap_index
        convolved = (
            convolved + tap_table[tap_index] * masked_values[begin_row : begin_row + row_count]
        )
    mixed_heads = (attended + projected[:, 3].astype(jnp.float32) * convolved).astype(jnp.bfloat16)
    slot_source = (
        row_count - window + (jnp.arange(window, dtype=jnp.int32) - length - row_count) % window
    )
    renewed = jnp.stack([projected[:, 1], projected[:, 2]])[:, slot_source]
    return (mixed_heads, renewed)


def add_rows(left, shard_piece):
    return jnp.dot(
        left, shard_piece.reshape(shard_piece.shape[0], -1), preferred_element_type=jnp.float32
    )


def local(
    tokens,
    norm_gain,
    ffn_gain,
    mix_weight,
    out_weight,
    ffn_weight,
    down_weight,
    conv_taps,
    past_cache,
    cached_len,
):
    feat_width = mix_weight.shape[2]
    ffn_width = ffn_weight.shape[2]
    normed_all = lax.all_gather(normed(tokens, norm_gain), "tp", axis=0, tiled=True)
    row_total = normed_all.shape[0]
    projected = add_rows(normed_all, lax.all_gather(mix_weight, "req", axis=0, tiled=True))
    projected = projected.astype(jnp.bfloat16).reshape(row_total, 4, feat_width)
    mixed_heads, renewed = mix_request(projected, past_cache[0], cached_len[0], conv_taps, WIN, HD)
    out_columns = lax.all_gather(out_weight, "req", axis=1, tiled=True)
    attn_part = lax.psum_scatter(
        jnp.dot(mixed_heads, out_columns, preferred_element_type=jnp.float32).astype(jnp.bfloat16),
        "tp",
        scatter_dimension=0,
        tiled=True,
    ).astype(jnp.float32)
    residual = (tokens.astype(jnp.float32) + attn_part).astype(jnp.bfloat16)
    ffn_in = lax.all_gather(normed(residual, ffn_gain), "tp", axis=0, tiled=True)
    gate_up = add_rows(ffn_in, lax.all_gather(ffn_weight, "req", axis=0, tiled=True))
    down_columns = lax.all_gather(down_weight, "req", axis=1, tiled=True)
    activated = (jax.nn.silu(gate_up[:, :ffn_width]) * gate_up[:, ffn_width:]).astype(jnp.bfloat16)
    ffn_part = lax.psum_scatter(
        jnp.dot(activated, down_columns, preferred_element_type=jnp.float32).astype(jnp.bfloat16),
        "tp",
        scatter_dimension=0,
        tiled=True,
    ).astype(jnp.float32)
    layer_out = (residual.astype(jnp.float32) + ffn_part).astype(jnp.bfloat16)
    return (layer_out, renewed[None])


def solution(mesh):
    in_specs = (
        P(("req", "tp"), None),
        P(),
        P(),
        P("req", None, "tp"),
        P("tp", "req"),
        P("req", None, "tp"),
        P("tp", "req"),
        P(None, "tp"),
        P("req", None, None, "tp"),
        P("req"),
    )
    out_specs = (P(("req", "tp"), None), P("req", None, None, "tp"))
    return jax.shard_map(local, mesh=mesh, in_specs=in_specs, out_specs=out_specs, check_vma=False)
```

profile of v0, /device:TPU:1, one launch (start us, length us, event | category | flops | bytes accessed | tf_op | source)
XLA Modules:
  0.0 474.2 jit_solution(1445607899470987340)
XLA Ops:
  8.0 1.2 fusion.43
  9.2 2.0 fusion.45
  13.9 44.4 %all_gather.20 = bf16[224,1792]{0,1:T(8,128)(2,1)S(1)} all-gather(bf16[224,56]{0,1:T(8,128)(2,1)} %param.16), channel_id=1, replica_groups=mesh['req'=32,'tp'=8] {'req'}, dimensions={1}, use_global_device_ids=true | all-gather | bytes 827904 | tf_op jit(solution)/shard_map/all_gather | solution.py:102
  58.3 34.1 %all-gather.8.cloned.1.call-done = bf16[1792,4,224]{2,1,0:T(4,128)(2,1)} async-done(((bf16[56,4,224]{2,1,0:T(4,128)(2,1)}), bf16[1792,4,224]{2,1,0:T(4,128)(2,1)}) %all-gather.8.cloned.1.call-update) | async-done | bytes 3211280 | tf_op jit(solution)/shard_map/all_gather | solution.py:99
  92.4 6.8 %copy.37 = bf16[1792,4,224]{0,2,1:T(8,128)(2,1)} copy(bf16[1792,4,224]{2,1,0:T(4,128)(2,1)} %all-gather.8.cloned.1.call-done) | data formatting | bytes 6422528 | tf_op jit(solution)/shard_map/all_gather | solution.py:99
  99.1 28.7 %all-gather.6.cloned.1.call-done = bf16[1024,1792]{1,0:T(8,128)(2,1)} async-done(((bf16[128,1792]{1,0:T(8,128)(2,1)}), bf16[1024,1792]{1,0:T(8,128)(2,1)}) %all-gather.6.cloned.1.call-update) | async-done | bytes 3670032 | tf_op jit(solution)/shard_map/all_gather | solution.py:97
  127.8 6.5 %convolution_convert_fusion.2 = bf16[1024,896]{0,1:T(8,128)(2,1)S(1)} fusion(bf16[1024,1792]{1,0:T(8,128)(2,1)} %all-gather.6.cloned.1.call-done, bf16[1792,896]{0,1:T(8,128)(2,1)} %bitcast.62), kind=kOutput, calls=%fused_computation.34 | convolution fusion | flops 3289251840 | bytes 8716288 | tf_op jit(solution)/shard_map/dot_general | solution.py:78
  134.3 1.2 copy-done.2
  135.6 1.1 slice_bitcast_fusion.2
  137.7 1.0 pad_maximum_fusion.2
  138.7 32.4 %while.12 = (s32[]{:T(128)}, f32[2,512,2,112]{1,0,3,2:T(2,128)}, s32[2]{0:T(128)S(1)}, bf16[1088,2,112]{0,2,1:T(8,128)(2,1)}, s32[]{:T(128)}, /*index=5*/bf16[10...) while((s32[]{:T(128)}, f32[2,512,2,112]{1,0,3,2:T(2,128)}, ...), condition=%wide.region_4.5_spmd, body=%wide.region_1.4_spmd.sunk | while | flops 402854720 | bytes 4521316 | solution.py:41
  140.3 2.2 fusion.90
  142.5 2.7 convolution_bitcast_fusion.2
  145.8 9.2 %dynamic_update_slice.7 = f32[2,512,2,112]{1,0,3,2:T(2,128)} dynamic-update-slice(f32[2,512,2,112]{1,0,3,2:T(2,128)} %get-tuple-element.181, f32[1,512,2,112]{1,0,3,2:T(1,128)S(1)} %copy.57, s32[]{:T(128)} %get-tuple-element.180, s32[]{:T(128)} %constant.82.clone.1..sunk, s32[]{:T(128)} %constant.82.clone.1..sunk, s32[]{:T(128)} %constant.82.clone.1..sunk) | dynamic-update-slice | bytes 917508 | tf_op jit(solution)/shard_map/while/body/jit(dynamic_update_index_in_dim)/dynamic_update_slice | solution.py:41
  156.5 2.2 fusion.90
  158.7 2.7 convolution_bitcast_fusion.2
  161.9 9.2 %dynamic_update_slice.7 = f32[2,512,2,112]{1,0,3,2:T(2,128)} dynamic-update-slice(f32[2,512,2,112]{1,0,3,2:T(2,128)} %get-tuple-element.181, f32[1,512,2,112]{1,0,3,2:T(1,128)S(1)} %copy.57, s32[]{:T(128)} %get-tuple-element.180, s32[]{:T(128)} %constant.82.clone.1..sunk, s32[]{:T(128)} %constant.82.clone.1..sunk, s32[]{:T(128)} %constant.82.clone.1..sunk) | dynamic-update-slice | bytes 917508 | tf_op jit(solution)/shard_map/while/body/jit(dynamic_update_index_in_dim)/dynamic_update_slice | solution.py:41
  171.1 1.3 copy.52
  172.7 5.0 %convolution_convert_fusion.1 = bf16[1024,1792]{1,0:T(8,128)(2,1)} fusion(bf16[224,1792]{0,1:T(8,128)(2,1)S(1)} %all_gather.20, f32[1024,224]{0,1:T(8,128)S(1)} %bitcast.61, f32[1088,224]{0,1:T(8,128)S(1)} %convert_select_fusion, bf16[1024,4,224]{0,2,1:T(8,128)(2,1)} %bitcast.64, f32[224]{0:T(256)S(1)} %bitcast.76, f32[224]{0:T(256)S(1)} %bitcast.77, ...), kind=kOutput, calls=%fused_computation.30 | convolution fusion | flops 825982976 | bytes 8719360 | tf_op jit(solution)/shard_map/dot_general | solution.py:104
  178.3 35.6 %reduce-scatter.3.cloned.1.call-done = bf16[128,1792]{1,0:T(8,128)(2,1)} async-done(((bf16[1024,1792]{1,0:T(8,128)(2,1)}), bf16[128,1792]{1,0:T(8,128)(2,1)}) %reduce-scatter.3.cloned.1.call-update) | async-done | bytes 458768 | tf_op jit(solution)/shard_map/reduce_scatter | solution.py:103
  213.9 1.3 fusion.47
  215.2 2.0 fusion.49
  218.0 88.9 %all-gather.12.cloned.1.call-done = bf16[1792,2,896]{2,1,0:T(2,128)(2,1)} async-done(((bf16[56,2,896]{2,1,0:T(2,128)(2,1)}), bf16[1792,2,896]{2,1,0:T(2,128)(2,1)}) %all-gather.12.cloned.1.call-update) | async-done | bytes 6422544 | tf_op jit(solution)/shard_map/all_gather | solution.py:111
  306.9 6.8 %copy.53 = bf16[224,8,2,896]{3,1,2,0:T(8,128)(2,1)} copy(bf16[224,8,2,896]{3,2,1,0:T(2,128)(2,1)} %bitcast.59) | data formatting | bytes 12845056
  313.8 25.7 %all-gather.10.cloned.1.call-done = bf16[1024,1792]{1,0:T(8,128)(2,1)} async-done(((bf16[128,1792]{1,0:T(8,128)(2,1)}), bf16[1024,1792]{1,0:T(8,128)(2,1)}) %all-gather.10.cloned.1.call-update) | async-done | bytes 3670032 | tf_op jit(solution)/shard_map/all_gather | solution.py:110
  339.5 12.2 %fusion.72 = f32[1024,1792]{1,0:T(8,128)} fusion(bf16[1024,1792]{1,0:T(8,128)(2,1)} %all-gather.10.cloned.1.call-done, bf16[1792,1792]{1,0:T(8,128)(2,1)} %bitcast.60), kind=kOutput, calls=%fused_computation.90 | convolution fusion | flops 6576668672 | bytes 17432576 | tf_op jit(solution)/shard_map/dot_general | solution.py:78
  351.7 66.0 %all-gather.14.cloned.1.call-done = bf16[896,1792]{0,1:T(8,128)(2,1)} async-done(((bf16[896,56]{0,1:T(8,128)(2,1)}), bf16[896,1792]{0,1:T(8,128)(2,1)}) %all-gather.14.cloned.1.call-update) | async-done | bytes 3211280 | tf_op jit(solution)/shard_map/all_gather | solution.py:112
  417.7 10.4 %convolution_convert_fusion = bf16[1024,1792]{1,0:T(8,128)(2,1)} fusion(bf16[896,1792]{0,1:T(8,128)(2,1)} %all-gather.14.cloned.1.call-done, f32[1024,1792]{1,0:T(8,128)} %fusion.72), kind=kOutput, calls=%fused_computation.29 | convolution fusion | flops 3295674368 | bytes 14221312 | tf_op jit(solution)/shard_map/dot_general | solution.py:115
  429.8 3.4 pad_maximum_fusion
  433.2 1.9 gather_fusion.1
  435.8 29.6 %reduce-scatter.5.cloned.1.call-done = bf16[128,1792]{1,0:T(8,128)(2,1)} async-done(((bf16[1024,1792]{1,0:T(8,128)(2,1)}), bf16[128,1792]{1,0:T(8,128)(2,1)}) %reduce-scatter.5.cloned.1.call-update) | async-done | bytes 458768 | tf_op jit(solution)/shard_map/reduce_scatter | solution.py:114
  465.4 2.0 fusion.50
  (54 shorter events, 10.7 us)
Async XLA Ops:
  7.2 51.1 %copy-start.4 = (f32[3,224]{1,0:T(4,128)S(1)}, f32[3,224]{1,0:T(4,128)}, u32[]{:S(2)}) copy-start(f32[3,224]{1,0:T(4,128)} %param.19) | copy-start | bytes 8068
  7.2 85.2 %all-gather.8.cloned.1.call-start = ((), (), s32[]{:S(2)}) async-start(), calls=%async_computation.3 | async-start | bytes 3784704 | tf_op jit(solution)/shard_map/all_gather | solution.py:99
  7.9 119.9 %all-gather.6.cloned.1.call-start = ((), (), s32[]{:S(2)}) async-start(), calls=%async_computation.2 | async-start | bytes 4128768 | tf_op jit(solution)/shard_map/all_gather | solution.py:97
  11.1 202.8 %reduce-scatter.3.cloned.1.call-start = ((), (), s32[]{:S(2)}) async-start(), calls=%async_computation.4 | async-start | bytes 4128768 | tf_op jit(solution)/shard_map/reduce_scatter | solution.py:103
  134.3 1.3 copy-start.2
  177.7 36.3 %copy-start = (bf16[128,1792]{1,0:T(8,128)(2,1)S(1)}, bf16[128,1792]{1,0:T(8,128)(2,1)}, u32[]{:S(2)}) copy-start(bf16[128,1792]{1,0:T(8,128)(2,1)} %param.12) | copy-start | bytes 1376260
  177.7 37.5 %copy-start.3 = (f32[1792]{0:T(1024)S(1)}, f32[1792]{0:T(1024)}, u32[]{:S(2)}) copy-start(f32[1792]{0:T(1024)} %param.14) | copy-start | bytes 21508
  177.7 129.2 %all-gather.12.cloned.1.call-start = ((), (), s32[]{:S(2)}) async-start(), calls=%async_computation.6 | async-start | bytes 6623232 | tf_op jit(solution)/shard_map/all_gather | solution.py:111
  178.3 161.2 %all-gather.10.cloned.1.call-start = ((), (), s32[]{:S(2)}) async-start(), calls=%async_computation.5 | async-start | bytes 4128768 | tf_op jit(solution)/shard_map/all_gather | solution.py:110
  217.2 200.5 %all-gather.14.cloned.1.call-start = ((), (), s32[]{:S(2)}) async-start(), calls=%async_computation.7 | async-start | bytes 3311616 | tf_op jit(solution)/shard_map/all_gather | solution.py:112
  217.8 247.6 %reduce-scatter.5.cloned.1.call-start = ((), (), s32[]{:S(2)}) async-start(), calls=%async_computation.8 | async-start | bytes 4128768 | tf_op jit(solution)/shard_map/reduce_scatter | solution.py:114
  428.1 37.3 %copy-start.1 = (bf16[128,1792]{1,0:T(8,128)(2,1)S(1)}, bf16[128,1792]{1,0:T(8,128)(2,1)}, u32[]{:S(2)}) copy-start(bf16[128,1792]{1,0:T(8,128)(2,1)} %reduce-scatter.3.cloned.1.call-done) | copy-start | bytes 1376260
Sparse Core Ops, SparseCore 0:
  10.6 81.7 all-gather.7
  94.8 32.9 all-gather.5
  177.8 36.0 reduce-scatter.2
  216.4 90.4 all-gather.11
  309.2 30.2 all-gather.9
  341.9 75.6 all-gather.13
  428.2 37.1 reduce-scatter.4
where the time goes:
time: 478 us; the launch traced here: 474 us
  waiting for transfers between devices  310 us (65%)
  blocking collectives  44.4 us (9%)
  local copies, waits for them, and re-layouts  44.1 us (9%)
  matrix products  44 us (9%)
  between operations  14.9 us (3%)
  other arithmetic  14.8 us (3%)
    all_gather x1, waiting for transfers between devices, local(): lax.all_gather(ffn_weight, 'req', axis=0, tiled=True)  88.9 us
    all_gather x1, waiting for transfers between devices, local(): down_columns = lax.all_gather(down_weight, 'req', axis=1, tiled=True)  66 us
    all_gather x1, blocking collectives, local(): out_columns = lax.all_gather(out_weight, 'req', axis=1, tiled=True)  44.4 us
    reduce_scatter x1, waiting for transfers between devices, local(): lax.psum_scatter(jnp.dot(mixed_heads, out_columns, preferred_element_type...  35.6 us
    all_gather x1, waiting for transfers between devices, local(): lax.all_gather(mix_weight, 'req', axis=0, tiled=True)  34.1 us
    reduce_scatter x1, waiting for transfers between devices, local(): lax.psum_scatter(jnp.dot(activated, down_columns, preferred_element_type=...  29.6 us
    all_gather x1, waiting for transfers between devices, local(): lax.all_gather(normed(tokens, norm_gain), 'tp', axis=0, tiled=True)  28.7 us
    all_gather x1, waiting for transfers between devices, local(): lax.all_gather(normed(residual, ffn_gain), 'tp', axis=0, tiled=True)  25.7 us
  transfers between devices with their start and end apart: 7, of which 7 were waited for; matrix products, arithmetic and copies ran while one was open for 9% of the time, Pallas kernels for 0%

commit v1 on v0

v1 whole, which is shorter than its diff:
```python
import math

import jax
import jax.numpy as jnp
from jax import lax
from jax.sharding import PartitionSpec as P

HD = 112
WIN = 64


def normed(row_vals, gain):
    floats = row_vals.astype(jnp.float32)
    scaled = floats * lax.rsqrt(jnp.mean(floats * floats, axis=-1, keepdims=True) + 1e-05)
    return (scaled * gain).astype(jnp.bfloat16)


def window_attend(queries, key_rows, value_rows, length, window):
    row_count, head_count, head_size = queries.shape
    nb = row_count // window
    score_scale = 1.0 / math.sqrt(head_size)
    qb = queries.reshape(nb, window, head_count, head_size)

    def blocks(rows):
        lo = rows[:row_count].reshape(nb, window, head_count, head_size)
        hi = rows[window:].reshape(nb, window, head_count, head_size)
        return jnp.concatenate([lo, hi], axis=1)

    kb = blocks(key_rows)
    vb = blocks(value_rows)
    scores = (
        jnp.einsum("bqhd,bkhd->bhqk", qb, kb, preferred_element_type=jnp.float32) * score_scale
    )
    i = jnp.arange(window, dtype=jnp.int32)[:, None]
    j = jnp.arange(2 * window, dtype=jnp.int32)[None, :]
    b = jnp.arange(nb, dtype=jnp.int32)[:, None, None]
    usable = (j > i)[None] & (j <= i + window)[None] & (b * window + j >= window - length)
    scores = jnp.where(usable[:, None], scores, -1e30)
    row_max = jnp.max(scores, axis=-1, keepdims=True)
    exponent = jnp.exp(scores - row_max)
    weights = (exponent / jnp.sum(exponent, axis=-1, keepdims=True)).astype(jnp.bfloat16)
    out = jnp.einsum("bhqk,bkhd->bqhd", weights, vb, preferred_element_type=jnp.float32)
    return out.reshape(row_count, head_count, head_size)


def mix_request(projected, cache_rows, length, tap_table, window, head_size):
    row_count, feat_width = (projected.shape[0], projected.shape[2])
    time_order = (length + jnp.arange(window, dtype=jnp.int32)) % window
    earlier = cache_rows[:, time_order]
    key_rows = jnp.concatenate([earlier[0], projected[:, 1]], axis=0)
    value_rows = jnp.concatenate([earlier[1], projected[:, 2]], axis=0)
    head_count = feat_width // head_size
    attended = window_attend(
        projected[:, 0].reshape(row_count, head_count, head_size),
        key_rows.reshape(-1, head_count, head_size),
        value_rows.reshape(-1, head_count, head_size),
        length,
        window,
    ).reshape(row_count, feat_width)
    positions = jnp.arange(window + row_count, dtype=jnp.int32)
    alive_mask = (positions >= window - length)[:, None]
    masked_values = jnp.where(alive_mask, value_rows.astype(jnp.float32), jnp.float32(0.0))
    tap_count = tap_table.shape[0]
    convolved = jnp.zeros((row_count, feat_width), jnp.float32)
    for tap_index in range(tap_count):
        begin_row = window - (tap_count - 1) + tap_index
        convolved = (
            convolved + tap_table[tap_index] * masked_values[begin_row : begin_row + row_count]
        )
    mixed_heads = (attended + projected[:, 3].astype(jnp.float32) * convolved).astype(jnp.bfloat16)
    slot_source = (
        row_count - window + (jnp.arange(window, dtype=jnp.int32) - length - row_count) % window
    )
    renewed = jnp.stack([projected[:, 1], projected[:, 2]])[:, slot_source]
    return (mixed_heads, renewed)


def gather_weights(mix_weight, out_weight, ffn_weight, down_weight):
    rows = mix_weight.shape[0]
    pieces = [
        mix_weight.reshape(rows, -1),
        ffn_weight.reshape(rows, -1),
        down_weight.T,
        out_weight.T,
    ]
    widths = [p.shape[1] for p in pieces]
    got = lax.all_gather(jnp.concatenate(pieces, axis=1), "req", axis=0, tiled=True)
    parts = []
    start = 0
    for w in widths:
        parts.append(got[:, start : start + w])
        start += w
    return parts


def tp_gather(x):
    n = lax.axis_size("tp")
    return lax.all_to_all(jnp.tile(x, (n, 1)), "tp", 0, 0, tiled=True)


def tp_sum_scatter(x):
    n = lax.axis_size("tp")
    got = lax.all_to_all(x, "tp", 0, 0, tiled=True)
    return got.reshape((n, -1) + x.shape[1:]).astype(jnp.float32).sum(axis=0)


def local(
    tokens,
    norm_gain,
    ffn_gain,
    mix_weight,
    out_weight,
    ffn_weight,
    down_weight,
    conv_taps,
    past_cache,
    cached_len,
):
    feat_width = mix_weight.shape[2]
    ffn_width = ffn_weight.shape[2]
    mix_all, ffn_all, down_t, out_t = gather_weights(mix_weight, out_weight, ffn_weight, down_weight)
    normed_all = tp_gather(normed(tokens, norm_gain))
    row_total = normed_all.shape[0]
    projected = jnp.dot(normed_all, mix_all, preferred_element_type=jnp.float32)
    projected = projected.astype(jnp.bfloat16).reshape(row_total, 4, feat_width)
    mixed_heads, renewed = mix_request(projected, past_cache[0], cached_len[0], conv_taps, WIN, HD)
    attn_full = lax.dot_general(
        mixed_heads, out_t, (((1,), (1,)), ((), ())), preferred_element_type=jnp.float32
    )
    attn_part = tp_sum_scatter(attn_full.astype(jnp.bfloat16))
    residual = (tokens.astype(jnp.float32) + attn_part).astype(jnp.bfloat16)
    ffn_in = tp_gather(normed(residual, ffn_gain))
    gate_up = jnp.dot(ffn_in, ffn_all, preferred_element_type=jnp.float32)
    activated = (jax.nn.silu(gate_up[:, :ffn_width]) * gate_up[:, ffn_width:]).astype(jnp.bfloat16)
    ffn_full = lax.dot_general(
        activated, down_t, (((1,), (1,)), ((), ())), preferred_element_type=jnp.float32
    )
    ffn_part = tp_sum_scatter(ffn_full.astype(jnp.bfloat16))
    layer_out = (residual.astype(jnp.float32) + ffn_part).astype(jnp.bfloat16)
    return (layer_out, renewed[None])


def solution(mesh):
    in_specs = (
        P(("req", "tp"), None),
        P(),
        P(),
        P("req", None, "tp"),
        P("tp", "req"),
        P("req", None, "tp"),
        P("tp", "req"),
        P(None, "tp"),
        P("req", None, None, "tp"),
        P("req"),
    )
    out_specs = (P(("req", "tp"), None), P("req", None, None, "tp"))
    return jax.shard_map(local, mesh=mesh, in_specs=in_specs, out_specs=out_specs, check_vma=False)
```

time: 478 us -> 343 us (0.72)
  waiting for transfers between devices: 310 us -> 153 us
  blocking collectives: 44.4 us -> 95.9 us
  local copies, waits for them, and re-layouts: 44.1 us -> 20 us
  starting transfers between devices: 0.46 us -> 13.2 us
  matrix products: 44 us -> 34 us
    all_gather x5 -> x1, waiting for transfers between devices: 243 us -> 73.7 us  [gather_weights(): lax.all_gather(jnp.concatenate(pieces, axis=1), 'req', axis=0, tiled=True)]
    all_to_all x0 -> x2, blocking collectives: none -> 95.9 us  [the longest x1 48.7 us: tp_sum_scatter(): got = lax.all_to_all(x, 'tp', 0, 0, tiled=True)]
    all_to_all x0 -> x2, waiting for transfers between devices: none -> 78.9 us  [the longest x1 41.3 us: tp_gather(): return lax.all_to_all(jnp.tile(x, (n, 1)), 'tp', 0, 0, tiled=True)]
    reduce_scatter x2 -> x0, waiting for transfers between devices: 65.2 us -> none  [the longest x1 35.6 us: local(): lax.psum_scatter(jnp.dot(mixed_heads, out_columns, preferred_element_type...]
    all_gather x1 -> x0, blocking collectives: 44.4 us -> none  [local(): out_columns = lax.all_gather(out_weight, 'req', axis=1, tiled=True)]
    dynamic_update_slice x4 -> x0, local copies, waits for them, and re-layouts: 19.3 us -> none  [window_attend(): lax.map(one_block, jnp.arange(row_count // block_rows, dtype=jnp.int32))]
    all_to_all x0 -> x2, starting transfers between devices: none -> 13.2 us  [the longest x1 7.76 us: tp_gather(): return lax.all_to_all(jnp.tile(x, (n, 1)), 'tp', 0, 0, tiled=True)]
    dot_general x6, matrix products: 39.5 us -> 31.5 us  [the longest x1 6.81 us: local(): gate_up = jnp.dot(ffn_in, ffn_all, preferred_element_type=jnp.float32)]
  transfers between devices with their start and end apart: 7 -> 3, of which waited for: 7 -> 3; matrix products, arithmetic and copies ran while one was open for 9% -> 3% of each run, Pallas kernels for 0% -> 0%
where the time goes in v1:
time: 343 us
  waiting for transfers between devices  153 us (45%)
  blocking collectives  95.9 us (28%)
  matrix products  34 us (10%)
  local copies, waits for them, and re-layouts  20 us (6%)
  between operations  15 us (4%)
  starting transfers between devices  13.2 us (4%)
  other arithmetic  11.9 us (3%)
    all_gather x1, waiting for transfers between devices, gather_weights(): lax.all_gather(jnp.concatenate(pieces, axis=1), 'req', axis=0, tiled=True)  73.7 us
    all_to_all x1, blocking collectives, tp_sum_scatter(): got = lax.all_to_all(x, 'tp', 0, 0, tiled=True)  48.7 us
    all_to_all x1, blocking collectives, tp_gather(): return lax.all_to_all(jnp.tile(x, (n, 1)), 'tp', 0, 0, tiled=True)  47.2 us
    all_to_all x1, waiting for transfers between devices, tp_gather(): return lax.all_to_all(jnp.tile(x, (n, 1)), 'tp', 0, 0, tiled=True)  41.3 us
    all_to_all x1, waiting for transfers between devices, tp_sum_scatter(): got = lax.all_to_all(x, 'tp', 0, 0, tiled=True)  37.6 us
    all_to_all x1, starting transfers between devices, tp_gather(): return lax.all_to_all(jnp.tile(x, (n, 1)), 'tp', 0, 0, tiled=True)  7.76 us
  transfers between devices with their start and end apart: 3, of which 3 were waited for; matrix products, arithmetic and copies ran while one was open for 3% of the time, Pallas kernels for 0%

profile of v1, /device:TPU:1, one launch (start us, length us, event | category | flops | bytes accessed | tf_op | source)
XLA Modules:
  0.0 342.7 jit_solution(4850070380336900980)
XLA Ops:
  7.2 1.0 reshape.257
  8.3 1.0 copy.55
  9.2 1.7 pad_maximum_fusion.3
  11.0 1.2 fusion.20
  12.2 1.2 fusion.22
  13.4 2.0 tile.4
  15.4 7.8 %all-to-all-start = ((bf16[8,128,1792]{2,1,0:T(8,128)(2,1)}), bf16[8,128,1792]{2,1,0:T(8,128)(2,1)}, u32[]{:S(2)}, u32[]{:S(2)}) async-start(bf16[8,128,1792]{2,1,0:T(8,128)(2,1)} %tile.4), calls=%async_computation | async-start | bytes 7340032 | tf_op jit(solution)/shard_map/all_to_all | solution.py:98
  25.2 41.3 %all-to-all-done = bf16[8,128,1792]{2,1,0:T(8,128)(2,1)} async-done(((bf16[8,128,1792]{2,1,0:T(8,128)(2,1)}), bf16[8,128,1792]{2,1,0:T(8,128)(2,1)}, u32[]{:S(2)}, u32[]{:S(2)}) %all-to-all-start) | async-done | bytes 3670048 | tf_op jit(solution)/shard_map/all_to_all | solution.py:98
  66.5 73.7 %all-gather.2.cloned.1.call-done = bf16[1792,3808]{1,0:T(8,128)(2,1)} async-done(((bf16[56,3808]{1,0:T(8,128)(2,1)}), bf16[1792,3808]{1,0:T(8,128)(2,1)}) %all-gather.2.cloned.1.call-update) | async-done | bytes 13647888 | tf_op jit(solution)/shard_map/all_gather | solution.py:87
  140.2 6.6 %fusion.9 = bf16[1024,896]{0,1:T(8,128)(2,1)S(1)} fusion(bf16[1024,1792]{1,0:T(8,128)(2,1)} %bitcast.4, bf16[1792,3808]{1,0:T(8,128)(2,1)} %all-gather.2.cloned.1.call-done), kind=kOutput, calls=%fused_computation.15 | convolution fusion | flops 3289251840 | bytes 8716288 | tf_op jit(solution)/shard_map/dot_general | solution.py:124
  146.7 1.2 slice_bitcast_fusion
  149.0 1.5 reshape.281
  150.5 1.7 reshape.283
  152.5 2.5 fusion.63
  155.0 3.0 fusion.14
  158.9 1.2 copy.28
  160.1 1.2 copy.29
  161.4 1.0 copy.54
  162.4 6.3 %convolution_bitcast_fusion = f32[16,64,2,112]{3,1,2,0:T(8,128)S(1)} fusion(bf16[16,64,2,112]{1,3,2,0:T(8,128)(2,1)} %copy.29, bf16[16,64,2,112]{1,3,2,0:T(8,128)(2,1)} %copy.28, f32[16,2,64]{2,1,0:T(2,128)S(1)} %fusion.63, f32[16,2,64,128]{3,2,1,0:T(8,128)} %fusion.14), kind=kOutput, calls=%fused_computation.26 | convolution fusion | flops 61343872 | bytes 2891776 | tf_op jit(solution)/shard_map/bhqk,bkhd->bqhd/dot_general | solution.py:42
  168.6 0.8 copy.37
  170.3 2.9 convolution_convert_fusion.1
  173.2 48.7 %all_to_all.36 = bf16[8,128,1792]{2,1,0:T(8,128)(2,1)S(1)} all-to-all(bf16[8,128,1792]{2,1,0:T(8,128)(2,1)S(1)} %bitcast.59), channel_id=1, replica_groups=mesh['req'=32,'tp'=8] {'tp'}, dimensions={0} | all-to-all | bytes 7340032 | tf_op jit(solution)/shard_map/all_to_all | solution.py:103
  223.6 47.2 %all_to_all.37 = bf16[8,128,1792]{2,1,0:T(8,128)(2,1)S(1)} all-to-all(bf16[8,128,1792]{2,1,0:T(8,128)(2,1)S(1)} %tile.5), channel_id=1, replica_groups=mesh['req'=32,'tp'=8] {'tp'}, dimensions={0} | all-to-all | bytes 7340032 | tf_op jit(solution)/shard_map/all_to_all | solution.py:98
  270.8 6.8 %fusion.1 = f32[1024,1792]{1,0:T(8,128)S(1)} fusion(bf16[1024,1792]{1,0:T(8,128)(2,1)S(1)} %bitcast.60, bf16[1792,3808]{1,0:T(8,128)(2,1)S(1)} %bitcast.76), kind=kOutput, calls=%fused_computation.5 | convolution fusion | flops 6576668672 | bytes 17432576 | tf_op jit(solution)/shard_map/dot_general | solution.py:133
  277.7 6.0 %convolution_convert_fusion = bf16[1024,1792]{1,0:T(8,128)(2,1)} fusion(bf16[1792,3808]{1,0:T(8,128)(2,1)S(1)} %bitcast.76, f32[1024,1792]{1,0:T(8,128)S(1)} %fusion.1), kind=kOutput, calls=%fused_computation.7 | convolution fusion | flops 3295674368 | bytes 14221312 | tf_op jit(solution)/shard_map/dot_general | solution.py:135
  283.6 5.4 %all-to-all-start.3 = ((bf16[8,128,1792]{2,1,0:T(8,128)(2,1)}), bf16[8,128,1792]{2,1,0:T(8,128)(2,1)}, u32[]{:S(2)}, u32[]{:S(2)}) async-start(bf16[8,128,1792]{2,1,0:T(8,128)(2,1)} %bitcast.58), calls=%async_computation.3 | async-start | bytes 7340032 | tf_op jit(solution)/shard_map/all_to_all | solution.py:103
  289.1 0.9 copy.40
  289.9 0.8 copy.41
  290.7 2.6 pad_maximum_fusion
  294.7 37.6 %all-to-all-done.3 = bf16[8,128,1792]{2,1,0:T(8,128)(2,1)} async-done(((bf16[8,128,1792]{2,1,0:T(8,128)(2,1)}), bf16[8,128,1792]{2,1,0:T(8,128)(2,1)}, u32[]{:S(2)}, u32[]{:S(2)}) %all-to-all-start.3) | async-done | bytes 3670048 | tf_op jit(solution)/shard_map/all_to_all | solution.py:103
  332.4 2.6 convert_reduce_fusion
  335.0 0.8 fusion.27
  (56 shorter events, 7.3 us)
Async XLA Ops:
  7.2 133.0 %all-gather.2.cloned.1.call-start = ((), (), s32[]{:S(2)}) async-start(), calls=%async_computation.4 | async-start | bytes 14192640 | tf_op jit(solution)/shard_map/all_gather | solution.py:87
  15.4 8.4 %copy-start.3 = (bf16[1,2,64,224]{3,2,1,0:T(8,128)(2,1)S(1)}, bf16[1,2,64,224]{3,2,1,0:T(8,128)(2,1)}, u32[]{:S(2)}) copy-start(bf16[1,2,64,224]{3,2,1,0:T(8,128)(2,1)} %param.18) | copy-start | bytes 172036
  15.4 9.6 %copy-start.5 = (f32[3,224]{1,0:T(4,128)S(1)}, f32[3,224]{1,0:T(4,128)}, u32[]{:S(2)}) copy-start(f32[3,224]{1,0:T(4,128)} %param.17) | copy-start | bytes 8068
  15.4 51.1 %all-to-all-start = ((bf16[8,128,1792]{2,1,0:T(8,128)(2,1)}), bf16[8,128,1792]{2,1,0:T(8,128)(2,1)}, u32[]{:S(2)}, u32[]{:S(2)}) async-start(bf16[8,128,1792]{2,1,0:T(8,128)(2,1)} %tile.4), calls=%async_computation | async-start | bytes 7340032 | tf_op jit(solution)/shard_map/all_to_all | solution.py:98
  152.4 5.5 %copy-start.2 = (bf16[1024,1,224]{0,2,1:T(8,128)(2,1)S(1)}, bf16[1024,1,224]{0,2,1:T(8,128)(2,1)}, u32[]{:S(2)}) copy-start(bf16[1024,1,224]{0,2,1:T(8,128)(2,1)} %get-tuple-element.10) | copy-start | bytes 1376260
  158.0 3.4 copy-start.1
  170.3 100.5 %slice-start = ((s8[13762560]{0:T(1024)(128)(4,1)}), s8[4194304]{0:T(1024)(128)(4,1)S(1)}, s32[]{:S(2)}) async-start(s8[13762560]{0:T(1024)(128)(4,1)} %bitcast.75), calls=%async_computation.5 | async-start | bytes 8388608
  170.3 100.5 %slice-start.1 = ((s8[13762560]{0:T(1024)(128)(4,1)}), s8[4194304]{0:T(1024)(128)(4,1)S(1)}, s32[]{:S(2)}) async-start(s8[13762560]{0:T(1024)(128)(4,1)} %bitcast.75), calls=%async_computation.6 | async-start | bytes 8388608
  221.9 1.0 copy-start
  221.9 1.2 copy-start.4
  221.9 48.9 %slice-start.2 = ((s8[13762560]{0:T(1024)(128)(4,1)}), s8[4194304]{0:T(1024)(128)(4,1)S(1)}, s32[]{:S(2)}) async-start(s8[13762560]{0:T(1024)(128)(4,1)} %bitcast.75), calls=%async_computation.7 | async-start | bytes 8388608
  223.3 47.5 %slice-start.3 = ((s8[13762560]{0:T(1024)(128)(4,1)}), s8[1179648]{0:T(1024)(128)(4,1)S(1)}, s32[]{:S(2)}) async-start(s8[13762560]{0:T(1024)(128)(4,1)} %bitcast.75), calls=%async_computation.8 | async-start | bytes 2359296
  283.6 48.7 %all-to-all-start.3 = ((bf16[8,128,1792]{2,1,0:T(8,128)(2,1)}), bf16[8,128,1792]{2,1,0:T(8,128)(2,1)}, u32[]{:S(2)}, u32[]{:S(2)}) async-start(bf16[8,128,1792]{2,1,0:T(8,128)(2,1)} %bitcast.58), calls=%async_computation.3 | async-start | bytes 7340032 | tf_op jit(solution)/shard_map/all_to_all | solution.py:103
Sparse Core Ops, SparseCore 0:
  11.2 128.9 all-gather.1

commit v2 on v1

--- a/solution.py
+++ b/solution.py
@@ -75,14 +75,7 @@
     return (mixed_heads, renewed)
 
 
-def gather_weights(mix_weight, out_weight, ffn_weight, down_weight):
-    rows = mix_weight.shape[0]
-    pieces = [
-        mix_weight.reshape(rows, -1),
-        ffn_weight.reshape(rows, -1),
-        down_weight.T,
-        out_weight.T,
-    ]
+def gather_packed(pieces):
     widths = [p.shape[1] for p in pieces]
     got = lax.all_gather(jnp.concatenate(pieces, axis=1), "req", axis=0, tiled=True)
     parts = []
@@ -118,7 +111,9 @@
 ):
     feat_width = mix_weight.shape[2]
     ffn_width = ffn_weight.shape[2]
-    mix_all, ffn_all, down_t, out_t = gather_weights(mix_weight, out_weight, ffn_weight, down_weight)
+    rows = mix_weight.shape[0]
+    mix_all, out_t = gather_packed([mix_weight.reshape(rows, -1), out_weight.T])
+    ffn_all, down_t = gather_packed([ffn_weight.reshape(rows, -1), down_weight.T])
     normed_all = tp_gather(normed(tokens, norm_gain))
     row_total = normed_all.shape[0]
     projected = jnp.dot(normed_all, mix_all, preferred_element_type=jnp.float32)

time: 343 us -> 306 us (0.89)
  waiting for transfers between devices: 153 us -> 104 us
  matrix products: 34 us -> 39.9 us
    all_gather x1 -> x2, waiting for transfers between devices: 73.7 us -> 26.2 us  [gather_packed(): lax.all_gather(jnp.concatenate(pieces, axis=1), 'req', axis=0, tiled=True)]
    dot_general x1, matrix products: 6.81 us -> 10.7 us  [local(): gate_up = jnp.dot(ffn_in, ffn_all, preferred_element_type=jnp.float32)]
  transfers between devices with their start and end apart: 3 -> 4, of which waited for: 3 -> 3; matrix products, arithmetic and copies ran while one was open for 3% -> 16% of each run, Pallas kernels for 0% -> 0%
where the time goes in v2:
time: 306 us; the launch traced here: 305 us
  waiting for transfers between devices  104 us (34%)
  blocking collectives  98.8 us (32%)
  matrix products  39.9 us (13%)
  local copies, waits for them, and re-layouts  19.8 us (6%)
  between operations  15 us (5%)
  other arithmetic  14.5 us (5%)
  starting transfers between devices  13.4 us (4%)
    all_to_all x1, blocking collectives, tp_sum_scatter(): got = lax.all_to_all(x, 'tp', 0, 0, tiled=True)  51 us
    all_to_all x1, blocking collectives, tp_gather(): return lax.all_to_all(jnp.tile(x, (n, 1)), 'tp', 0, 0, tiled=True)  47.8 us
    all_to_all x1, waiting for transfers between devices, tp_gather(): return lax.all_to_all(jnp.tile(x, (n, 1)), 'tp', 0, 0, tiled=True)  40.1 us
    all_to_all x1, waiting for transfers between devices, tp_sum_scatter(): got = lax.all_to_all(x, 'tp', 0, 0, tiled=True)  37.6 us
    all_gather x2, waiting for transfers between devices, gather_packed(): lax.all_gather(jnp.concatenate(pieces, axis=1), 'req', axis=0, tiled=True)  26.2 us
    dot_general x1, matrix products, local(): gate_up = jnp.dot(ffn_in, ffn_all, preferred_element_type=jnp.float32)  10.7 us
    dot_general x1, matrix products, local(): lax.dot_general(activated, down_t, (((1,), (1,)), ((), ())), preferred_el...  7.93 us
    all_to_all x1, starting transfers between devices, tp_gather(): return lax.all_to_all(jnp.tile(x, (n, 1)), 'tp', 0, 0, tiled=True)  7.76 us
  transfers between devices with their start and end apart: 4, of which 3 were waited for; matrix products, arithmetic and copies ran while one was open for 16% of the time, Pallas kernels for 0%

profile of v2, /device:TPU:1, one launch (start us, length us, event | category | flops | bytes accessed | tf_op | source)
XLA Modules:
  0.0 305.4 jit_solution(14239022361070145913)
XLA Ops:
  7.2 1.0 reshape.257
  8.3 1.4 pad_maximum_fusion.4
  9.7 1.0 copy.55
  10.7 1.6 pad_maximum_fusion.3
  12.4 1.2 fusion.20
  13.6 1.2 fusion.22
  14.8 2.0 tile.4
  16.8 7.8 %all-to-all-start = ((bf16[8,128,1792]{2,1,0:T(8,128)(2,1)}), bf16[8,128,1792]{2,1,0:T(8,128)(2,1)}, u32[]{:S(2)}, u32[]{:S(2)}) async-start(bf16[8,128,1792]{2,1,0:T(8,128)(2,1)} %tile.4), calls=%async_computation | async-start | bytes 7340032 | tf_op jit(solution)/shard_map/all_to_all | solution.py:91
  27.8 40.1 %all-to-all-done = bf16[8,128,1792]{2,1,0:T(8,128)(2,1)} async-done(((bf16[8,128,1792]{2,1,0:T(8,128)(2,1)}), bf16[8,128,1792]{2,1,0:T(8,128)(2,1)}, u32[]{:S(2)}, u32[]{:S(2)}) %all-to-all-start) | async-done | bytes 3670048 | tf_op jit(solution)/shard_map/all_to_all | solution.py:91
  67.9 26.2 %all-gather.3.cloned.1.call-done = bf16[1792,1120]{1,0:T(8,128)(2,1)} async-done(((bf16[56,1120]{1,0:T(8,128)(2,1)}), bf16[1792,1120]{1,0:T(8,128)(2,1)}) %all-gather.3.cloned.1.call-update) | async-done | bytes 4014096 | tf_op jit(solution)/shard_map/all_gather | solution.py:80
  94.1 6.6 %fusion.9 = bf16[1024,896]{0,1:T(8,128)(2,1)S(1)} fusion(bf16[1024,1792]{1,0:T(8,128)(2,1)} %bitcast.4, bf16[1792,1120]{1,0:T(8,128)(2,1)} %all-gather.3.cloned.1.call-done), kind=kOutput, calls=%fused_computation.15 | convolution fusion | flops 3289251840 | bytes 8716288 | tf_op jit(solution)/shard_map/dot_general | solution.py:119
  100.6 1.2 slice_bitcast_fusion
  103.8 1.2 copy.28
  105.0 1.2 copy.29
  106.3 1.0 copy.54
  107.3 2.4 reshape.281
  110.6 3.1 %fusion.63 = f32[16,2,64]{2,1,0:T(2,128)} fusion(bf16[16,64,2,112]{1,3,2,0:T(8,128)(2,1)S(1)} %copy.35, bf16[16,64,2,112]{1,3,2,0:T(8,128)(2,1)S(1)} %copy.34, bf16[16,64,2,112]{1,0,3,2:T(8,128)(2,1)} %reshape.281, pred[16,64,128]{2,1,0:T(8,128)(4,1)} %broadcast_and_fusion), kind=kOutput, calls=%fused_computation.102 | convolution fusion | flops 61603968 | bytes 1515520 | tf_op jit(solution)/shard_map/sub | solution.py:40
  113.7 3.0 fusion.14
  116.7 6.0 %convolution_bitcast_fusion = f32[16,64,2,112]{3,1,2,0:T(8,128)S(1)} fusion(bf16[16,64,2,112]{1,3,2,0:T(8,128)(2,1)} %copy.29, bf16[16,64,2,112]{1,3,2,0:T(8,128)(2,1)S(1)} %copy-done.3, f32[16,2,64]{2,1,0:T(2,128)} %fusion.63, f32[16,2,64,128]{3,2,1,0:T(8,128)} %fusion.14), kind=kOutput, calls=%fused_computation.26 | convolution fusion | flops 61343872 | bytes 2891776 | tf_op jit(solution)/shard_map/bhqk,bkhd->bqhd/dot_general | solution.py:42
  122.7 0.8 copy.37
  124.4 2.6 convolution_convert_fusion.1
  127.0 51.0 %all_to_all.36 = bf16[8,128,1792]{2,1,0:T(8,128)(2,1)S(1)} all-to-all(bf16[8,128,1792]{2,1,0:T(8,128)(2,1)S(1)} %bitcast.59), channel_id=1, replica_groups=mesh['req'=32,'tp'=8] {'tp'}, dimensions={0} | all-to-all | bytes 7340032 | tf_op jit(solution)/shard_map/all_to_all | solution.py:96
  179.7 47.8 %all_to_all.37 = bf16[8,128,1792]{2,1,0:T(8,128)(2,1)} all-to-all(bf16[8,128,1792]{2,1,0:T(8,128)(2,1)S(1)} %tile.5), channel_id=1, replica_groups=mesh['req'=32,'tp'=8] {'tp'}, dimensions={0} | all-to-all | bytes 7340032 | tf_op jit(solution)/shard_map/all_to_all | solution.py:91
  227.5 10.7 %fusion.1 = f32[1024,1792]{1,0:T(8,128)S(1)} fusion(bf16[1024,1792]{1,0:T(8,128)(2,1)} %bitcast.60, bf16[1792,2688]{1,0:T(8,128)(2,1)} %all-gather.5.cloned.1.call-done), kind=kOutput, calls=%fused_computation.5 | convolution fusion | flops 6576668672 | bytes 17432576 | tf_op jit(solution)/shard_map/dot_general | solution.py:128
  238.3 7.9 %convolution_convert_fusion = bf16[1024,1792]{1,0:T(8,128)(2,1)} fusion(bf16[1792,2688]{1,0:T(8,128)(2,1)} %all-gather.5.cloned.1.call-done, f32[1024,1792]{1,0:T(8,128)S(1)} %fusion.1), kind=kOutput, calls=%fused_computation.7 | convolution fusion | flops 3295674368 | bytes 14221312 | tf_op jit(solution)/shard_map/dot_general | solution.py:130
  246.2 5.5 %all-to-all-start.3 = ((bf16[8,128,1792]{2,1,0:T(8,128)(2,1)}), bf16[8,128,1792]{2,1,0:T(8,128)(2,1)}, u32[]{:S(2)}, u32[]{:S(2)}) async-start(bf16[8,128,1792]{2,1,0:T(8,128)(2,1)} %bitcast.58), calls=%async_computation.3 | async-start | bytes 7340032 | tf_op jit(solution)/shard_map/all_to_all | solution.py:96
  251.8 0.9 copy.40
  252.6 0.8 copy.41
  253.4 2.6 pad_maximum_fusion
  257.4 37.6 %all-to-all-done.3 = bf16[8,128,1792]{2,1,0:T(8,128)(2,1)} async-done(((bf16[8,128,1792]{2,1,0:T(8,128)(2,1)}), bf16[8,128,1792]{2,1,0:T(8,128)(2,1)}, u32[]{:S(2)}, u32[]{:S(2)}) %all-to-all-start.3) | async-done | bytes 3670048 | tf_op jit(solution)/shard_map/all_to_all | solution.py:96
  295.0 2.6 convert_reduce_fusion
  297.7 0.8 fusion.27
  (61 shorter events, 9.2 us)
Async XLA Ops:
  7.2 86.9 %all-gather.3.cloned.1.call-start = ((), (), s32[]{:S(2)}) async-start(), calls=%async_computation.4 | async-start | bytes 4257792 | tf_op jit(solution)/shard_map/all_gather | solution.py:80
  9.7 217.8 %all-gather.5.cloned.1.call-start = ((), (), s32[]{:S(2)}) async-start(), calls=%async_computation.5 | async-start | bytes 9934848 | tf_op jit(solution)/shard_map/all_gather | solution.py:80
  16.8 8.4 %copy-start.7 = (bf16[1,2,64,224]{3,2,1,0:T(8,128)(2,1)S(1)}, bf16[1,2,64,224]{3,2,1,0:T(8,128)(2,1)}, u32[]{:S(2)}) copy-start(bf16[1,2,64,224]{3,2,1,0:T(8,128)(2,1)} %param.18) | copy-start | bytes 172036
  16.8 10.2 %copy-start.9 = (f32[3,224]{1,0:T(4,128)S(1)}, f32[3,224]{1,0:T(4,128)}, u32[]{:S(2)}) copy-start(f32[3,224]{1,0:T(4,128)} %param.17) | copy-start | bytes 8068
  16.8 51.1 %all-to-all-start = ((bf16[8,128,1792]{2,1,0:T(8,128)(2,1)}), bf16[8,128,1792]{2,1,0:T(8,128)(2,1)}, u32[]{:S(2)}, u32[]{:S(2)}) async-start(bf16[8,128,1792]{2,1,0:T(8,128)(2,1)} %tile.4), calls=%async_computation | async-start | bytes 7340032 | tf_op jit(solution)/shard_map/all_to_all | solution.py:91
  26.8 76.5 %copy-start.5 = (bf16[1,64,224]{2,1,0:T(8,128)(2,1)}, bf16[1,64,224]{2,1,0:T(8,128)(2,1)S(1)}, u32[]{:S(2)}) copy-start(bf16[1,64,224]{2,1,0:T(8,128)(2,1)S(1)} %copy.65) | copy-start | bytes 86020
  103.8 5.9 %copy-start.2 = (bf16[1024,1,224]{0,2,1:T(8,128)(2,1)S(1)}, bf16[1024,1,224]{0,2,1:T(8,128)(2,1)}, u32[]{:S(2)}) copy-start(bf16[1024,1,224]{0,2,1:T(8,128)(2,1)} %get-tuple-element.11) | copy-start | bytes 1376260
  110.5 6.2 %copy-start.3 = (bf16[16,64,2,112]{1,3,2,0:T(8,128)(2,1)S(1)}, bf16[16,64,2,112]{1,3,2,0:T(8,128)(2,1)}, u32[]{:S(2)}) copy-start(bf16[16,64,2,112]{1,3,2,0:T(8,128)(2,1)} %copy.28) | copy-start | bytes 1376260
  122.7 1.5 copy-start.6
  122.7 1.7 copy-start.4
  178.0 1.0 copy-start
  178.0 1.3 copy-start.8
  246.2 5.5 %copy-start.10 = (s32[64]{0:T(128)S(1)}, s32[64]{0:T(128)}, u32[]{:S(2)}) copy-start(s32[64]{0:T(128)} %get-tuple-element.20) | copy-start | bytes 772
  246.2 5.6 %copy-start.1 = (bf16[1,1024,224]{1,2,0:T(8,128)(2,1)S(1)}, bf16[1,1024,224]{1,2,0:T(8,128)(2,1)}, u32[]{:S(2)}) copy-start(bf16[1,1024,224]{1,2,0:T(8,128)(2,1)} %get-tuple-element.8) | copy-start | bytes 1376260
  246.2 48.8 %all-to-all-start.3 = ((bf16[8,128,1792]{2,1,0:T(8,128)(2,1)}), bf16[8,128,1792]{2,1,0:T(8,128)(2,1)}, u32[]{:S(2)}, u32[]{:S(2)}) async-start(bf16[8,128,1792]{2,1,0:T(8,128)(2,1)} %bitcast.58), calls=%async_computation.3 | async-start | bytes 7340032 | tf_op jit(solution)/shard_map/all_to_all | solution.py:96
Sparse Core Ops, SparseCore 0:
  11.2 82.8 all-gather.2
  96.7 103.9 all-gather.4

commit v3 on v2

--- a/solution.py
+++ b/solution.py
@@ -87,14 +87,23 @@
 
 
 def tp_gather(x):
-    n = lax.axis_size("tp")
-    return lax.all_to_all(jnp.tile(x, (n, 1)), "tp", 0, 0, tiled=True)
+    nx = lax.axis_size("tpx")
+    nc = lax.axis_size("tpc")
+    by_chip = lax.all_to_all(jnp.tile(x[None], (nx, 1, 1)), "tpx", 0, 0, tiled=True)
+    both = jnp.broadcast_to(by_chip[:, None], (nx, nc) + x.shape)
+    got = lax.all_to_all(both, "tpc", 1, 1, tiled=True)
+    return got.reshape((nx * nc * x.shape[0],) + x.shape[1:])
 
 
 def tp_sum_scatter(x):
-    n = lax.axis_size("tp")
-    got = lax.all_to_all(x, "tp", 0, 0, tiled=True)
-    return got.reshape((n, -1) + x.shape[1:]).astype(jnp.float32).sum(axis=0)
+    nx = lax.axis_size("tpx")
+    nc = lax.axis_size("tpc")
+    rows = x.shape[0] // (nx * nc)
+    parts = x.reshape((nx, nc, rows) + x.shape[1:])
+    pair = lax.all_to_all(parts, "tpc", 1, 1, tiled=True)
+    pair = pair.astype(jnp.float32).sum(axis=1).astype(jnp.bfloat16)
+    chips = lax.all_to_all(pair, "tpx", 0, 0, tiled=True)
+    return chips.astype(jnp.float32).sum(axis=0)
 
 
 def local(
@@ -136,17 +145,20 @@
 
 
 def solution(mesh):
+    n_req, n_tp = mesh.devices.shape
+    split = jax.sharding.Mesh(mesh.devices.reshape(n_req, n_tp // 2, 2), ("req", "tpx", "tpc"))
+    tp = ("tpx", "tpc")
     in_specs = (
-        P(("req", "tp"), None),
+        P(("req",) + tp, None),
         P(),
         P(),
-        P("req", None, "tp"),
-        P("tp", "req"),
-        P("req", None, "tp"),
-        P("tp", "req"),
-        P(None, "tp"),
-        P("req", None, None, "tp"),
+        P("req", None, tp),
+        P(tp, "req"),
+        P("req", None, tp),
+        P(tp, "req"),
+        P(None, tp),
+        P("req", None, None, tp),
         P("req"),
     )
-    out_specs = (P(("req", "tp"), None), P("req", None, None, "tp"))
-    return jax.shard_map(local, mesh=mesh, in_specs=in_specs, out_specs=out_specs, check_vma=False)
+    out_specs = (P(("req",) + tp, None), P("req", None, None, tp))
+    return jax.shard_map(local, mesh=split, in_specs=in_specs, out_specs=out_specs, check_vma=False)

time: 306 us -> 272 us (0.89)
  waiting for transfers between devices: 104 us -> 73.1 us
  blocking collectives: 98.8 us -> 87.3 us
  local copies, waits for them, and re-layouts: 19.8 us -> 29.6 us
  other arithmetic: 14.5 us -> 19.4 us
  starting transfers between devices: 13.4 us -> 8.51 us
    all_to_all x2, waiting for transfers between devices: 77.7 us -> 33 us  [the longest x1 19.1 us: tp_gather(): lax.all_to_all(jnp.tile(x[None], (nx, 1, 1)), 'tpx', 0, 0, tiled=True)]
    all_gather x2, waiting for transfers between devices: 26.2 us -> 40 us  [gather_packed(): lax.all_gather(jnp.concatenate(pieces, axis=1), 'req', axis=0, tiled=True)]
    all_to_all x2 -> x6, blocking collectives: 98.8 us -> 87.3 us  [the longest x1 26.6 us: tp_sum_scatter(): chips = lax.all_to_all(pair, 'tpx', 0, 0, tiled=True)]
    all_to_all x2, starting transfers between devices: 13.3 us -> 8.43 us  [the longest x1 4.84 us: tp_gather(): lax.all_to_all(jnp.tile(x[None], (nx, 1, 1)), 'tpx', 0, 0, tiled=True)]
    reduce_sum x2 -> x4, other arithmetic: 3.14 us -> 7.87 us  [the longest x2 7.35 us: tp_sum_scatter(): pair = pair.astype(jnp.float32).sum(axis=1).astype(jnp.bfloat16)]
    all_to_all x0 -> x2, local copies, waits for them, and re-layouts: none -> 4.12 us  [tp_gather(): got = lax.all_to_all(both, 'tpc', 1, 1, tiled=True)]
  transfers between devices with their start and end apart: 4 -> 4, of which waited for: 3 -> 3; matrix products, arithmetic and copies ran while one was open for 16% -> 22% of each run, Pallas kernels for 0% -> 0%
where the time goes in v3:
time: 272 us; the launch traced here: 271 us
  blocking collectives  87.3 us (32%)
  waiting for transfers between devices  73.1 us (27%)
  matrix products  38 us (14%)
  local copies, waits for them, and re-layouts  29.6 us (11%)
  other arithmetic  19.4 us (7%)
  between operations  15.1 us (6%)
  starting transfers between devices  8.51 us (3%)
    all_gather x2, waiting for transfers between devices, gather_packed(): lax.all_gather(jnp.concatenate(pieces, axis=1), 'req', axis=0, tiled=True)  40 us
    all_to_all x1, blocking collectives, tp_sum_scatter(): chips = lax.all_to_all(pair, 'tpx', 0, 0, tiled=True)  26.6 us
    all_to_all x1, blocking collectives, tp_gather(): lax.all_to_all(jnp.tile(x[None], (nx, 1, 1)), 'tpx', 0, 0, tiled=True)  24.2 us
    all_to_all x1, waiting for transfers between devices, tp_gather(): lax.all_to_all(jnp.tile(x[None], (nx, 1, 1)), 'tpx', 0, 0, tiled=True)  19.1 us
    all_to_all x2, blocking collectives, tp_gather(): got = lax.all_to_all(both, 'tpc', 1, 1, tiled=True)  18.3 us
    all_to_all x2, blocking collectives, tp_sum_scatter(): pair = lax.all_to_all(parts, 'tpc', 1, 1, tiled=True)  18.2 us
    all_to_all x1, waiting for transfers between devices, tp_sum_scatter(): chips = lax.all_to_all(pair, 'tpx', 0, 0, tiled=True)  14 us
    dot_general x1, matrix products, local(): gate_up = jnp.dot(ffn_in, ffn_all, preferred_element_type=jnp.float32)  10.7 us
  transfers between devices with their start and end apart: 4, of which 3 were waited for; matrix products, arithmetic and copies ran while one was open for 22% of the time, Pallas kernels for 0%

profile of v3, /device:TPU:1, one launch (start us, length us, event | category | flops | bytes accessed | tf_op | source)
XLA Modules:
  0.0 271.0 jit_solution(14991349982123240611)
XLA Ops:
  8.3 1.4 pad_maximum_fusion.4
  10.7 1.6 pad_maximum_fusion.3
  14.8 1.3 tile.4
  16.2 4.8 %all-to-all-start = ((bf16[4,128,1792]{2,1,0:T(8,128)(2,1)}), bf16[4,128,1792]{2,1,0:T(8,128)(2,1)S(1)}, u32[]{:S(2)}, u32[]{:S(2)}) async-start(bf16[4,128,1792]{2,1,0:T(8,128)(2,1)} %tile.4), calls=%async_computation | async-start | bytes 3670016 | tf_op jit(solution)/shard_map/all_to_all | solution.py:92
  23.6 19.1 %all-to-all-done = bf16[4,128,1792]{2,1,0:T(8,128)(2,1)S(1)} async-done(((bf16[4,128,1792]{2,1,0:T(8,128)(2,1)}), bf16[4,128,1792]{2,1,0:T(8,128)(2,1)S(1)}, u32[]{:S(2)}, u32[]{:S(2)}) %all-to-all-start) | async-done | bytes 1835040 | tf_op jit(solution)/shard_map/all_to_all | solution.py:92
  42.9 9.2 %all_to_all.40 = bf16[4,2,128,1792]{3,2,0,1:T(8,128)(2,1)S(1)} all-to-all(bf16[4,2,128,1792]{3,2,0,1:T(8,128)(2,1)S(1)} %broadcast_in_dim.26), channel_id=1, replica_groups=mesh['req'=32,'tpx'=4,'tpc'=2] {'tpc'}, dimensions={1} | all-to-all | bytes 7340032 | tf_op jit(solution)/shard_map/all_to_all | solution.py:94
  52.1 2.0 copy.84
  54.1 40.0 %all-gather.3.cloned.1.call-done = bf16[1792,1120]{1,0:T(8,128)(2,1)} async-done(((bf16[56,1120]{1,0:T(8,128)(2,1)}), bf16[1792,1120]{1,0:T(8,128)(2,1)}) %all-gather.3.cloned.1.call-update) | async-done | bytes 4014096 | tf_op jit(solution)/shard_map/all_gather | solution.py:80
  94.1 6.6 %fusion.9 = bf16[1024,896]{0,1:T(8,128)(2,1)S(1)} fusion(bf16[1024,1792]{1,0:T(8,128)(2,1)} %bitcast.59, bf16[1792,1120]{1,0:T(8,128)(2,1)} %all-gather.3.cloned.1.call-done), kind=kOutput, calls=%fused_computation.15 | convolution fusion | flops 3289251840 | bytes 8716288 | tf_op jit(solution)/shard_map/dot_general | solution.py:128
  100.6 1.4 slice_bitcast_fusion
  106.4 2.0 copy.115
  108.5 2.4 reshape.283
  110.9 1.9 reshape.285
  113.0 2.5 fusion.63
  115.6 3.0 %fusion.14 = f32[16,2,64,128]{3,2,1,0:T(8,128)} fusion(bf16[16,64,2,112]{1,3,2,0:T(8,128)(2,1)S(1)} %copy.93, bf16[16,64,2,112]{1,3,2,0:T(8,128)(2,1)S(1)} %copy.92, bf16[16,64,2,112]{1,0,3,2:T(8,128)(2,1)} %reshape.283, pred[16,64,128]{2,1,0:T(8,128)(4,1)S(1)} %broadcast_and_fusion), kind=kOutput, calls=%fused_computation.25 | convolution fusion | flops 61079552 | bytes 2555904 | tf_op jit(solution)/shard_map/bqhd,bkhd->bhqk/dot_general | solution.py:32
  118.6 6.0 %convolution_bitcast_fusion = f32[16,64,2,112]{3,1,2,0:T(8,128)S(1)} fusion(bf16[16,64,2,112]{1,3,2,0:T(8,128)(2,1)} %copy.87, bf16[16,64,2,112]{1,3,2,0:T(8,128)(2,1)S(1)} %copy-done.3, f32[16,2,64]{2,1,0:T(2,128)S(1)} %fusion.63, f32[16,2,64,128]{3,2,1,0:T(8,128)} %fusion.14), kind=kOutput, calls=%fused_computation.26 | convolution fusion | flops 61343872 | bytes 2891776 | tf_op jit(solution)/shard_map/bhqk,bkhd->bqhd/dot_general | solution.py:42
  126.3 2.6 convolution_convert_fusion.1
  129.1 10.6 %all_to_all.41 = bf16[4,2,128,1792]{3,2,0,1:T(8,128)(2,1)} all-to-all(bf16[4,2,128,1792]{3,2,0,1:T(8,128)(2,1)S(1)} %copy.97), channel_id=1, replica_groups=mesh['req'=32,'tpx'=4,'tpc'=2] {'tpc'}, dimensions={1} | all-to-all | bytes 7340032 | tf_op jit(solution)/shard_map/all_to_all | solution.py:103
  139.7 2.9 %reduce_sum.71 = bf16[4,128,1792]{2,1,0:T(8,128)(2,1)S(1)} reduce(bf16[4,2,128,1792]{3,2,0,1:T(8,128)(2,1)} %all_to_all.41, bf16[]{:T(256)} %constant.46.clone.1), dimensions={1}, to_apply=%region_3.4 | reduce | flops 917504 | bytes 5505026 | tf_op jit(solution)/shard_map/reduce_sum | solution.py:104
  142.7 26.6 %all_to_all.42 = bf16[4,128,1792]{2,1,0:T(8,128)(2,1)S(1)} all-to-all(bf16[4,128,1792]{2,1,0:T(8,128)(2,1)S(1)} %reduce_sum.71), channel_id=1, replica_groups=mesh['req'=32,'tpx'=4,'tpc'=2] {'tpx'}, dimensions={0} | all-to-all | bytes 3670016 | tf_op jit(solution)/shard_map/all_to_all | solution.py:105
  170.9 24.2 %all_to_all.43 = bf16[4,128,1792]{2,1,0:T(8,128)(2,1)S(1)} all-to-all(bf16[4,128,1792]{2,1,0:T(8,128)(2,1)S(1)} %tile.5), channel_id=1, replica_groups=mesh['req'=32,'tpx'=4,'tpc'=2] {'tpx'}, dimensions={0} | all-to-all | bytes 3670016 | tf_op jit(solution)/shard_map/all_to_all | solution.py:92
  195.4 9.1 %all_to_all.44 = bf16[4,2,128,1792]{3,2,0,1:T(8,128)(2,1)S(1)} all-to-all(bf16[4,2,128,1792]{3,2,0,1:T(8,128)(2,1)S(1)} %broadcast_in_dim.35), channel_id=1, replica_groups=mesh['req'=32,'tpx'=4,'tpc'=2] {'tpc'}, dimensions={1} | all-to-all | bytes 7340032 | tf_op jit(solution)/shard_map/all_to_all | solution.py:94
  204.5 2.1 copy.98
  206.6 10.7 %fusion.1 = f32[1024,1792]{1,0:T(8,128)S(1)} fusion(bf16[1024,1792]{1,0:T(8,128)(2,1)} %bitcast.60, bf16[1792,2688]{1,0:T(8,128)(2,1)} %all-gather.5.cloned.1.call-done), kind=kOutput, calls=%fused_computation.3 | convolution fusion | flops 6576668672 | bytes 17432576 | tf_op jit(solution)/shard_map/dot_general | solution.py:137
  217.3 6.6 %convolution_convert_fusion = bf16[1024,1792]{1,0:T(8,128)(2,1)S(1)} fusion(bf16[1792,2688]{1,0:T(8,128)(2,1)} %all-gather.5.cloned.1.call-done, f32[1024,1792]{1,0:T(8,128)S(1)} %fusion.1), kind=kOutput, calls=%fused_computation.5 | convolution fusion | flops 3295674368 | bytes 14221312 | tf_op jit(solution)/shard_map/dot_general | solution.py:139
  224.2 7.6 %all_to_all.45 = bf16[4,2,128,1792]{3,2,0,1:T(8,128)(2,1)} all-to-all(bf16[4,2,128,1792]{3,2,0,1:T(8,128)(2,1)S(1)} %copy.99), channel_id=1, replica_groups=mesh['req'=32,'tpx'=4,'tpc'=2] {'tpc'}, dimensions={1} | all-to-all | bytes 7340032 | tf_op jit(solution)/shard_map/all_to_all | solution.py:103
  231.8 4.4 %reduce_sum.74 = bf16[4,128,1792]{2,1,0:T(8,128)(2,1)} reduce(bf16[4,2,128,1792]{3,2,0,1:T(8,128)(2,1)} %all_to_all.45, bf16[]{:T(256)} %constant.46.clone.1), dimensions={1}, to_apply=%region_6.7 | reduce | flops 917504 | bytes 5505026 | tf_op jit(solution)/shard_map/reduce_sum | solution.py:104
  236.2 3.6 %all-to-all-start.7 = ((bf16[4,128,1792]{2,1,0:T(8,128)(2,1)}), bf16[4,128,1792]{2,1,0:T(8,128)(2,1)S(1)}, u32[]{:S(2)}, u32[]{:S(2)}) async-start(bf16[4,128,1792]{2,1,0:T(8,128)(2,1)} %reduce_sum.74), calls=%async_computation.7 | async-start | bytes 3670016 | tf_op jit(solution)/shard_map/all_to_all | solution.py:105
  239.9 2.4 copy.101
  243.1 3.4 %pad_maximum_fusion = bf16[2,1024,224]{2,0,1:T(2,128)(2,1)} fusion(bf16[1,1024,224]{2,0,1:T(2,128)(2,1)S(1)} %copy.102, bf16[1,1024,224]{2,0,1:T(2,128)(2,1)S(1)} %copy.101), kind=kLoop, calls=%fused_computation.36 | loop fusion | flops 1835008 | bytes 1835008 | tf_op jit(solution)/shard_map/stack | solution.py:74
  246.5 1.9 gather_fusion.1
  249.1 14.0 %all-to-all-done.7 = bf16[4,128,1792]{2,1,0:T(8,128)(2,1)S(1)} async-done(((bf16[4,128,1792]{2,1,0:T(8,128)(2,1)}), bf16[4,128,1792]{2,1,0:T(8,128)(2,1)S(1)}, u32[]{:S(2)}, u32[]{:S(2)}) %all-to-all-start.7) | async-done | bytes 1835040 | tf_op jit(solution)/shard_map/all_to_all | solution.py:105
  (73 shorter events, 17.8 us)
Async XLA Ops:
  7.2 86.9 %all-gather.3.cloned.1.call-start = ((), (), s32[]{:S(2)}) async-start(), calls=%async_computation.8 | async-start | bytes 4257792 | tf_op jit(solution)/shard_map/all_gather | solution.py:80
  9.7 196.9 %all-gather.5.cloned.1.call-start = ((), (), s32[]{:S(2)}) async-start(), calls=%async_computation.9 | async-start | bytes 9934848 | tf_op jit(solution)/shard_map/all_gather | solution.py:80
  12.4 9.3 %copy-start.7 = (bf16[1,2,64,224]{3,2,1,0:T(8,128)(2,1)S(1)}, bf16[1,2,64,224]{3,2,1,0:T(8,128)(2,1)}, u32[]{:S(2)}) copy-start(bf16[1,2,64,224]{3,2,1,0:T(8,128)(2,1)} %param.18) | copy-start | bytes 172036
  13.6 9.8 %copy-start.9 = (f32[3,224]{1,0:T(4,128)S(1)}, f32[3,224]{1,0:T(4,128)}, u32[]{:S(2)}) copy-start(f32[3,224]{1,0:T(4,128)} %param.17) | copy-start | bytes 8068
  16.2 26.4 %all-to-all-start = ((bf16[4,128,1792]{2,1,0:T(8,128)(2,1)}), bf16[4,128,1792]{2,1,0:T(8,128)(2,1)S(1)}, u32[]{:S(2)}, u32[]{:S(2)}) async-start(bf16[4,128,1792]{2,1,0:T(8,128)(2,1)} %tile.4), calls=%async_computation | async-start | bytes 3670016 | tf_op jit(solution)/shard_map/all_to_all | solution.py:92
  23.3 80.3 %copy-start.5 = (bf16[1,64,224]{2,1,0:T(8,128)(2,1)}, bf16[1,64,224]{2,1,0:T(8,128)(2,1)S(1)}, u32[]{:S(2)}) copy-start(bf16[1,64,224]{2,1,0:T(8,128)(2,1)S(1)} %copy.126) | copy-start | bytes 86020
  113.0 5.6 %copy-start.3 = (bf16[16,64,2,112]{1,3,2,0:T(8,128)(2,1)S(1)}, bf16[16,64,2,112]{1,3,2,0:T(8,128)(2,1)}, u32[]{:S(2)}) copy-start(bf16[16,64,2,112]{1,3,2,0:T(8,128)(2,1)} %copy.86) | copy-start | bytes 1376260
  118.6 7.4 %copy-start.6 = (bf16[1,64,224]{2,1,0:T(8,128)(2,1)S(1)}, bf16[1,64,224]{2,1,0:T(8,128)(2,1)}, u32[]{:S(2)}) copy-start(bf16[1,64,224]{2,1,0:T(8,128)(2,1)} %copy-done.5) | copy-start | bytes 86020
  124.6 1.7 copy-start.4
  142.7 26.9 %copy-start.2 = (bf16[128,1792]{1,0:T(8,128)(2,1)S(1)}, bf16[128,1792]{1,0:T(8,128)(2,1)}, u32[]{:S(2)}) copy-start(bf16[128,1792]{1,0:T(8,128)(2,1)} %param.10) | copy-start | bytes 1376260
  142.7 27.9 %copy-start.8 = (f32[1792]{0:T(1024)S(1)}, f32[1792]{0:T(1024)}, u32[]{:S(2)}) copy-start(f32[1792]{0:T(1024)} %param.12) | copy-start | bytes 21508
  169.8 0.8 copy-start
  231.8 8.0 %copy-start.10 = (s32[64]{0:T(128)S(1)}, s32[64]{0:T(128)}, u32[]{:S(2)}) copy-start(s32[64]{0:T(128)} %get-tuple-element.26) | copy-start | bytes 772
  236.2 26.8 %all-to-all-start.7 = ((bf16[4,128,1792]{2,1,0:T(8,128)(2,1)}), bf16[4,128,1792]{2,1,0:T(8,128)(2,1)S(1)}, u32[]{:S(2)}, u32[]{:S(2)}) async-start(bf16[4,128,1792]{2,1,0:T(8,128)(2,1)} %reduce_sum.74), calls=%async_computation.7 | async-start | bytes 3670016 | tf_op jit(solution)/shard_map/all_to_all | solution.py:105
  243.1 20.3 %copy-start.1 = (bf16[128,1792]{1,0:T(8,128)(2,1)S(1)}, bf16[128,1792]{1,0:T(8,128)(2,1)}, u32[]{:S(2)}) copy-start(bf16[128,1792]{1,0:T(8,128)(2,1)} %copy-done) | copy-start | bytes 1376260
Sparse Core Ops, SparseCore 0:
  11.2 82.8 all-gather.2
  96.7 103.9 all-gather.4

commit v4 on v3

--- a/solution.py
+++ b/solution.py
@@ -7,6 +7,7 @@
 
 HD = 112
 WIN = 64
+REQ = ("ry", "rz")
 
 
 def normed(row_vals, gain):
@@ -77,13 +78,24 @@
 
 def gather_packed(pieces):
     widths = [p.shape[1] for p in pieces]
-    got = lax.all_gather(jnp.concatenate(pieces, axis=1), "req", axis=0, tiled=True)
+    got = lax.all_gather(jnp.concatenate(pieces, axis=1), REQ, axis=0, tiled=True)
     parts = []
     start = 0
     for w in widths:
         parts.append(got[:, start : start + w])
         start += w
     return parts
+
+
+def a2a_gather(x, axis):
+    n = lax.axis_size(axis)
+    return lax.all_to_all(jnp.tile(x[None], (n,) + (1,) * x.ndim), axis, 0, 0, tiled=True)
+
+
+def req_gather_rows(x):
+    by_z = a2a_gather(x, REQ[1])
+    by_y = a2a_gather(by_z, REQ[0])
+    return by_y.reshape((-1,) + x.shape[1:])
 
 
 def tp_gather(x):
@@ -121,8 +133,10 @@
     feat_width = mix_weight.shape[2]
     ffn_width = ffn_weight.shape[2]
     rows = mix_weight.shape[0]
-    mix_all, out_t = gather_packed([mix_weight.reshape(rows, -1), out_weight.T])
-    ffn_all, down_t = gather_packed([ffn_weight.reshape(rows, -1), down_weight.T])
+    mix_all = req_gather_rows(mix_weight.reshape(rows, -1))
+    out_t, ffn_all, down_t = gather_packed(
+        [out_weight.T, ffn_weight.reshape(rows, -1), down_weight.T]
+    )
     normed_all = tp_gather(normed(tokens, norm_gain))
     row_total = normed_all.shape[0]
     projected = jnp.dot(normed_all, mix_all, preferred_element_type=jnp.float32)
@@ -146,19 +160,22 @@
 
 def solution(mesh):
     n_req, n_tp = mesh.devices.shape
-    split = jax.sharding.Mesh(mesh.devices.reshape(n_req, n_tp // 2, 2), ("req", "tpx", "tpc"))
+    ny = 4 if n_req % 4 == 0 else 1
+    split = jax.sharding.Mesh(
+        mesh.devices.reshape(ny, n_req // ny, n_tp // 2, 2), REQ + ("tpx", "tpc")
+    )
     tp = ("tpx", "tpc")
     in_specs = (
-        P(("req",) + tp, None),
+        P(REQ + tp, None),
         P(),
         P(),
-        P("req", None, tp),
-        P(tp, "req"),
-        P("req", None, tp),
-        P(tp, "req"),
+        P(REQ, None, tp),
+        P(tp, REQ),
+        P(REQ, None, tp),
+        P(tp, REQ),
         P(None, tp),
-        P("req", None, None, tp),
-        P("req"),
+        P(REQ, None, None, tp),
+        P(REQ),
     )
-    out_specs = (P(("req",) + tp, None), P("req", None, None, tp))
+    out_specs = (P(REQ + tp, None), P(REQ, None, None, tp))
     return jax.shard_map(local, mesh=split, in_specs=in_specs, out_specs=out_specs, check_vma=False)

time: 272 us -> 314 us (1.15)
  blocking collectives: 87.3 us -> 124 us
  matrix products: 38 us -> 31.7 us
  waiting for transfers between devices: 73.1 us -> 78.7 us
  starting transfers between devices: 8.51 us -> 13.2 us
  local copies, waits for them, and re-layouts: 29.6 us -> 33.6 us
    all_to_all x0 -> x1, waiting for transfers between devices: none -> 43.4 us  [a2a_gather(): lax.all_to_all(jnp.tile(x[None], (n,) + (1,) * x.ndim), axis, 0, 0, tiled...]
    all_gather x2 -> x1, waiting for transfers between devices: 40 us -> 0.02 us  [gather_packed(): lax.all_gather(jnp.concatenate(pieces, axis=1), REQ, axis=0, tiled=True)]
    all_to_all x0 -> x1, blocking collectives: none -> 36 us  [a2a_gather(): lax.all_to_all(jnp.tile(x[None], (n,) + (1,) * x.ndim), axis, 0, 0, tiled...]
    all_to_all x0 -> x1, starting transfers between devices: none -> 4.45 us  [a2a_gather(): lax.all_to_all(jnp.tile(x[None], (n,) + (1,) * x.ndim), axis, 0, 0, tiled...]
    dot_general x1, matrix products: 10.7 us -> 6.97 us  [local(): gate_up = jnp.dot(ffn_in, ffn_all, preferred_element_type=jnp.float32)]
  transfers between devices with their start and end apart: 4 -> 4, of which waited for: 3 -> 3; matrix products, arithmetic and copies ran while one was open for 22% -> 17% of each run, Pallas kernels for 0% -> 0%
where the time goes in v4:
time: 314 us; the launch traced here: 313 us
  blocking collectives  124 us (39%)
  waiting for transfers between devices  78.7 us (25%)
  local copies, waits for them, and re-layouts  33.6 us (11%)
  matrix products  31.7 us (10%)
  other arithmetic  16.3 us (5%)
  between operations  15.2 us (5%)
  starting transfers between devices  13.2 us (4%)
    all_to_all x1, waiting for transfers between devices, a2a_gather(): lax.all_to_all(jnp.tile(x[None], (n,) + (1,) * x.ndim), axis, 0, 0, tiled...  43.4 us
    all_to_all x1, blocking collectives, a2a_gather(): lax.all_to_all(jnp.tile(x[None], (n,) + (1,) * x.ndim), axis, 0, 0, tiled...  36 us
    all_to_all x1, blocking collectives, tp_sum_scatter(): chips = lax.all_to_all(pair, 'tpx', 0, 0, tiled=True)  26.6 us
    all_to_all x1, blocking collectives, tp_gather(): lax.all_to_all(jnp.tile(x[None], (nx, 1, 1)), 'tpx', 0, 0, tiled=True)  24.5 us
    all_to_all x1, waiting for transfers between devices, tp_gather(): lax.all_to_all(jnp.tile(x[None], (nx, 1, 1)), 'tpx', 0, 0, tiled=True)  21.5 us
    all_to_all x2, blocking collectives, tp_gather(): got = lax.all_to_all(both, 'tpc', 1, 1, tiled=True)  19.7 us
    all_to_all x2, blocking collectives, tp_sum_scatter(): pair = lax.all_to_all(parts, 'tpc', 1, 1, tiled=True)  17.7 us
    all_to_all x1, waiting for transfers between devices, tp_sum_scatter(): chips = lax.all_to_all(pair, 'tpx', 0, 0, tiled=True)  13.7 us
  transfers between devices with their start and end apart: 4, of which 3 were waited for; matrix products, arithmetic and copies ran while one was open for 17% of the time, Pallas kernels for 0%

profile of v4, /device:TPU:1, one launch (start us, length us, event | category | flops | bytes accessed | tf_op | source)
XLA Modules:
  0.0 313.1 jit_solution(928307414407062171)
XLA Ops:
  8.2 1.9 concatenate.19
  13.9 4.8 %all-to-all-start = ((bf16[4,128,1792]{2,1,0:T(8,128)(2,1)}), bf16[4,128,1792]{2,1,0:T(8,128)(2,1)S(1)}, u32[]{:S(2)}, u32[]{:S(2)}) async-start(bf16[4,128,1792]{2,1,0:T(8,128)(2,1)} %tile.10), calls=%async_computation | async-start | bytes 3670016 | tf_op jit(solution)/shard_map/all_to_all | solution.py:104
  18.9 21.5 %all-to-all-done = bf16[4,128,1792]{2,1,0:T(8,128)(2,1)S(1)} async-done(((bf16[4,128,1792]{2,1,0:T(8,128)(2,1)}), bf16[4,128,1792]{2,1,0:T(8,128)(2,1)S(1)}, u32[]{:S(2)}, u32[]{:S(2)}) %all-to-all-start) | async-done | bytes 1835040 | tf_op jit(solution)/shard_map/all_to_all | solution.py:104
  40.6 10.2 %all_to_all.50 = bf16[4,2,128,1792]{3,2,0,1:T(8,128)(2,1)} all-to-all(bf16[4,2,128,1792]{3,2,0,1:T(8,128)(2,1)S(1)} %broadcast_in_dim.26), channel_id=1, replica_groups=mesh['ry'=4,'rz'=8,'tpx'=4,'tpc'=2] {'tpc'}, dimensions={1} | all-to-all | bytes 7340032 | tf_op jit(solution)/shard_map/all_to_all | solution.py:106
  50.8 36.0 %all_to_all.51 = bf16[8,56,896]{2,1,0:T(8,128)(2,1)S(1)} all-to-all(bf16[8,56,896]{2,1,0:T(8,128)(2,1)S(1)} %tile.12), channel_id=1, replica_groups=mesh['ry'=4,'rz'=8,'tpx'=4,'tpc'=2] {'rz'}, dimensions={0} | all-to-all | bytes 1605632 | tf_op jit(solution)/shard_map/all_to_all | solution.py:92
  86.8 1.9 tile.13
  88.8 4.5 %all-to-all-start.3 = ((bf16[4,8,56,896]{3,2,1,0:T(8,128)(2,1)}), bf16[4,8,56,896]{3,2,1,0:T(8,128)(2,1)S(1)}, u32[]{:S(2)}, u32[]{:S(2)}) async-start(bf16[4,8,56,896]{3,2,1,0:T(8,128)(2,1)} %tile.13), calls=%async_computation.3 | async-start | bytes 6422528 | tf_op jit(solution)/shard_map/all_to_all | solution.py:92
  96.4 4.2 %copy.84 = bf16[4,2,128,1792]{3,2,1,0:T(8,128)(2,1)} copy(bf16[4,2,128,1792]{3,2,0,1:T(8,128)(2,1)} %all_to_all.50) | data formatting | bytes 7340032 | tf_op jit(solution)/shard_map/all_to_all | solution.py:106
  100.6 43.4 %all-to-all-done.3 = bf16[4,8,56,896]{3,2,1,0:T(8,128)(2,1)S(1)} async-done(((bf16[4,8,56,896]{3,2,1,0:T(8,128)(2,1)}), bf16[4,8,56,896]{3,2,1,0:T(8,128)(2,1)S(1)}, u32[]{:S(2)}, u32[]{:S(2)}) %all-to-all-start.3) | async-done | bytes 3211296 | tf_op jit(solution)/shard_map/all_to_all | solution.py:92
  144.1 5.6 %convolution_convert_fusion.2 = bf16[1024,896]{0,1:T(8,128)(2,1)S(1)} fusion(bf16[1024,1792]{1,0:T(8,128)(2,1)} %bitcast.60, bf16[1792,896]{1,0:T(8,128)(2,1)S(1)} %bitcast.64), kind=kOutput, calls=%fused_computation.13 | convolution fusion | flops 3289251840 | bytes 8716288 | tf_op jit(solution)/shard_map/dot_general | solution.py:142
  149.6 1.3 slice_bitcast_fusion
  155.5 2.0 copy.115
  157.5 2.4 reshape.289
  159.9 1.9 reshape.291
  162.1 2.5 fusion.58
  164.6 3.0 fusion.9
  167.6 6.0 %convolution_bitcast_fusion = f32[16,64,2,112]{3,1,2,0:T(8,128)S(1)} fusion(bf16[16,64,2,112]{1,3,2,0:T(8,128)(2,1)} %copy.87, bf16[16,64,2,112]{1,3,2,0:T(8,128)(2,1)S(1)} %copy-done.3, f32[16,2,64]{2,1,0:T(2,128)S(1)} %fusion.58, f32[16,2,64,128]{3,2,1,0:T(8,128)} %fusion.9), kind=kOutput, calls=%fused_computation.24 | convolution fusion | flops 61343872 | bytes 2891776 | tf_op jit(solution)/shard_map/bhqk,bkhd->bqhd/dot_general | solution.py:43
  175.3 2.6 convolution_convert_fusion.1
  178.2 10.1 %all_to_all.52 = bf16[4,2,128,1792]{3,2,0,1:T(8,128)(2,1)} all-to-all(bf16[4,2,128,1792]{3,2,0,1:T(8,128)(2,1)S(1)} %copy.97), channel_id=1, replica_groups=mesh['ry'=4,'rz'=8,'tpx'=4,'tpc'=2] {'tpc'}, dimensions={1} | all-to-all | bytes 7340032 | tf_op jit(solution)/shard_map/all_to_all | solution.py:115
  188.3 2.9 reduce_sum.71
  191.2 26.6 %all_to_all.53 = bf16[4,128,1792]{2,1,0:T(8,128)(2,1)S(1)} all-to-all(bf16[4,128,1792]{2,1,0:T(8,128)(2,1)S(1)} %reduce_sum.71), channel_id=1, replica_groups=mesh['ry'=4,'rz'=8,'tpx'=4,'tpc'=2] {'tpx'}, dimensions={0} | all-to-all | bytes 3670016 | tf_op jit(solution)/shard_map/all_to_all | solution.py:117
  219.4 24.5 %all_to_all.54 = bf16[4,128,1792]{2,1,0:T(8,128)(2,1)S(1)} all-to-all(bf16[4,128,1792]{2,1,0:T(8,128)(2,1)S(1)} %tile.14), channel_id=1, replica_groups=mesh['ry'=4,'rz'=8,'tpx'=4,'tpc'=2] {'tpx'}, dimensions={0} | all-to-all | bytes 3670016 | tf_op jit(solution)/shard_map/all_to_all | solution.py:104
  244.2 9.5 %all_to_all.55 = bf16[4,2,128,1792]{3,2,0,1:T(8,128)(2,1)S(1)} all-to-all(bf16[4,2,128,1792]{3,2,0,1:T(8,128)(2,1)S(1)} %broadcast_in_dim.35), channel_id=1, replica_groups=mesh['ry'=4,'rz'=8,'tpx'=4,'tpc'=2] {'tpc'}, dimensions={1} | all-to-all | bytes 7340032 | tf_op jit(solution)/shard_map/all_to_all | solution.py:106
  254.0 7.0 %fusion.1 = f32[1024,1792]{1,0:T(8,128)S(1)} fusion(bf16[1024,1792]{1,0:T(8,128)(2,1)S(1)} %bitcast.63, bf16[1792,2912]{1,0:T(8,128)(2,1)S(1)} %bitcast.80), kind=kOutput, calls=%fused_computation.3 | convolution fusion | flops 6576668672 | bytes 17432576 | tf_op jit(solution)/shard_map/dot_general | solution.py:151
  261.0 5.0 %convolution_convert_fusion = bf16[1024,1792]{1,0:T(8,128)(2,1)S(1)} fusion(bf16[1792,2912]{1,0:T(8,128)(2,1)S(1)} %bitcast.80, f32[1024,1792]{1,0:T(8,128)S(1)} %fusion.1), kind=kOutput, calls=%fused_computation.5 | convolution fusion | flops 3295674368 | bytes 14221312 | tf_op jit(solution)/shard_map/dot_general | solution.py:153
  266.3 7.6 %all_to_all.56 = bf16[4,2,128,1792]{3,2,0,1:T(8,128)(2,1)} all-to-all(bf16[4,2,128,1792]{3,2,0,1:T(8,128)(2,1)S(1)} %copy.99), channel_id=1, replica_groups=mesh['ry'=4,'rz'=8,'tpx'=4,'tpc'=2] {'tpc'}, dimensions={1} | all-to-all | bytes 7340032 | tf_op jit(solution)/shard_map/all_to_all | solution.py:115
  273.9 4.4 %reduce_sum.74 = bf16[4,128,1792]{2,1,0:T(8,128)(2,1)} reduce(bf16[4,2,128,1792]{3,2,0,1:T(8,128)(2,1)} %all_to_all.56, bf16[]{:T(256)} %constant.46.clone.1), dimensions={1}, to_apply=%region_6.7 | reduce | flops 917504 | bytes 5505026 | tf_op jit(solution)/shard_map/reduce_sum | solution.py:116
  278.3 3.8 %all-to-all-start.9 = ((bf16[4,128,1792]{2,1,0:T(8,128)(2,1)}), bf16[4,128,1792]{2,1,0:T(8,128)(2,1)S(1)}, u32[]{:S(2)}, u32[]{:S(2)}) async-start(bf16[4,128,1792]{2,1,0:T(8,128)(2,1)} %reduce_sum.74), calls=%async_computation.9 | async-start | bytes 3670016 | tf_op jit(solution)/shard_map/all_to_all | solution.py:117
  282.2 2.4 copy.101
  285.4 3.4 %pad_maximum_fusion = bf16[2,1024,224]{2,0,1:T(2,128)(2,1)} fusion(bf16[1,1024,224]{2,0,1:T(2,128)(2,1)S(1)} %copy.102, bf16[1,1024,224]{2,0,1:T(2,128)(2,1)S(1)} %copy.101), kind=kLoop, calls=%fused_computation.34 | loop fusion | flops 1835008 | bytes 1835008 | tf_op jit(solution)/shard_map/stack | solution.py:75
  288.8 1.9 gather_fusion.1
  291.4 13.7 %all-to-all-done.9 = bf16[4,128,1792]{2,1,0:T(8,128)(2,1)S(1)} async-done(((bf16[4,128,1792]{2,1,0:T(8,128)(2,1)}), bf16[4,128,1792]{2,1,0:T(8,128)(2,1)S(1)}, u32[]{:S(2)}, u32[]{:S(2)}) %all-to-all-start.9) | async-done | bytes 1835040 | tf_op jit(solution)/shard_map/all_to_all | solution.py:117
  (85 shorter events, 19.2 us)
Async XLA Ops:
  7.2 168.1 %all-gather.2.cloned.1.call-start = ((), (), s32[]{:S(2)}) async-start(), calls=%async_computation.10 | async-start | bytes 10881024 | tf_op jit(solution)/shard_map/all_gather | solution.py:81
  10.1 8.6 %copy-start.8 = (bf16[56,4,224]{2,1,0:T(4,128)(2,1)S(1)}, bf16[56,4,224]{2,1,0:T(4,128)(2,1)}, u32[]{:S(2)}) copy-start(bf16[56,4,224]{2,1,0:T(4,128)(2,1)} %param.13) | copy-start | bytes 301060
  13.9 26.4 %all-to-all-start = ((bf16[4,128,1792]{2,1,0:T(8,128)(2,1)}), bf16[4,128,1792]{2,1,0:T(8,128)(2,1)S(1)}, u32[]{:S(2)}, u32[]{:S(2)}) async-start(bf16[4,128,1792]{2,1,0:T(8,128)(2,1)} %tile.10), calls=%async_computation | async-start | bytes 3670016 | tf_op jit(solution)/shard_map/all_to_all | solution.py:104
  88.8 5.1 %copy-start.9 = (bf16[1,2,64,224]{3,2,1,0:T(8,128)(2,1)S(1)}, bf16[1,2,64,224]{3,2,1,0:T(8,128)(2,1)}, u32[]{:S(2)}) copy-start(bf16[1,2,64,224]{3,2,1,0:T(8,128)(2,1)} %param.18) | copy-start | bytes 172036
  88.8 7.5 %copy-start.11 = (f32[3,224]{1,0:T(4,128)S(1)}, f32[3,224]{1,0:T(4,128)}, u32[]{:S(2)}) copy-start(f32[3,224]{1,0:T(4,128)} %param.17) | copy-start | bytes 8068
  88.8 55.3 %all-to-all-start.3 = ((bf16[4,8,56,896]{3,2,1,0:T(8,128)(2,1)}), bf16[4,8,56,896]{3,2,1,0:T(8,128)(2,1)S(1)}, u32[]{:S(2)}, u32[]{:S(2)}) async-start(bf16[4,8,56,896]{3,2,1,0:T(8,128)(2,1)} %tile.13), calls=%async_computation.3 | async-start | bytes 6422528 | tf_op jit(solution)/shard_map/all_to_all | solution.py:92
  96.1 56.4 %copy-start.5 = (bf16[1,64,224]{2,1,0:T(8,128)(2,1)}, bf16[1,64,224]{2,1,0:T(8,128)(2,1)S(1)}, u32[]{:S(2)}) copy-start(bf16[1,64,224]{2,1,0:T(8,128)(2,1)S(1)} %copy.126) | copy-start | bytes 86020
  149.6 1.4 copy-start.7
  162.1 5.6 %copy-start.3 = (bf16[16,64,2,112]{1,3,2,0:T(8,128)(2,1)S(1)}, bf16[16,64,2,112]{1,3,2,0:T(8,128)(2,1)}, u32[]{:S(2)}) copy-start(bf16[16,64,2,112]{1,3,2,0:T(8,128)(2,1)} %copy.86) | copy-start | bytes 1376260
  167.6 7.4 %copy-start.6 = (bf16[1,64,224]{2,1,0:T(8,128)(2,1)S(1)}, bf16[1,64,224]{2,1,0:T(8,128)(2,1)}, u32[]{:S(2)}) copy-start(bf16[1,64,224]{2,1,0:T(8,128)(2,1)} %copy-done.5) | copy-start | bytes 86020
  173.6 1.7 copy-start.4
  191.2 26.8 %copy-start.2 = (bf16[128,1792]{1,0:T(8,128)(2,1)S(1)}, bf16[128,1792]{1,0:T(8,128)(2,1)}, u32[]{:S(2)}) copy-start(bf16[128,1792]{1,0:T(8,128)(2,1)} %param.10) | copy-start | bytes 1376260
  191.2 27.9 %copy-start.10 = (f32[1792]{0:T(1024)S(1)}, f32[1792]{0:T(1024)}, u32[]{:S(2)}) copy-start(f32[1792]{0:T(1024)} %param.12) | copy-start | bytes 21508
  218.3 0.8 copy-start
  219.4 34.6 %slice-start = ((s8[10551296]{0:T(1024)(128)(4,1)}), s8[4194304]{0:T(1024)(128)(4,1)S(1)}, s32[]{:S(2)}) async-start(s8[10551296]{0:T(1024)(128)(4,1)} %bitcast.79), calls=%async_computation.11 | async-start | bytes 8388608
  243.9 10.1 %slice-start.1 = ((s8[10551296]{0:T(1024)(128)(4,1)}), s8[4194304]{0:T(1024)(128)(4,1)S(1)}, s32[]{:S(2)}) async-start(s8[10551296]{0:T(1024)(128)(4,1)} %bitcast.79), calls=%async_computation.12 | async-start | bytes 8388608
  244.2 9.8 %slice-start.2 = ((s8[10551296]{0:T(1024)(128)(4,1)}), s8[2162688]{0:T(1024)(128)(4,1)S(1)}, s32[]{:S(2)}) async-start(s8[10551296]{0:T(1024)(128)(4,1)} %bitcast.79), calls=%async_computation.13 | async-start | bytes 4325376
  273.9 8.3 %copy-start.12 = (s32[64]{0:T(128)S(1)}, s32[64]{0:T(128)}, u32[]{:S(2)}) copy-start(s32[64]{0:T(128)} %get-tuple-element.26) | copy-start | bytes 772
  278.3 26.8 %all-to-all-start.9 = ((bf16[4,128,1792]{2,1,0:T(8,128)(2,1)}), bf16[4,128,1792]{2,1,0:T(8,128)(2,1)S(1)}, u32[]{:S(2)}, u32[]{:S(2)}) async-start(bf16[4,128,1792]{2,1,0:T(8,128)(2,1)} %reduce_sum.74), calls=%async_computation.9 | async-start | bytes 3670016 | tf_op jit(solution)/shard_map/all_to_all | solution.py:117
  285.4 20.0 %copy-start.1 = (bf16[128,1792]{1,0:T(8,128)(2,1)S(1)}, bf16[128,1792]{1,0:T(8,128)(2,1)}, u32[]{:S(2)}) copy-start(bf16[128,1792]{1,0:T(8,128)(2,1)} %copy-done) | copy-start | bytes 1376260
Sparse Core Ops, SparseCore 0:
  10.6 128.7 all-gather.1

commit v5 on v3

--- a/solution.py
+++ b/solution.py
@@ -16,62 +16,56 @@
 
 
 def window_attend(queries, key_rows, value_rows, length, window):
-    row_count, head_count, head_size = queries.shape
+    head_count, row_count, head_size = queries.shape
     nb = row_count // window
     score_scale = 1.0 / math.sqrt(head_size)
-    qb = queries.reshape(nb, window, head_count, head_size)
+    qb = queries.reshape(head_count, nb, window, head_size)
 
     def blocks(rows):
-        lo = rows[:row_count].reshape(nb, window, head_count, head_size)
-        hi = rows[window:].reshape(nb, window, head_count, head_size)
-        return jnp.concatenate([lo, hi], axis=1)
+        lo = rows[:, :row_count].reshape(head_count, nb, window, head_size)
+        hi = rows[:, window:].reshape(head_count, nb, window, head_size)
+        return jnp.concatenate([lo, hi], axis=2)
 
     kb = blocks(key_rows)
     vb = blocks(value_rows)
     scores = (
-        jnp.einsum("bqhd,bkhd->bhqk", qb, kb, preferred_element_type=jnp.float32) * score_scale
+        jnp.einsum("hbqd,hbkd->hbqk", qb, kb, preferred_element_type=jnp.float32) * score_scale
     )
     i = jnp.arange(window, dtype=jnp.int32)[:, None]
     j = jnp.arange(2 * window, dtype=jnp.int32)[None, :]
     b = jnp.arange(nb, dtype=jnp.int32)[:, None, None]
     usable = (j > i)[None] & (j <= i + window)[None] & (b * window + j >= window - length)
-    scores = jnp.where(usable[:, None], scores, -1e30)
+    scores = jnp.where(usable[None], scores, -1e30)
     row_max = jnp.max(scores, axis=-1, keepdims=True)
     exponent = jnp.exp(scores - row_max)
     weights = (exponent / jnp.sum(exponent, axis=-1, keepdims=True)).astype(jnp.bfloat16)
-    out = jnp.einsum("bhqk,bkhd->bqhd", weights, vb, preferred_element_type=jnp.float32)
-    return out.reshape(row_count, head_count, head_size)
+    out = jnp.einsum("hbqk,hbkd->hbqd", weights, vb, preferred_element_type=jnp.float32)
+    return out.reshape(head_count, row_count, head_size)
 
 
 def mix_request(projected, cache_rows, length, tap_table, window, head_size):
-    row_count, feat_width = (projected.shape[0], projected.shape[2])
+    _, head_count, row_count, _ = projected.shape
     time_order = (length + jnp.arange(window, dtype=jnp.int32)) % window
-    earlier = cache_rows[:, time_order]
-    key_rows = jnp.concatenate([earlier[0], projected[:, 1]], axis=0)
-    value_rows = jnp.concatenate([earlier[1], projected[:, 2]], axis=0)
-    head_count = feat_width // head_size
-    attended = window_attend(
-        projected[:, 0].reshape(row_count, head_count, head_size),
-        key_rows.reshape(-1, head_count, head_size),
-        value_rows.reshape(-1, head_count, head_size),
-        length,
-        window,
-    ).reshape(row_count, feat_width)
+    earlier = cache_rows[:, time_order].reshape(2, window, head_count, head_size)
+    earlier = earlier.transpose(0, 2, 1, 3)
+    key_rows = jnp.concatenate([earlier[0], projected[1]], axis=1)
+    value_rows = jnp.concatenate([earlier[1], projected[2]], axis=1)
+    attended = window_attend(projected[0], key_rows, value_rows, length, window)
     positions = jnp.arange(window + row_count, dtype=jnp.int32)
-    alive_mask = (positions >= window - length)[:, None]
+    alive_mask = (positions >= window - length)[None, :, None]
     masked_values = jnp.where(alive_mask, value_rows.astype(jnp.float32), jnp.float32(0.0))
     tap_count = tap_table.shape[0]
-    convolved = jnp.zeros((row_count, feat_width), jnp.float32)
+    taps = tap_table.reshape(tap_count, head_count, 1, head_size)
+    convolved = jnp.zeros((head_count, row_count, head_size), jnp.float32)
     for tap_index in range(tap_count):
         begin_row = window - (tap_count - 1) + tap_index
-        convolved = (
-            convolved + tap_table[tap_index] * masked_values[begin_row : begin_row + row_count]
-        )
-    mixed_heads = (attended + projected[:, 3].astype(jnp.float32) * convolved).astype(jnp.bfloat16)
+        convolved = convolved + taps[tap_index] * masked_values[:, begin_row : begin_row + row_count]
+    mixed_heads = (attended + projected[3].astype(jnp.float32) * convolved).astype(jnp.bfloat16)
     slot_source = (
         row_count - window + (jnp.arange(window, dtype=jnp.int32) - length - row_count) % window
     )
-    renewed = jnp.stack([projected[:, 1], projected[:, 2]])[:, slot_source]
+    renewed = projected[1:3][:, :, slot_source].transpose(0, 2, 1, 3)
+    renewed = renewed.reshape(2, window, head_count * head_size)
     return (mixed_heads, renewed)
 
 
@@ -125,11 +119,19 @@
     ffn_all, down_t = gather_packed([ffn_weight.reshape(rows, -1), down_weight.T])
     normed_all = tp_gather(normed(tokens, norm_gain))
     row_total = normed_all.shape[0]
-    projected = jnp.dot(normed_all, mix_all, preferred_element_type=jnp.float32)
-    projected = projected.astype(jnp.bfloat16).reshape(row_total, 4, feat_width)
+    heads = feat_width // HD
+    projected = jnp.einsum(
+        "td,djhe->jhte",
+        normed_all,
+        mix_all.reshape(-1, 4, heads, HD),
+        preferred_element_type=jnp.float32,
+    ).astype(jnp.bfloat16)
     mixed_heads, renewed = mix_request(projected, past_cache[0], cached_len[0], conv_taps, WIN, HD)
-    attn_full = lax.dot_general(
-        mixed_heads, out_t, (((1,), (1,)), ((), ())), preferred_element_type=jnp.float32
+    attn_full = jnp.einsum(
+        "htd,fhd->tf",
+        mixed_heads,
+        out_t.reshape(out_t.shape[0], heads, HD),
+        preferred_element_type=jnp.float32,
     )
     attn_part = tp_sum_scatter(attn_full.astype(jnp.bfloat16))
     residual = (tokens.astype(jnp.float32) + attn_part).astype(jnp.bfloat16)

time: 272 us -> 288 us (1.059)
  local copies, waits for them, and re-layouts: 29.6 us -> 41.5 us
  waiting for transfers between devices: 73.1 us -> 77.9 us
  other arithmetic: 19.4 us -> 16.4 us
    slice x2 -> x14, local copies, waits for them, and re-layouts: 0.1 us -> 18.8 us  [the longest x5 8.3 us: gather_packed(): parts.append(got[:, start:start + w])]
    all_to_all x1, waiting for transfers between devices: 14 us -> 18.5 us  [tp_sum_scatter(): chips = lax.all_to_all(pair, 'tpx', 0, 0, tiled=True)]
    another operation x1 -> x0, other arithmetic: 3.44 us -> none  [mix_request(): renewed = jnp.stack([projected[:, 1], projected[:, 2]])[:, slot_source]]
    unnamed x28 -> x13, local copies, waits for them, and re-layouts: 4.72 us -> 1.69 us
    another operation x5 -> x3, local copies, waits for them, and re-layouts: 7.6 us -> 4.73 us  [the longest x2 4.6 us: blocks(): hi = rows[:, window:].reshape(head_count, nb, window, head_size)]
    reshape x8 -> x3, local copies, waits for them, and re-layouts: 5.98 us -> 4.26 us  [the longest x2 2.71 us: blocks(): lo = rows[:, :row_count].reshape(head_count, nb, window, head_size)]
  transfers between devices with their start and end apart: 4 -> 4, of which waited for: 3 -> 3; matrix products, arithmetic and copies ran while one was open for 22% -> 25% of each run, Pallas kernels for 0% -> 0%
where the time goes in v5:
time: 288 us; the launch traced here: 287 us
  blocking collectives  87.4 us (30%)
  waiting for transfers between devices  77.9 us (27%)
  local copies, waits for them, and re-layouts  41.5 us (14%)
  matrix products  39.8 us (14%)
  other arithmetic  16.4 us (6%)
  between operations  15 us (5%)
  starting transfers between devices  8.64 us (3%)
    all_gather x2, waiting for transfers between devices, gather_packed(): lax.all_gather(jnp.concatenate(pieces, axis=1), 'req', axis=0, tiled=True)  40 us
    all_to_all x1, blocking collectives, tp_sum_scatter(): chips = lax.all_to_all(pair, 'tpx', 0, 0, tiled=True)  26.6 us
    all_to_all x1, blocking collectives, tp_gather(): lax.all_to_all(jnp.tile(x[None], (nx, 1, 1)), 'tpx', 0, 0, tiled=True)  24.2 us
    all_to_all x1, waiting for transfers between devices, tp_gather(): lax.all_to_all(jnp.tile(x[None], (nx, 1, 1)), 'tpx', 0, 0, tiled=True)  19.4 us
    all_to_all x1, waiting for transfers between devices, tp_sum_scatter(): chips = lax.all_to_all(pair, 'tpx', 0, 0, tiled=True)  18.5 us
    all_to_all x2, blocking collectives, tp_sum_scatter(): pair = lax.all_to_all(parts, 'tpc', 1, 1, tiled=True)  18.4 us
    all_to_all x2, blocking collectives, tp_gather(): got = lax.all_to_all(both, 'tpc', 1, 1, tiled=True)  18.2 us
    dot_general x1, matrix products, local(): gate_up = jnp.dot(ffn_in, ffn_all, preferred_element_type=jnp.float32)  10.7 us
  transfers between devices with their start and end apart: 4, of which 3 were waited for; matrix products, arithmetic and copies ran while one was open for 25% of the time, Pallas kernels for 0%

profile of v5, /device:TPU:1, one launch (start us, length us, event | category | flops | bytes accessed | tf_op | source)
XLA Modules:
  0.0 286.7 jit_solution(13522672934878920422)
XLA Ops:
  16.2 4.8 %all-to-all-start = ((bf16[4,128,1792]{2,1,0:T(8,128)(2,1)}), bf16[4,128,1792]{2,1,0:T(8,128)(2,1)S(1)}, u32[]{:S(2)}, u32[]{:S(2)}) async-start(bf16[4,128,1792]{2,1,0:T(8,128)(2,1)} %tile.4), calls=%async_computation | async-start | bytes 3670016 | tf_op jit(solution)/shard_map/all_to_all | solution.py:86
  23.2 19.4 %all-to-all-done = bf16[4,128,1792]{2,1,0:T(8,128)(2,1)S(1)} async-done(((bf16[4,128,1792]{2,1,0:T(8,128)(2,1)}), bf16[4,128,1792]{2,1,0:T(8,128)(2,1)S(1)}, u32[]{:S(2)}, u32[]{:S(2)}) %all-to-all-start) | async-done | bytes 1835040 | tf_op jit(solution)/shard_map/all_to_all | solution.py:86
  42.9 9.2 %all_to_all.40 = bf16[4,2,128,1792]{3,2,0,1:T(8,128)(2,1)S(1)} all-to-all(bf16[4,2,128,1792]{3,2,0,1:T(8,128)(2,1)S(1)} %broadcast_in_dim.25), channel_id=1, replica_groups=mesh['req'=32,'tpx'=4,'tpc'=2] {'tpc'}, dimensions={1} | all-to-all | bytes 7340032 | tf_op jit(solution)/shard_map/all_to_all | solution.py:88
  52.1 2.0 copy.78
  54.1 40.0 %all-gather.3.cloned.1.call-done = bf16[1792,1120]{1,0:T(8,128)(2,1)} async-done(((bf16[56,1120]{1,0:T(8,128)(2,1)}), bf16[1792,1120]{1,0:T(8,128)(2,1)}) %all-gather.3.cloned.1.call-update) | async-done | bytes 4014096 | tf_op jit(solution)/shard_map/all_gather | solution.py:74
  94.1 2.2 slice.103
  96.3 2.4 copy.91
  98.6 3.8 %copy.77 = bf16[1792,896]{0,1:T(8,128)(2,1)} copy(bf16[1792,896]{1,0:T(8,128)(2,1)S(1)} %slice-done) | data formatting | bytes 6422528 | tf_op jit(solution)/shard_map/slice | solution.py:78
  102.4 6.5 %convert_bitcast_fusion = bf16[4,2,1024,112]{2,3,1,0:T(8,128)(2,1)S(1)} fusion(bf16[1792,4,2,112]{0,3,2,1:T(8,128)(2,1)} %bitcast.67, bf16[1024,1792,1,1]{1,0,3,2:T(8,128)(2,1)} %bitcast.64), kind=kOutput, calls=%fused_computation.13 | convolution fusion | flops 3289251840 | bytes 8716288 | tf_op jit(solution)/shard_map/td,djhe->jhte/dot_general | solution.py:123
  116.6 2.0 copy.87
  118.6 2.3 copy.89
  120.9 2.1 copy.83
  123.0 2.3 copy.85
  125.3 2.0 copy.79
  127.3 2.4 fusion.52
  129.7 3.1 %fusion.8 = f32[2,16,64,128]{3,2,1,0:T(8,128)} fusion(bf16[2,16,64,112]{3,2,1,0:T(8,128)(2,1)} %bitcast.70, bf16[2,16,64,112]{2,3,1,0:T(8,128)(2,1)} %copy.85, bf16[2,16,64,112]{2,3,1,0:T(8,128)(2,1)S(1)} %copy.84, pred[16,64,128]{2,1,0:T(8,128)(4,1)S(1)} %broadcast_and_fusion), kind=kOutput, calls=%fused_computation.22 | convolution fusion | flops 61079552 | bytes 2555904 | tf_op jit(solution)/shard_map/hbqd,hbkd->hbqk/dot_general | solution.py:32
  132.8 7.2 %fusion.26 = f32[2,16,64,112]{3,2,1,0:T(8,128)} fusion(bf16[2,16,64,112]{2,3,1,0:T(8,128)(2,1)} %copy.89, bf16[2,16,64,112]{2,3,1,0:T(8,128)(2,1)} %copy.88, f32[2,16,64]{2,1,0:T(8,128)S(1)} %fusion.52, f32[2,16,64,128]{3,2,1,0:T(8,128)} %fusion.8), kind=kOutput, calls=%fused_computation.45 | convolution fusion | flops 61343872 | bytes 2891776 | tf_op jit(solution)/shard_map/hbqk,hbkd->hbqd/dot_general | solution.py:42
  141.9 3.2 %bitcast_convert_fusion = bf16[1024,1792]{1,0:T(8,128)(2,1)S(1)} fusion(bf16[1792,2,112]{0,2,1:T(8,128)(2,1)} %bitcast.68, f32[2,1024,112]{1,2,0:T(8,128)S(1)} %copy.90, f32[2,1088,112]{1,2,0:T(8,128)S(1)} %convert_select_fusion, bf16[4,2,1024,112]{2,3,1,0:T(8,128)(2,1)S(1)} %convert_bitcast_fusion, f32[2,112]{1,0:T(2,128)S(1)} %mul.106, ...), kind=kOutput, calls=%fused_computation.3 | convolution fusion | flops 825982976 | bytes 8604672 | tf_op jit(solution)/shard_map/htd,fhd->tf/dot_general | solution.py:130
  145.3 10.7 %all_to_all.41 = bf16[4,2,128,1792]{3,2,0,1:T(8,128)(2,1)} all-to-all(bf16[4,2,128,1792]{3,2,0,1:T(8,128)(2,1)S(1)} %copy.92), channel_id=1, replica_groups=mesh['req'=32,'tpx'=4,'tpc'=2] {'tpc'}, dimensions={1} | all-to-all | bytes 7340032 | tf_op jit(solution)/shard_map/all_to_all | solution.py:97
  156.0 2.9 %reduce_sum.71 = bf16[4,128,1792]{2,1,0:T(8,128)(2,1)S(1)} reduce(bf16[4,2,128,1792]{3,2,0,1:T(8,128)(2,1)} %all_to_all.41, bf16[]{:T(256)} %constant.46.clone.1), dimensions={1}, to_apply=%region_3.4 | reduce | flops 917504 | bytes 5505026 | tf_op jit(solution)/shard_map/reduce_sum | solution.py:98
  159.0 26.6 %all_to_all.42 = bf16[4,128,1792]{2,1,0:T(8,128)(2,1)S(1)} all-to-all(bf16[4,128,1792]{2,1,0:T(8,128)(2,1)S(1)} %reduce_sum.71), channel_id=1, replica_groups=mesh['req'=32,'tpx'=4,'tpc'=2] {'tpx'}, dimensions={0} | all-to-all | bytes 3670016 | tf_op jit(solution)/shard_map/all_to_all | solution.py:99
  186.4 24.2 %all_to_all.43 = bf16[4,128,1792]{2,1,0:T(8,128)(2,1)S(1)} all-to-all(bf16[4,128,1792]{2,1,0:T(8,128)(2,1)S(1)} %tile.5), channel_id=1, replica_groups=mesh['req'=32,'tpx'=4,'tpc'=2] {'tpx'}, dimensions={0} | all-to-all | bytes 3670016 | tf_op jit(solution)/shard_map/all_to_all | solution.py:86
  210.9 9.0 %all_to_all.44 = bf16[4,2,128,1792]{3,2,0,1:T(8,128)(2,1)S(1)} all-to-all(bf16[4,2,128,1792]{3,2,0,1:T(8,128)(2,1)S(1)} %broadcast_in_dim.33), channel_id=1, replica_groups=mesh['req'=32,'tpx'=4,'tpc'=2] {'tpc'}, dimensions={1} | all-to-all | bytes 7340032 | tf_op jit(solution)/shard_map/all_to_all | solution.py:88
  219.9 2.1 copy.93
  222.0 10.7 %fusion.1 = f32[1024,1792]{1,0:T(8,128)S(1)} fusion(bf16[1024,1792]{1,0:T(8,128)(2,1)} %bitcast.65, bf16[1792,2688]{1,0:T(8,128)(2,1)} %all-gather.5.cloned.1.call-done), kind=kOutput, calls=%fused_computation.4 | convolution fusion | flops 6576668672 | bytes 17432576 | tf_op jit(solution)/shard_map/dot_general | solution.py:139
  232.8 6.6 %convolution_convert_fusion = bf16[1024,1792]{1,0:T(8,128)(2,1)S(1)} fusion(bf16[1792,2688]{1,0:T(8,128)(2,1)} %all-gather.5.cloned.1.call-done, f32[1024,1792]{1,0:T(8,128)S(1)} %fusion.1), kind=kOutput, calls=%fused_computation.6 | convolution fusion | flops 3295674368 | bytes 14221312 | tf_op jit(solution)/shard_map/dot_general | solution.py:141
  239.7 7.7 %all_to_all.45 = bf16[4,2,128,1792]{3,2,0,1:T(8,128)(2,1)} all-to-all(bf16[4,2,128,1792]{3,2,0,1:T(8,128)(2,1)S(1)} %copy.94), channel_id=1, replica_groups=mesh['req'=32,'tpx'=4,'tpc'=2] {'tpc'}, dimensions={1} | all-to-all | bytes 7340032 | tf_op jit(solution)/shard_map/all_to_all | solution.py:97
  247.4 4.4 %reduce_sum.74 = bf16[4,128,1792]{2,1,0:T(8,128)(2,1)} reduce(bf16[4,2,128,1792]{3,2,0,1:T(8,128)(2,1)} %all_to_all.45, bf16[]{:T(256)} %constant.46.clone.1), dimensions={1}, to_apply=%region_6.7 | reduce | flops 917504 | bytes 5505026 | tf_op jit(solution)/shard_map/reduce_sum | solution.py:98
  251.8 3.7 %all-to-all-start.7 = ((bf16[4,128,1792]{2,1,0:T(8,128)(2,1)}), bf16[4,128,1792]{2,1,0:T(8,128)(2,1)S(1)}, u32[]{:S(2)}, u32[]{:S(2)}) async-start(bf16[4,128,1792]{2,1,0:T(8,128)(2,1)} %reduce_sum.74), calls=%async_computation.7 | async-start | bytes 3670016 | tf_op jit(solution)/shard_map/all_to_all | solution.py:99
  255.6 2.0 copy.95
  257.6 2.0 gather_fusion.1
  260.3 18.5 %all-to-all-done.7 = bf16[4,128,1792]{2,1,0:T(8,128)(2,1)S(1)} async-done(((bf16[4,128,1792]{2,1,0:T(8,128)(2,1)}), bf16[4,128,1792]{2,1,0:T(8,128)(2,1)S(1)}, u32[]{:S(2)}, u32[]{:S(2)}) %all-to-all-start.7) | async-done | bytes 1835040 | tf_op jit(solution)/shard_map/all_to_all | solution.py:99
  (66 shorter events, 23.6 us)
Async XLA Ops:
  7.2 86.9 %all-gather.3.cloned.1.call-start = ((), (), s32[]{:S(2)}) async-start(), calls=%async_computation.8 | async-start | bytes 4257792 | tf_op jit(solution)/shard_map/all_gather | solution.py:74
  9.7 212.3 %all-gather.5.cloned.1.call-start = ((), (), s32[]{:S(2)}) async-start(), calls=%async_computation.9 | async-start | bytes 9934848 | tf_op jit(solution)/shard_map/all_gather | solution.py:74
  12.4 9.3 %copy-start.4 = (f32[3,224]{1,0:T(4,128)S(1)}, f32[3,224]{1,0:T(4,128)}, u32[]{:S(2)}) copy-start(f32[3,224]{1,0:T(4,128)} %param.17) | copy-start | bytes 8068
  12.4 9.6 %copy-start.2 = (bf16[1,2,64,224]{3,2,1,0:T(8,128)(2,1)S(1)}, bf16[1,2,64,224]{3,2,1,0:T(8,128)(2,1)}, u32[]{:S(2)}) copy-start(bf16[1,2,64,224]{3,2,1,0:T(8,128)(2,1)} %param.18) | copy-start | bytes 172036
  16.2 26.4 %all-to-all-start = ((bf16[4,128,1792]{2,1,0:T(8,128)(2,1)}), bf16[4,128,1792]{2,1,0:T(8,128)(2,1)S(1)}, u32[]{:S(2)}, u32[]{:S(2)}) async-start(bf16[4,128,1792]{2,1,0:T(8,128)(2,1)} %tile.4), calls=%async_computation | async-start | bytes 3670016 | tf_op jit(solution)/shard_map/all_to_all | solution.py:86
  96.3 2.4 slice-start
  108.9 32.9 %copy-start = (bf16[4,2,1024,112]{2,3,1,0:T(8,128)(2,1)}, bf16[4,2,1024,112]{2,3,1,0:T(8,128)(2,1)S(1)}, u32[]{:S(2)}) copy-start(bf16[4,2,1024,112]{2,3,1,0:T(8,128)(2,1)S(1)} %convert_bitcast_fusion) | copy-start | bytes 5505028
  158.9 26.9 %copy-start.1 = (bf16[128,1792]{1,0:T(8,128)(2,1)S(1)}, bf16[128,1792]{1,0:T(8,128)(2,1)}, u32[]{:S(2)}) copy-start(bf16[128,1792]{1,0:T(8,128)(2,1)} %param.10) | copy-start | bytes 1376260
  159.0 27.1 %copy-start.3 = (f32[1792]{0:T(1024)S(1)}, f32[1792]{0:T(1024)}, u32[]{:S(2)}) copy-start(f32[1792]{0:T(1024)} %param.12) | copy-start | bytes 21508
  251.8 3.8 %slice-start.1 = ((bf16[4,2,1024,112]{2,3,1,0:T(8,128)(2,1)}), bf16[2,2,1024,112]{2,3,1,0:T(8,128)(2,1)S(1)}, s32[]{:S(2)}) async-start(bf16[4,2,1024,112]{2,3,1,0:T(8,128)(2,1)} %copy-done), calls=%async_computation.11 | async-start | bytes 1835008 | tf_op jit(solution)/shard_map/slice | solution.py:67
  251.8 27.0 %all-to-all-start.7 = ((bf16[4,128,1792]{2,1,0:T(8,128)(2,1)}), bf16[4,128,1792]{2,1,0:T(8,128)(2,1)S(1)}, u32[]{:S(2)}, u32[]{:S(2)}) async-start(bf16[4,128,1792]{2,1,0:T(8,128)(2,1)} %reduce_sum.74), calls=%async_computation.7 | async-start | bytes 3670016 | tf_op jit(solution)/shard_map/all_to_all | solution.py:99
Sparse Core Ops, SparseCore 0:
  11.2 82.8 all-gather.2
  96.7 103.9 all-gather.4

commit v6 on v3

--- a/solution.py
+++ b/solution.py
@@ -86,10 +86,44 @@
     return parts
 
 
+def ring_pass(x, axis, step):
+    n = lax.axis_size(axis)
+    return lax.ppermute(x, axis, [(i, (i + step) % n) for i in range(n)])
+
+
+def x_gather(x):
+    n = lax.axis_size("tpx")
+    me = lax.axis_index("tpx")
+    half = x.shape[-1] // 2
+    from_left = ring_pass(x, "tpx", 1)
+    from_right = ring_pass(x, "tpx", -1)
+    far_a = ring_pass(from_left[..., :half], "tpx", 1)
+    far_b = ring_pass(from_right[..., half:], "tpx", -1)
+    far = jnp.concatenate([far_a, far_b], axis=-1)
+    rel = jnp.stack([x, from_right, far, from_left])
+    both = jnp.concatenate([rel, rel], axis=0)
+    return lax.dynamic_slice_in_dim(both, (n - me) % n, n, axis=0)
+
+
+def x_sum_scatter(parts):
+    n = lax.axis_size("tpx")
+    me = lax.axis_index("tpx")
+    both = jnp.concatenate([parts, parts], axis=0)
+    rel = lax.dynamic_slice_in_dim(both, me, n, axis=0)
+    half = parts.shape[-1] // 2
+    from_left = ring_pass(rel[1], "tpx", 1)
+    from_right = ring_pass(rel[3], "tpx", -1)
+    far_a = ring_pass(ring_pass(rel[2][..., :half], "tpx", 1), "tpx", 1)
+    far_b = ring_pass(ring_pass(rel[2][..., half:], "tpx", -1), "tpx", -1)
+    far = jnp.concatenate([far_a, far_b], axis=-1)
+    f32 = jnp.float32
+    return rel[0].astype(f32) + from_left.astype(f32) + from_right.astype(f32) + far.astype(f32)
+
+
 def tp_gather(x):
     nx = lax.axis_size("tpx")
     nc = lax.axis_size("tpc")
-    by_chip = lax.all_to_all(jnp.tile(x[None], (nx, 1, 1)), "tpx", 0, 0, tiled=True)
+    by_chip = x_gather(x)
     both = jnp.broadcast_to(by_chip[:, None], (nx, nc) + x.shape)
     got = lax.all_to_all(both, "tpc", 1, 1, tiled=True)
     return got.reshape((nx * nc * x.shape[0],) + x.shape[1:])
@@ -102,8 +136,7 @@
     parts = x.reshape((nx, nc, rows) + x.shape[1:])
     pair = lax.all_to_all(parts, "tpc", 1, 1, tiled=True)
     pair = pair.astype(jnp.float32).sum(axis=1).astype(jnp.bfloat16)
-    chips = lax.all_to_all(pair, "tpx", 0, 0, tiled=True)
-    return chips.astype(jnp.float32).sum(axis=0)
+    return x_sum_scatter(pair)
 
 
 def local(

time: 272 us -> 272 us (level); the launches traced: 271 us -> 267 us
  blocking collectives: 87.3 us -> 37.2 us
  starting transfers between devices: 8.51 us -> 28.3 us
  waiting for transfers between devices: 73.1 us -> 84.8 us
  other arithmetic: 19.4 us -> 26.4 us
  local copies, waits for them, and re-layouts: 29.6 us -> 36.5 us
    all_to_all x2 -> x0, blocking collectives: 50.8 us -> none  [the longest x1 26.6 us: tp_sum_scatter(): chips = lax.all_to_all(pair, 'tpx', 0, 0, tiled=True)]
    ppermute x0 -> x20, waiting for transfers between devices: none -> 44.4 us  [ring_pass(): return lax.ppermute(x, axis, [(i, (i + step) % n) for i in range(n)])]
    all_to_all x2 -> x0, waiting for transfers between devices: 33 us -> none  [the longest x1 19.1 us: tp_gather(): lax.all_to_all(jnp.tile(x[None], (nx, 1, 1)), 'tpx', 0, 0, tiled=True)]
    ppermute x0 -> x20, starting transfers between devices: none -> 28.2 us  [ring_pass(): return lax.ppermute(x, axis, [(i, (i + step) % n) for i in range(n)])]
    all_to_all x2 -> x0, starting transfers between devices: 8.43 us -> none  [the longest x1 4.84 us: tp_gather(): lax.all_to_all(jnp.tile(x[None], (nx, 1, 1)), 'tpx', 0, 0, tiled=True)]
    unnamed x0 -> x6, other arithmetic: none -> 3.86 us
    concatenate x0 -> x2, other arithmetic: none -> 2.82 us  [x_sum_scatter(): both = jnp.concatenate([parts, parts], axis=0)]
    unnamed x28 -> x26, local copies, waits for them, and re-layouts: 4.72 us -> 5.52 us
  transfers between devices with their start and end apart: 4 -> 22, of which waited for: 3 -> 10; matrix products, arithmetic and copies ran while one was open for 22% -> 27% of each run, Pallas kernels for 0% -> 0%
where the time goes in v6:
time: 272 us; the launch traced here: 267 us
  waiting for transfers between devices  84.8 us (31%)
  matrix products  38.3 us (14%)
  blocking collectives  37.2 us (14%)
  local copies, waits for them, and re-layouts  36.5 us (13%)
  starting transfers between devices  28.3 us (10%)
  other arithmetic  26.4 us (10%)
  between operations  15.5 us (6%)
    ppermute x20, waiting for transfers between devices, ring_pass(): return lax.ppermute(x, axis, [(i, (i + step) % n) for i in range(n)])  44.4 us
    all_gather x2, waiting for transfers between devices, gather_packed(): lax.all_gather(jnp.concatenate(pieces, axis=1), 'req', axis=0, tiled=True)  40.4 us
    ppermute x20, starting transfers between devices, ring_pass(): return lax.ppermute(x, axis, [(i, (i + step) % n) for i in range(n)])  28.2 us
    all_to_all x2, blocking collectives, tp_sum_scatter(): pair = lax.all_to_all(parts, 'tpc', 1, 1, tiled=True)  19 us
    all_to_all x2, blocking collectives, tp_gather(): got = lax.all_to_all(both, 'tpc', 1, 1, tiled=True)  18.2 us
    dot_general x1, matrix products, local(): gate_up = jnp.dot(ffn_in, ffn_all, preferred_element_type=jnp.float32)  10.7 us
    reduce_sum x2, other arithmetic, tp_sum_scatter(): pair = pair.astype(jnp.float32).sum(axis=1).astype(jnp.bfloat16)  7.36 us
    dot_general x1, matrix products, local(): lax.dot_general(activated, down_t, (((1,), (1,)), ((), ())), preferred_el...  6.61 us
  transfers between devices with their start and end apart: 22, of which 10 were waited for; matrix products, arithmetic and copies ran while one was open for 27% of the time, Pallas kernels for 0%

profile of v6, /device:TPU:1, one launch (start us, length us, event | category | flops | bytes accessed | tf_op | source)
XLA Modules:
  0.0 267.0 jit_solution(9797429189071806517)
XLA Ops:
  15.6 3.3 %collective-permute-start = (bf16[128,1792]{1,0:T(8,128)(2,1)S(1)}, bf16[128,1792]{1,0:T(8,128)(2,1)S(1)}, u32[]{:S(2)}, u32[]{:S(2)}) collective-permute-start(bf16[128,1792]{1,0:T(8,128)(2,1)S(1)} %get-tuple-element.15), channel_id=1, source_target_pairs={{0,6},{2,0},{4,2},{6,4},{1,7},{3,1},{5,3},{7,5},{8,14},{10,8},{12,... | collective-permute-start | bytes 1376264 | tf_op jit(solution)/shard_map/ppermute | solution.py:91
  20.9 10.2 %collective-permute-done.1 = bf16[128,1792]{1,0:T(8,128)(2,1)S(1)} collective-permute-done((bf16[128,1792]{1,0:T(8,128)(2,1)S(1)}, bf16[128,1792]{1,0:T(8,128)(2,1)S(1)}, u32[]{:S(2)}, u32[]{:S(2)}) %collective-permute-start.1) | collective-permute-done | bytes 458784 | tf_op jit(solution)/shard_map/ppermute | solution.py:91
  31.3 2.7 %collective-permute-start.3 = (bf16[128,896]{1,0:T(8,128)(2,1)S(1)}, bf16[128,896]{1,0:T(8,128)(2,1)S(1)}, u32[]{:S(2)}, u32[]{:S(2)}) collective-permute-start(bf16[128,896]{1,0:T(8,128)(2,1)S(1)} %slice.160), channel_id=1, source_target_pairs={{0,6},{2,0},{4,2},{6,4},{1,7},{3,1},{5,3},{7,5},{8,14},{10,8},{12,... | collective-permute-start | bytes 688136 | tf_op jit(solution)/shard_map/ppermute | solution.py:91
  34.9 2.9 %collective-permute-done.2 = bf16[128,896]{1,0:T(8,128)(2,1)S(1)} collective-permute-done((bf16[128,896]{1,0:T(8,128)(2,1)S(1)}, bf16[128,896]{1,0:T(8,128)(2,1)S(1)}, u32[]{:S(2)}, u32[]{:S(2)}) %collective-permute-start.2) | collective-permute-done | bytes 229408 | tf_op jit(solution)/shard_map/ppermute | solution.py:91
  44.6 9.2 %all_to_all.20 = bf16[4,2,128,1792]{3,2,0,1:T(8,128)(2,1)S(1)} all-to-all(bf16[4,2,128,1792]{3,2,0,1:T(8,128)(2,1)S(1)} %broadcast_in_dim.26), channel_id=1, replica_groups=mesh['req'=32,'tpx'=4,'tpc'=2] {'tpc'}, dimensions={1} | all-to-all | bytes 7340032 | tf_op jit(solution)/shard_map/all_to_all | solution.py:128
  55.8 38.3 %all-gather.3.cloned.1.call-done = bf16[1792,1120]{1,0:T(8,128)(2,1)} async-done(((bf16[56,1120]{1,0:T(8,128)(2,1)}), bf16[1792,1120]{1,0:T(8,128)(2,1)}) %all-gather.3.cloned.1.call-update) | async-done | bytes 4014096 | tf_op jit(solution)/shard_map/all_gather | solution.py:80
  94.1 6.6 %fusion.11 = bf16[1024,896]{0,1:T(8,128)(2,1)S(1)} fusion(bf16[1024,1792]{1,0:T(8,128)(2,1)} %bitcast.112, bf16[1792,1120]{1,0:T(8,128)(2,1)} %all-gather.3.cloned.1.call-done), kind=kOutput, calls=%fused_computation.19 | convolution fusion | flops 3289251840 | bytes 8716288 | tf_op jit(solution)/shard_map/dot_general | solution.py:161
  110.8 2.6 copy.66
  113.4 2.5 fusion.77
  115.9 3.0 %fusion.16 = f32[16,2,64,128]{3,2,1,0:T(8,128)} fusion(bf16[16,64,2,112]{1,3,2,0:T(8,128)(2,1)S(1)} %copy.72, bf16[16,64,2,112]{1,3,2,0:T(8,128)(2,1)S(1)} %copy.71, bf16[16,64,2,112]{1,0,3,2:T(8,128)(2,1)} %reshape.283, pred[16,64,128]{2,1,0:T(8,128)(4,1)S(1)} %broadcast_and_fusion), kind=kOutput, calls=%fused_computation.29 | convolution fusion | flops 61079552 | bytes 2555904 | tf_op jit(solution)/shard_map/bqhd,bkhd->bhqk/dot_general | solution.py:32
  118.9 6.3 %convolution_bitcast_fusion = f32[16,64,2,112]{3,1,2,0:T(8,128)S(1)} fusion(bf16[16,64,2,112]{1,3,2,0:T(8,128)(2,1)} %copy.66, bf16[16,64,2,112]{1,3,2,0:T(8,128)(2,1)} %copy.65, f32[16,2,64]{2,1,0:T(2,128)S(1)} %fusion.77, f32[16,2,64,128]{3,2,1,0:T(8,128)} %fusion.16), kind=kOutput, calls=%fused_computation.30 | convolution fusion | flops 61343872 | bytes 2891776 | tf_op jit(solution)/shard_map/bhqk,bkhd->bqhd/dot_general | solution.py:42
  127.1 2.6 convolution_convert_fusion.1
  130.0 10.6 %all_to_all.21 = bf16[4,2,128,1792]{3,2,0,1:T(8,128)(2,1)} all-to-all(bf16[4,2,128,1792]{3,2,0,1:T(8,128)(2,1)S(1)} %copy.76), channel_id=1, replica_groups=mesh['req'=32,'tpx'=4,'tpc'=2] {'tpc'}, dimensions={1} | all-to-all | bytes 7340032 | tf_op jit(solution)/shard_map/all_to_all | solution.py:137
  140.5 2.9 %reduce_sum.53 = bf16[4,128,1792]{2,1,0:T(8,128)(2,1)S(1)} reduce(bf16[4,2,128,1792]{3,2,0,1:T(8,128)(2,1)} %all_to_all.21, bf16[]{:T(256)} %constant.69.clone.1), dimensions={1}, to_apply=%region_3.4 | reduce | flops 917504 | bytes 5505026 | tf_op jit(solution)/shard_map/reduce_sum | solution.py:138
  147.0 2.7 %collective-permute-start.5 = (bf16[128,1792]{1,0:T(8,128)(2,1)S(1)}, bf16[128,1792]{1,0:T(8,128)(2,1)S(1)}, u32[]{:S(2)}, u32[]{:S(2)}) collective-permute-start(bf16[128,1792]{1,0:T(8,128)(2,1)S(1)} %get-tuple-element.26), channel_id=1, source_target_pairs={{0,6},{2,0},{4,2},{6,4},{1,7},{3,1},{5,3},{7,5},{8,14},{10,8},{12,... | collective-permute-start | bytes 1376264 | tf_op jit(solution)/shard_map/ppermute | solution.py:91
  149.7 2.8 %collective-permute-done.6 = bf16[128,896]{1,0:T(8,128)(2,1)S(1)} collective-permute-done((bf16[128,896]{1,0:T(8,128)(2,1)S(1)}, bf16[128,896]{1,0:T(8,128)(2,1)S(1)}, u32[]{:S(2)}, u32[]{:S(2)}) %collective-permute-start.6) | collective-permute-done | bytes 229408 | tf_op jit(solution)/shard_map/ppermute | solution.py:91
  152.7 2.7 collective-permute-start.9
  155.3 11.9 %collective-permute-done.7 = bf16[128,896]{1,0:T(8,128)(2,1)S(1)} collective-permute-done((bf16[128,896]{1,0:T(8,128)(2,1)S(1)}, bf16[128,896]{1,0:T(8,128)(2,1)S(1)}, u32[]{:S(2)}, u32[]{:S(2)}) %collective-permute-start.7) | collective-permute-done | bytes 229408 | tf_op jit(solution)/shard_map/ppermute | solution.py:91
  170.7 9.6 %collective-permute-done.11 = bf16[128,1792]{1,0:T(8,128)(2,1)S(1)} collective-permute-done((bf16[128,1792]{1,0:T(8,128)(2,1)S(1)}, bf16[128,1792]{1,0:T(8,128)(2,1)S(1)}, u32[]{:S(2)}, u32[]{:S(2)}) %collective-permute-start.11) | collective-permute-done | bytes 458784 | tf_op jit(solution)/shard_map/ppermute | solution.py:91
  180.4 2.7 %collective-permute-start.13 = (bf16[128,896]{1,0:T(8,128)(2,1)S(1)}, bf16[128,896]{1,0:T(8,128)(2,1)S(1)}, u32[]{:S(2)}, u32[]{:S(2)}) collective-permute-start(bf16[128,896]{1,0:T(8,128)(2,1)S(1)} %slice.180), channel_id=1, source_target_pairs={{0,6},{2,0},{4,2},{6,4},{1,7},{3,1},{5,3},{7,5},{8,14},{10,8},{12,... | collective-permute-start | bytes 688136 | tf_op jit(solution)/shard_map/ppermute | solution.py:91
  183.1 3.7 %collective-permute-done.12 = bf16[128,896]{1,0:T(8,128)(2,1)S(1)} collective-permute-done((bf16[128,896]{1,0:T(8,128)(2,1)S(1)}, bf16[128,896]{1,0:T(8,128)(2,1)S(1)}, u32[]{:S(2)}, u32[]{:S(2)}) %collective-permute-start.12) | collective-permute-done | bytes 229408 | tf_op jit(solution)/shard_map/ppermute | solution.py:91
  187.5 9.0 %all_to_all.22 = bf16[4,2,128,1792]{3,2,0,1:T(8,128)(2,1)S(1)} all-to-all(bf16[4,2,128,1792]{3,2,0,1:T(8,128)(2,1)S(1)} %broadcast_in_dim.35), channel_id=1, replica_groups=mesh['req'=32,'tpx'=4,'tpc'=2] {'tpc'}, dimensions={1} | all-to-all | bytes 7340032 | tf_op jit(solution)/shard_map/all_to_all | solution.py:128
  200.8 10.7 %fusion.1 = f32[1024,1792]{1,0:T(8,128)S(1)} fusion(bf16[1024,1792]{1,0:T(8,128)(2,1)} %bitcast.113, bf16[1792,2688]{1,0:T(8,128)(2,1)} %all-gather.5.cloned.1.call-done), kind=kOutput, calls=%fused_computation.3 | convolution fusion | flops 6576668672 | bytes 17432576 | tf_op jit(solution)/shard_map/dot_general | solution.py:170
  211.5 6.6 %convolution_convert_fusion = bf16[1024,1792]{1,0:T(8,128)(2,1)S(1)} fusion(bf16[1792,2688]{1,0:T(8,128)(2,1)} %all-gather.5.cloned.1.call-done, f32[1024,1792]{1,0:T(8,128)S(1)} %fusion.1), kind=kOutput, calls=%fused_computation.5 | convolution fusion | flops 3295674368 | bytes 14221312 | tf_op jit(solution)/shard_map/dot_general | solution.py:172
  218.4 8.4 %all_to_all.23 = bf16[4,2,128,1792]{3,2,0,1:T(8,128)(2,1)} all-to-all(bf16[4,2,128,1792]{3,2,0,1:T(8,128)(2,1)S(1)} %copy.78), channel_id=1, replica_groups=mesh['req'=32,'tpx'=4,'tpc'=2] {'tpc'}, dimensions={1} | all-to-all | bytes 7340032 | tf_op jit(solution)/shard_map/all_to_all | solution.py:137
  226.8 4.4 %reduce_sum.55 = bf16[4,128,1792]{2,1,0:T(8,128)(2,1)} reduce(bf16[4,2,128,1792]{3,2,0,1:T(8,128)(2,1)} %all_to_all.23, bf16[]{:T(256)} %constant.69.clone.1), dimensions={1}, to_apply=%region_5.6 | reduce | flops 917504 | bytes 5505026 | tf_op jit(solution)/shard_map/reduce_sum | solution.py:138
  237.2 2.7 %collective-permute-start.15 = (bf16[128,1792]{1,0:T(8,128)(2,1)}, bf16[128,1792]{1,0:T(8,128)(2,1)}, u32[]{:S(2)}, u32[]{:S(2)}) collective-permute-start(bf16[128,1792]{1,0:T(8,128)(2,1)} %get-tuple-element.23), channel_id=1, source_target_pairs={{0,6},{2,0},{4,2},{6,4},{1,7},{3,1},{5,3},{7,5},{8,14},{10,8},{12,... | collective-permute-start | bytes 1376264 | tf_op jit(solution)/shard_map/ppermute | solution.py:91
  239.9 2.8 %collective-permute-done.16 = bf16[128,896]{1,0:T(8,128)(2,1)} collective-permute-done((bf16[128,896]{1,0:T(8,128)(2,1)S(1)}, bf16[128,896]{1,0:T(8,128)(2,1)}, u32[]{:S(2)}, u32[]{:S(2)}) %collective-permute-start.16) | collective-permute-done | bytes 229408 | tf_op jit(solution)/shard_map/ppermute | solution.py:91
  242.9 2.7 collective-permute-start.19
  246.4 3.5 %copy.80 = bf16[1,1024,224]{2,0,1:T(2,128)(2,1)} copy(bf16[1,1024,224]{1,2,0:T(8,128)(2,1)} %get-tuple-element.16) | data formatting | bytes 917504 | tf_op jit(solution)/shard_map/stack;squeeze | solution.py:74
  249.9 4.5 %pad_maximum_fusion = bf16[2,1024,224]{2,0,1:T(2,128)(2,1)} fusion(bf16[1,1024,224]{2,0,1:T(2,128)(2,1)S(1)} %copy.81, bf16[1,1024,224]{2,0,1:T(2,128)(2,1)} %copy.80), kind=kLoop, calls=%fused_computation.40 | loop fusion | flops 1835008 | bytes 1835008 | tf_op jit(solution)/shard_map/stack | solution.py:74
  257.4 2.5 fusion.29
  (119 shorter events, 54.0 us)
Async XLA Ops:
  7.2 12.4 %copy-start.3 = (bf16[1,2,64,224]{3,2,1,0:T(8,128)(2,1)S(1)}, bf16[1,2,64,224]{3,2,1,0:T(8,128)(2,1)}, u32[]{:S(2)}) copy-start(bf16[1,2,64,224]{3,2,1,0:T(8,128)(2,1)} %param.18) | copy-start | bytes 172036
  7.2 13.3 %copy-start.5 = (f32[3,224]{1,0:T(4,128)S(1)}, f32[3,224]{1,0:T(4,128)}, u32[]{:S(2)}) copy-start(f32[3,224]{1,0:T(4,128)} %param.17) | copy-start | bytes 8068
  7.2 86.9 %all-gather.3.cloned.1.call-start = ((), (), s32[]{:S(2)}) async-start(), calls=%async_computation.4 | async-start | bytes 4257792 | tf_op jit(solution)/shard_map/all_gather | solution.py:80
  9.7 191.0 %all-gather.5.cloned.1.call-start = ((), (), s32[]{:S(2)}) async-start(), calls=%async_computation.5 | async-start | bytes 9934848 | tf_op jit(solution)/shard_map/all_gather | solution.py:80
  15.6 15.7 %collective-permute-start = (bf16[128,1792]{1,0:T(8,128)(2,1)S(1)}, bf16[128,1792]{1,0:T(8,128)(2,1)S(1)}, u32[]{:S(2)}, u32[]{:S(2)}) collective-permute-start(bf16[128,1792]{1,0:T(8,128)(2,1)S(1)} %get-tuple-element.15), channel_id=1, source_target_pairs={{0,6},{2,0},{4,2},{6,4},{1,7},{3,1},{5,3},{7,5},{8,14},{10,8},{12,... | collective-permute-start | bytes 1376264 | tf_op jit(solution)/shard_map/ppermute | solution.py:91
  18.9 12.3 %collective-permute-start.1 = (bf16[128,1792]{1,0:T(8,128)(2,1)S(1)}, bf16[128,1792]{1,0:T(8,128)(2,1)S(1)}, u32[]{:S(2)}, u32[]{:S(2)}) collective-permute-start(bf16[128,1792]{1,0:T(8,128)(2,1)S(1)} %get-tuple-element.15), channel_id=1, source_target_pairs={{0,2},{2,4},{4,6},{6,0},{1,3},{3,5},{5,7},{7,1},{8,10},{10,12},{12... | collective-permute-start | bytes 1376264 | tf_op jit(solution)/shard_map/ppermute | solution.py:91
  31.2 6.6 %collective-permute-start.2 = (bf16[128,896]{1,0:T(8,128)(2,1)S(1)}, bf16[128,896]{1,0:T(8,128)(2,1)S(1)}, u32[]{:S(2)}, u32[]{:S(2)}) collective-permute-start(bf16[128,896]{1,0:T(8,128)(2,1)S(1)} %slice.159), channel_id=1, source_target_pairs={{0,2},{2,4},{4,6},{6,0},{1,3},{3,5},{5,7},{7,1},{8,10},{10,12},{12... | collective-permute-start | bytes 688136 | tf_op jit(solution)/shard_map/ppermute | solution.py:91
  31.3 6.5 %collective-permute-start.3 = (bf16[128,896]{1,0:T(8,128)(2,1)S(1)}, bf16[128,896]{1,0:T(8,128)(2,1)S(1)}, u32[]{:S(2)}, u32[]{:S(2)}) collective-permute-start(bf16[128,896]{1,0:T(8,128)(2,1)S(1)} %slice.160), channel_id=1, source_target_pairs={{0,6},{2,0},{4,2},{6,4},{1,7},{3,1},{5,3},{7,5},{8,14},{10,8},{12,... | collective-permute-start | bytes 688136 | tf_op jit(solution)/shard_map/ppermute | solution.py:91
  118.9 7.8 %copy-start.2 = (bf16[1024,1,224]{0,2,1:T(8,128)(2,1)S(1)}, bf16[1024,1,224]{0,2,1:T(8,128)(2,1)}, u32[]{:S(2)}) copy-start(bf16[1024,1,224]{0,2,1:T(8,128)(2,1)} %get-tuple-element.21) | copy-start | bytes 1376260
  143.4 23.8 %copy-start = (bf16[128,1792]{1,0:T(8,128)(2,1)S(1)}, bf16[128,1792]{1,0:T(8,128)(2,1)}, u32[]{:S(2)}) copy-start(bf16[128,1792]{1,0:T(8,128)(2,1)} %param.10) | copy-start | bytes 1376260
  144.1 23.6 %copy-start.4 = (f32[1792]{0:T(1024)S(1)}, f32[1792]{0:T(1024)}, u32[]{:S(2)}) copy-start(f32[1792]{0:T(1024)} %param.12) | copy-start | bytes 21508
  144.3 8.2 %collective-permute-start.6 = (bf16[128,896]{1,0:T(8,128)(2,1)S(1)}, bf16[128,896]{1,0:T(8,128)(2,1)S(1)}, u32[]{:S(2)}, u32[]{:S(2)}) collective-permute-start(bf16[128,896]{1,0:T(8,128)(2,1)S(1)} %get-tuple-element.30), channel_id=1, source_target_pairs={{0,2},{2,4},{4,6},{6,0},{1,3},{3,5},{5,7},{7,1},{8,10},{10,12},{12... | collective-permute-start | bytes 688136 | tf_op jit(solution)/shard_map/ppermute | solution.py:91
  145.5 7.1 %collective-permute-start.8 = (bf16[128,896]{1,0:T(8,128)(2,1)S(1)}, bf16[128,896]{1,0:T(8,128)(2,1)S(1)}, u32[]{:S(2)}, u32[]{:S(2)}) collective-permute-start(bf16[128,896]{1,0:T(8,128)(2,1)S(1)} %get-tuple-element.31), channel_id=1, source_target_pairs={{0,6},{2,0},{4,2},{6,4},{1,7},{3,1},{5,3},{7,5},{8,14},{10,8},{12,... | collective-permute-start | bytes 688136 | tf_op jit(solution)/shard_map/ppermute | solution.py:91
  147.0 20.2 %collective-permute-start.4 = (bf16[128,1792]{1,0:T(8,128)(2,1)S(1)}, bf16[128,1792]{1,0:T(8,128)(2,1)S(1)}, u32[]{:S(2)}, u32[]{:S(2)}) collective-permute-start(bf16[128,1792]{1,0:T(8,128)(2,1)S(1)} %get-tuple-element.25), channel_id=1, source_target_pairs={{0,2},{2,4},{4,6},{6,0},{1,3},{3,5},{5,7},{7,1},{8,10},{10,12},{12... | collective-permute-start | bytes 1376264 | tf_op jit(solution)/shard_map/ppermute | solution.py:91
  147.0 20.2 %collective-permute-start.5 = (bf16[128,1792]{1,0:T(8,128)(2,1)S(1)}, bf16[128,1792]{1,0:T(8,128)(2,1)S(1)}, u32[]{:S(2)}, u32[]{:S(2)}) collective-permute-start(bf16[128,1792]{1,0:T(8,128)(2,1)S(1)} %get-tuple-element.26), channel_id=1, source_target_pairs={{0,6},{2,0},{4,2},{6,4},{1,7},{3,1},{5,3},{7,5},{8,14},{10,8},{12,... | collective-permute-start | bytes 1376264 | tf_op jit(solution)/shard_map/ppermute | solution.py:91
  152.5 14.7 %collective-permute-start.7 = (bf16[128,896]{1,0:T(8,128)(2,1)S(1)}, bf16[128,896]{1,0:T(8,128)(2,1)S(1)}, u32[]{:S(2)}, u32[]{:S(2)}) collective-permute-start(bf16[128,896]{1,0:T(8,128)(2,1)S(1)} %collective-permute-done.6), channel_id=1, source_target_pairs={{0,2},{2,4},{4,6},{6,0},{1,3},{3,5},{5,7},{7,1},{8,10},{10,12},{12... | collective-permute-start | bytes 688136 | tf_op jit(solution)/shard_map/ppermute | solution.py:91
  152.7 14.6 %collective-permute-start.9 = (bf16[128,896]{1,0:T(8,128)(2,1)S(1)}, bf16[128,896]{1,0:T(8,128)(2,1)S(1)}, u32[]{:S(2)}, u32[]{:S(2)}) collective-permute-start(bf16[128,896]{1,0:T(8,128)(2,1)S(1)} %collective-permute-done.8), channel_id=1, source_target_pairs={{0,6},{2,0},{4,2},{6,4},{1,7},{3,1},{5,3},{7,5},{8,14},{10,8},{12,... | collective-permute-start | bytes 688136 | tf_op jit(solution)/shard_map/ppermute | solution.py:91
  167.7 19.3 %copy-start.1 = (bf16[128,1792]{1,0:T(8,128)(2,1)}, bf16[128,1792]{1,0:T(8,128)(2,1)S(1)}, u32[]{:S(2)}) copy-start(bf16[128,1792]{1,0:T(8,128)(2,1)S(1)} %get-tuple-element.13) | copy-start | bytes 1376260
  167.9 12.3 %collective-permute-start.11 = (bf16[128,1792]{1,0:T(8,128)(2,1)S(1)}, bf16[128,1792]{1,0:T(8,128)(2,1)S(1)}, u32[]{:S(2)}, u32[]{:S(2)}) collective-permute-start(bf16[128,1792]{1,0:T(8,128)(2,1)S(1)} %get-tuple-element.11), channel_id=1, source_target_pairs={{0,2},{2,4},{4,6},{6,0},{1,3},{3,5},{5,7},{7,1},{8,10},{10,12},{12... | collective-permute-start | bytes 1376264 | tf_op jit(solution)/shard_map/ppermute | solution.py:91
  168.8 11.5 %collective-permute-start.10 = (bf16[128,1792]{1,0:T(8,128)(2,1)S(1)}, bf16[128,1792]{1,0:T(8,128)(2,1)S(1)}, u32[]{:S(2)}, u32[]{:S(2)}) collective-permute-start(bf16[128,1792]{1,0:T(8,128)(2,1)S(1)} %get-tuple-element.11), channel_id=1, source_target_pairs={{0,6},{2,0},{4,2},{6,4},{1,7},{3,1},{5,3},{7,5},{8,14},{10,8},{12,... | collective-permute-start | bytes 1376264 | tf_op jit(solution)/shard_map/ppermute | solution.py:91
  180.3 6.6 %collective-permute-start.12 = (bf16[128,896]{1,0:T(8,128)(2,1)S(1)}, bf16[128,896]{1,0:T(8,128)(2,1)S(1)}, u32[]{:S(2)}, u32[]{:S(2)}) collective-permute-start(bf16[128,896]{1,0:T(8,128)(2,1)S(1)} %slice.179), channel_id=1, source_target_pairs={{0,2},{2,4},{4,6},{6,0},{1,3},{3,5},{5,7},{7,1},{8,10},{10,12},{12... | collective-permute-start | bytes 688136 | tf_op jit(solution)/shard_map/ppermute | solution.py:91
  180.4 6.4 %collective-permute-start.13 = (bf16[128,896]{1,0:T(8,128)(2,1)S(1)}, bf16[128,896]{1,0:T(8,128)(2,1)S(1)}, u32[]{:S(2)}, u32[]{:S(2)}) collective-permute-start(bf16[128,896]{1,0:T(8,128)(2,1)S(1)} %slice.180), channel_id=1, source_target_pairs={{0,6},{2,0},{4,2},{6,4},{1,7},{3,1},{5,3},{7,5},{8,14},{10,8},{12,... | collective-permute-start | bytes 688136 | tf_op jit(solution)/shard_map/ppermute | solution.py:91
  234.5 8.2 %collective-permute-start.16 = (bf16[128,896]{1,0:T(8,128)(2,1)S(1)}, bf16[128,896]{1,0:T(8,128)(2,1)}, u32[]{:S(2)}, u32[]{:S(2)}) collective-permute-start(bf16[128,896]{1,0:T(8,128)(2,1)S(1)} %get-tuple-element.28), channel_id=1, source_target_pairs={{0,2},{2,4},{4,6},{6,0},{1,3},{3,5},{5,7},{7,1},{8,10},{10,12},{12... | collective-permute-start | bytes 688136 | tf_op jit(solution)/shard_map/ppermute | solution.py:91
  235.7 7.2 %collective-permute-start.18 = (bf16[128,896]{1,0:T(8,128)(2,1)S(1)}, bf16[128,896]{1,0:T(8,128)(2,1)}, u32[]{:S(2)}, u32[]{:S(2)}) collective-permute-start(bf16[128,896]{1,0:T(8,128)(2,1)S(1)} %get-tuple-element.29), channel_id=1, source_target_pairs={{0,6},{2,0},{4,2},{6,4},{1,7},{3,1},{5,3},{7,5},{8,14},{10,8},{12,... | collective-permute-start | bytes 688136 | tf_op jit(solution)/shard_map/ppermute | solution.py:91
  237.2 19.7 %collective-permute-start.14 = (bf16[128,1792]{1,0:T(8,128)(2,1)}, bf16[128,1792]{1,0:T(8,128)(2,1)}, u32[]{:S(2)}, u32[]{:S(2)}) collective-permute-start(bf16[128,1792]{1,0:T(8,128)(2,1)} %get-tuple-element.24), channel_id=1, source_target_pairs={{0,2},{2,4},{4,6},{6,0},{1,3},{3,5},{5,7},{7,1},{8,10},{10,12},{12... | collective-permute-start | bytes 1376264 | tf_op jit(solution)/shard_map/ppermute | solution.py:91
  237.2 19.7 %collective-permute-start.15 = (bf16[128,1792]{1,0:T(8,128)(2,1)}, bf16[128,1792]{1,0:T(8,128)(2,1)}, u32[]{:S(2)}, u32[]{:S(2)}) collective-permute-start(bf16[128,1792]{1,0:T(8,128)(2,1)} %get-tuple-element.23), channel_id=1, source_target_pairs={{0,6},{2,0},{4,2},{6,4},{1,7},{3,1},{5,3},{7,5},{8,14},{10,8},{12,... | collective-permute-start | bytes 1376264 | tf_op jit(solution)/shard_map/ppermute | solution.py:91
  242.7 14.7 %collective-permute-start.17 = (bf16[128,896]{1,0:T(8,128)(2,1)}, bf16[128,896]{1,0:T(8,128)(2,1)}, u32[]{:S(2)}, u32[]{:S(2)}) collective-permute-start(bf16[128,896]{1,0:T(8,128)(2,1)} %collective-permute-done.16), channel_id=1, source_target_pairs={{0,2},{2,4},{4,6},{6,0},{1,3},{3,5},{5,7},{7,1},{8,10},{10,12},{12... | collective-permute-start | bytes 688136 | tf_op jit(solution)/shard_map/ppermute | solution.py:91
  242.9 14.5 %collective-permute-start.19 = (bf16[128,896]{1,0:T(8,128)(2,1)}, bf16[128,896]{1,0:T(8,128)(2,1)}, u32[]{:S(2)}, u32[]{:S(2)}) collective-permute-start(bf16[128,896]{1,0:T(8,128)(2,1)} %collective-permute-done.18), channel_id=1, source_target_pairs={{0,6},{2,0},{4,2},{6,4},{1,7},{3,1},{5,3},{7,5},{8,14},{10,8},{12,... | collective-permute-start | bytes 688136 | tf_op jit(solution)/shard_map/ppermute | solution.py:91
Sparse Core Ops, SparseCore 0:
  11.2 82.8 all-gather.2
  96.7 104.0 all-gather.4

commit v7 on v3

--- a/solution.py
+++ b/solution.py
@@ -106,6 +106,19 @@
     return chips.astype(jnp.float32).sum(axis=0)
 
 
+def core_swap(x):
+    return lax.ppermute(x, "tpc", [(0, 1), (1, 0)])
+
+
+def mlp_rows(rows, ffn_all, down_t, ffn_width):
+    gate_up = jnp.dot(rows, ffn_all, preferred_element_type=jnp.float32)
+    activated = (jax.nn.silu(gate_up[:, :ffn_width]) * gate_up[:, ffn_width:]).astype(jnp.bfloat16)
+    out = lax.dot_general(
+        activated, down_t, (((1,), (1,)), ((), ())), preferred_element_type=jnp.float32
+    )
+    return out.astype(jnp.bfloat16)
+
+
 def local(
     tokens,
     norm_gain,
@@ -133,13 +146,18 @@
     )
     attn_part = tp_sum_scatter(attn_full.astype(jnp.bfloat16))
     residual = (tokens.astype(jnp.float32) + attn_part).astype(jnp.bfloat16)
-    ffn_in = tp_gather(normed(residual, ffn_gain))
-    gate_up = jnp.dot(ffn_in, ffn_all, preferred_element_type=jnp.float32)
-    activated = (jax.nn.silu(gate_up[:, :ffn_width]) * gate_up[:, ffn_width:]).astype(jnp.bfloat16)
-    ffn_full = lax.dot_general(
-        activated, down_t, (((1,), (1,)), ((), ())), preferred_element_type=jnp.float32
+    nx = lax.axis_size("tpx")
+    mine = lax.all_to_all(
+        jnp.tile(normed(residual, ffn_gain)[None], (nx, 1, 1)), "tpx", 0, 0, tiled=True
     )
-    ffn_part = tp_sum_scatter(ffn_full.astype(jnp.bfloat16))
+    flat = mine.reshape((-1,) + mine.shape[2:])
+    theirs = core_swap(flat)
+    part_mine = mlp_rows(flat, ffn_all, down_t, ffn_width)
+    part_theirs = mlp_rows(theirs, ffn_all, down_t, ffn_width)
+    back = core_swap(part_theirs)
+    pair = (part_mine.astype(jnp.float32) + back.astype(jnp.float32)).astype(jnp.bfloat16)
+    chips = lax.all_to_all(pair.reshape(mine.shape), "tpx", 0, 0, tiled=True)
+    ffn_part = chips.astype(jnp.float32).sum(axis=0)
     layer_out = (residual.astype(jnp.float32) + ffn_part).astype(jnp.bfloat16)
     return (layer_out, renewed[None])
 

time: 272 us -> 258 us (0.949)
  blocking collectives: 87.3 us -> 70.5 us
  other arithmetic: 19.4 us -> 13.3 us
  waiting for transfers between devices: 73.1 us -> 76.7 us
  starting transfers between devices: 8.51 us -> 12.1 us
    all_to_all x2 -> x1, blocking collectives: 18.3 us -> 9.19 us  [tp_gather(): got = lax.all_to_all(both, 'tpc', 1, 1, tiled=True)]
    all_to_all x2 -> x1, blocking collectives: 18.2 us -> 10.6 us  [tp_sum_scatter(): pair = lax.all_to_all(parts, 'tpc', 1, 1, tiled=True)]
    reduce_sum x2 -> x1, other arithmetic: 7.35 us -> 2.92 us  [tp_sum_scatter(): pair = pair.astype(jnp.float32).sum(axis=1).astype(jnp.bfloat16)]
    ppermute x0 -> x2, waiting for transfers between devices: none -> 3.55 us  [core_swap(): return lax.ppermute(x, 'tpc', [(0, 1), (1, 0)])]
    ppermute x0 -> x2, starting transfers between devices: none -> 3.16 us  [core_swap(): return lax.ppermute(x, 'tpc', [(0, 1), (1, 0)])]
    dot_general x2 -> x4, matrix products: 17.3 us -> 16.4 us  [the longest x2 10.5 us: mlp_rows(): gate_up = jnp.dot(rows, ffn_all, preferred_element_type=jnp.float32)]
  transfers between devices with their start and end apart: 4 -> 6, of which waited for: 3 -> 4; matrix products, arithmetic and copies ran while one was open for 22% -> 25% of each run, Pallas kernels for 0% -> 0%
where the time goes in v7:
time: 258 us; the launch traced here: 257 us
  waiting for transfers between devices  76.7 us (30%)
  blocking collectives  70.5 us (27%)
  matrix products  39.2 us (15%)
  local copies, waits for them, and re-layouts  30 us (12%)
  between operations  15 us (6%)
  other arithmetic  13.3 us (5%)
  starting transfers between devices  12.1 us (5%)
    all_gather x2, waiting for transfers between devices, gather_packed(): lax.all_gather(jnp.concatenate(pieces, axis=1), 'req', axis=0, tiled=True)  41.9 us
    all_to_all x1, blocking collectives, tp_sum_scatter(): chips = lax.all_to_all(pair, 'tpx', 0, 0, tiled=True)  26.5 us
    all_to_all x1, blocking collectives, local(): lax.all_to_all(jnp.tile(normed(residual, ffn_gain)[None], (nx, 1, 1)), 't...  24.2 us
    all_to_all x1, waiting for transfers between devices, tp_gather(): lax.all_to_all(jnp.tile(x[None], (nx, 1, 1)), 'tpx', 0, 0, tiled=True)  19.6 us
    all_to_all x1, waiting for transfers between devices, local(): chips = lax.all_to_all(pair.reshape(mine.shape), 'tpx', 0, 0, tiled=True)  11.7 us
    all_to_all x1, blocking collectives, tp_sum_scatter(): pair = lax.all_to_all(parts, 'tpc', 1, 1, tiled=True)  10.6 us
    dot_general x2, matrix products, mlp_rows(): gate_up = jnp.dot(rows, ffn_all, preferred_element_type=jnp.float32)  10.5 us
    all_to_all x1, blocking collectives, tp_gather(): got = lax.all_to_all(both, 'tpc', 1, 1, tiled=True)  9.19 us
  transfers between devices with their start and end apart: 6, of which 4 were waited for; matrix products, arithmetic and copies ran while one was open for 25% of the time, Pallas kernels for 0%

profile of v7, /device:TPU:1, one launch (start us, length us, event | category | flops | bytes accessed | tf_op | source)
XLA Modules:
  0.0 256.9 jit_solution(17358209932625492572)
XLA Ops:
  8.3 1.4 pad_maximum_fusion.4
  10.8 1.6 pad_maximum_fusion.3
  14.2 5.0 %all-to-all-start = ((bf16[4,128,1792]{2,1,0:T(8,128)(2,1)}), bf16[4,128,1792]{2,1,0:T(8,128)(2,1)S(1)}, u32[]{:S(2)}, u32[]{:S(2)}) async-start(bf16[4,128,1792]{2,1,0:T(8,128)(2,1)} %tile.4), calls=%async_computation | async-start | bytes 3670016 | tf_op jit(solution)/shard_map/all_to_all | solution.py:92
  21.1 19.6 %all-to-all-done = bf16[4,128,1792]{2,1,0:T(8,128)(2,1)S(1)} async-done(((bf16[4,128,1792]{2,1,0:T(8,128)(2,1)}), bf16[4,128,1792]{2,1,0:T(8,128)(2,1)S(1)}, u32[]{:S(2)}, u32[]{:S(2)}) %all-to-all-start) | async-done | bytes 1835040 | tf_op jit(solution)/shard_map/all_to_all | solution.py:92
  41.0 9.2 %all_to_all.30 = bf16[4,2,128,1792]{3,2,0,1:T(8,128)(2,1)S(1)} all-to-all(bf16[4,2,128,1792]{3,2,0,1:T(8,128)(2,1)S(1)} %broadcast_in_dim.24), channel_id=1, replica_groups=mesh['req'=32,'tpx'=4,'tpc'=2] {'tpc'}, dimensions={1} | all-to-all | bytes 7340032 | tf_op jit(solution)/shard_map/all_to_all | solution.py:94
  50.2 2.0 copy.81
  52.2 41.9 %all-gather.3.cloned.1.call-done = bf16[1792,1120]{1,0:T(8,128)(2,1)} async-done(((bf16[56,1120]{1,0:T(8,128)(2,1)}), bf16[1792,1120]{1,0:T(8,128)(2,1)}) %all-gather.3.cloned.1.call-update) | async-done | bytes 4014096 | tf_op jit(solution)/shard_map/all_gather | solution.py:80
  94.1 6.6 %fusion.13 = bf16[1024,896]{0,1:T(8,128)(2,1)S(1)} fusion(bf16[1024,1792]{1,0:T(8,128)(2,1)} %bitcast.60, bf16[1792,1120]{1,0:T(8,128)(2,1)} %all-gather.3.cloned.1.call-done), kind=kOutput, calls=%fused_computation.21 | convolution fusion | flops 3289251840 | bytes 8716288 | tf_op jit(solution)/shard_map/dot_general | solution.py:141
  102.9 1.7 reshape.284
  105.8 1.5 reshape.282
  109.0 2.2 copy.83
  112.4 2.7 %fusion.72 = f32[16,2,64]{2,1,0:T(2,128)S(1)} fusion(bf16[16,64,2,112]{1,3,2,0:T(8,128)(2,1)} %copy.90, bf16[16,64,2,112]{1,3,2,0:T(8,128)(2,1)S(1)} %copy.89, bf16[16,64,2,112]{1,0,3,2:T(8,128)(2,1)} %reshape.282, pred[16,64,128]{2,1,0:T(8,128)(4,1)S(1)} %broadcast_and_fusion), kind=kOutput, calls=%fused_computation.111 | convolution fusion | flops 61603968 | bytes 1515520 | tf_op jit(solution)/shard_map/sub | solution.py:40
  115.1 3.3 %fusion.18 = f32[16,2,64,128]{3,2,1,0:T(8,128)} fusion(bf16[16,64,2,112]{1,3,2,0:T(8,128)(2,1)} %copy.90, bf16[16,64,2,112]{1,3,2,0:T(8,128)(2,1)S(1)} %copy.89, bf16[16,64,2,112]{1,0,3,2:T(8,128)(2,1)} %reshape.282, pred[16,64,128]{2,1,0:T(8,128)(4,1)S(1)} %broadcast_and_fusion), kind=kOutput, calls=%fused_computation.31 | convolution fusion | flops 61079552 | bytes 2555904 | tf_op jit(solution)/shard_map/bqhd,bkhd->bhqk/dot_general | solution.py:32
  118.4 7.3 %convolution_bitcast_fusion = f32[16,64,2,112]{3,1,2,0:T(8,128)} fusion(bf16[16,64,2,112]{1,3,2,0:T(8,128)(2,1)} %copy.84, bf16[16,64,2,112]{1,3,2,0:T(8,128)(2,1)} %copy.83, f32[16,2,64]{2,1,0:T(2,128)S(1)} %fusion.72, f32[16,2,64,128]{3,2,1,0:T(8,128)} %fusion.18), kind=kOutput, calls=%fused_computation.32 | convolution fusion | flops 61343872 | bytes 2891776 | tf_op jit(solution)/shard_map/bhqk,bkhd->bqhd/dot_general | solution.py:42
  125.7 2.1 copy.92
  127.8 1.6 reshape_reshape.3
  129.8 2.9 %convolution_convert_fusion = bf16[1024,1792]{1,0:T(8,128)(2,1)S(1)} fusion(bf16[1792,1120]{1,0:T(8,128)(2,1)} %all-gather.3.cloned.1.call-done, f32[1024,224]{1,0:T(8,128)} %reshape_reshape.3, f32[1088,224]{1,0:T(8,128)S(1)} %convert_select_fusion, bf16[1024,1,224]{2,0,1:T(8,128)(2,1)S(1)} %copy.110, f32[224]{0:T(256)S(1)} %bitcast.76, ...), kind=kOutput, calls=%fused_computation.7 | convolution fusion | flops 825982976 | bytes 9309184 | tf_op jit(solution)/shard_map/dot_general | solution.py:144
  133.0 10.6 %all_to_all.31 = bf16[4,2,128,1792]{3,2,0,1:T(8,128)(2,1)} all-to-all(bf16[4,2,128,1792]{3,2,0,1:T(8,128)(2,1)S(1)} %copy.94), channel_id=1, replica_groups=mesh['req'=32,'tpx'=4,'tpc'=2] {'tpc'}, dimensions={1} | all-to-all | bytes 7340032 | tf_op jit(solution)/shard_map/all_to_all | solution.py:103
  143.6 2.9 %reduce_sum.59 = bf16[4,128,1792]{2,1,0:T(8,128)(2,1)S(1)} reduce(bf16[4,2,128,1792]{3,2,0,1:T(8,128)(2,1)} %all_to_all.31, bf16[]{:T(256)} %constant.46.clone.1), dimensions={1}, to_apply=%region_3.4 | reduce | flops 917504 | bytes 5505026 | tf_op jit(solution)/shard_map/reduce_sum | solution.py:104
  146.5 26.5 %all_to_all.32 = bf16[4,128,1792]{2,1,0:T(8,128)(2,1)S(1)} all-to-all(bf16[4,128,1792]{2,1,0:T(8,128)(2,1)S(1)} %reduce_sum.59), channel_id=1, replica_groups=mesh['req'=32,'tpx'=4,'tpc'=2] {'tpx'}, dimensions={0} | all-to-all | bytes 3670016 | tf_op jit(solution)/shard_map/all_to_all | solution.py:105
  174.5 24.2 %all_to_all.33 = bf16[4,128,1792]{2,1,0:T(8,128)(2,1)S(1)} all-to-all(bf16[4,128,1792]{2,1,0:T(8,128)(2,1)S(1)} %tile.5), channel_id=1, replica_groups=mesh['req'=32,'tpx'=4,'tpc'=2] {'tpx'}, dimensions={0} | all-to-all | bytes 3670016 | tf_op jit(solution)/shard_map/all_to_all | solution.py:150
  198.8 2.7 %collective-permute-start = (bf16[512,1792]{1,0:T(8,128)(2,1)S(1)}, bf16[512,1792]{1,0:T(8,128)(2,1)}, u32[]{:S(2)}, u32[]{:S(2)}) collective-permute-start(bf16[512,1792]{1,0:T(8,128)(2,1)S(1)} %bitcast.62), channel_id=1, source_target_pairs={{0,1},{1,0},{2,3},{3,2},{4,5},{5,4},{6,7},{7,6},{8,9},{9,8},{10,11... | collective-permute-start | bytes 5505032 | tf_op jit(solution)/shard_map/ppermute | solution.py:110
  201.5 3.5 %collective-permute-done = bf16[512,1792]{1,0:T(8,128)(2,1)} collective-permute-done((bf16[512,1792]{1,0:T(8,128)(2,1)S(1)}, bf16[512,1792]{1,0:T(8,128)(2,1)}, u32[]{:S(2)}, u32[]{:S(2)}) %collective-permute-start) | collective-permute-done | bytes 1835040 | tf_op jit(solution)/shard_map/ppermute | solution.py:110
  205.0 7.0 %fusion.1 = f32[512,1792]{1,0:T(8,128)S(1)} fusion(bf16[512,1792]{1,0:T(8,128)(2,1)} %collective-permute-done, bf16[1792,2688]{1,0:T(8,128)(2,1)} %all-gather.5.cloned.1.call-done), kind=kOutput, calls=%fused_computation.3 | convolution fusion | flops 3288334336 | bytes 11927552 | tf_op jit(solution)/shard_map/dot_general | solution.py:114
  212.0 2.3 convolution_convert_fusion.1
  214.8 3.5 %fusion.3 = f32[512,1792]{1,0:T(8,128)S(1)} fusion(bf16[512,1792]{1,0:T(8,128)(2,1)S(1)} %bitcast.63, bf16[1792,2688]{1,0:T(8,128)(2,1)S(1)} %copy-done.8), kind=kOutput, calls=%fused_computation.5 | convolution fusion | flops 3288334336 | bytes 11927552 | tf_op jit(solution)/shard_map/dot_general | solution.py:114
  218.3 3.6 %add_convert_fusion = bf16[512,1792]{1,0:T(8,128)(2,1)} fusion(bf16[512,1792]{1,0:T(8,128)(2,1)S(1)} %collective-permute-done.1, bf16[1792,2688]{1,0:T(8,128)(2,1)S(1)} %copy-done.8, f32[512,1792]{1,0:T(8,128)S(1)} %fusion.3), kind=kOutput, calls=%fused_computation.9 | convolution fusion | flops 1651507200 | bytes 10551296 | tf_op jit(solution)/shard_map/dot_general | solution.py:116
  221.9 3.8 %all-to-all-start.5 = ((bf16[4,128,1792]{2,1,0:T(8,128)(2,1)}), bf16[4,128,1792]{2,1,0:T(8,128)(2,1)S(1)}, u32[]{:S(2)}, u32[]{:S(2)}) async-start(bf16[4,128,1792]{2,1,0:T(8,128)(2,1)} %bitcast.61), calls=%async_computation.5 | async-start | bytes 3670016 | tf_op jit(solution)/shard_map/all_to_all | solution.py:159
  226.6 3.5 %copy.96 = bf16[1,1024,224]{2,0,1:T(2,128)(2,1)} copy(bf16[1,1024,224]{1,2,0:T(8,128)(2,1)} %get-tuple-element.14) | data formatting | bytes 917504 | tf_op jit(solution)/shard_map/stack;squeeze | solution.py:74
  230.2 4.4 %pad_maximum_fusion = bf16[2,1024,224]{2,0,1:T(2,128)(2,1)} fusion(bf16[1,1024,224]{2,0,1:T(2,128)(2,1)S(1)} %copy.97, bf16[1,1024,224]{2,0,1:T(2,128)(2,1)} %copy.96), kind=kLoop, calls=%fused_computation.42 | loop fusion | flops 1835008 | bytes 1835008 | tf_op jit(solution)/shard_map/stack | solution.py:74
  234.6 2.0 gather_fusion.1
  237.2 11.7 %all-to-all-done.5 = bf16[4,128,1792]{2,1,0:T(8,128)(2,1)S(1)} async-done(((bf16[4,128,1792]{2,1,0:T(8,128)(2,1)}), bf16[4,128,1792]{2,1,0:T(8,128)(2,1)S(1)}, u32[]{:S(2)}, u32[]{:S(2)}) %all-to-all-start.5) | async-done | bytes 1835040 | tf_op jit(solution)/shard_map/all_to_all | solution.py:159
  (69 shorter events, 16.9 us)
Async XLA Ops:
  7.2 5.3 %copy-start.2 = (bf16[128,1792]{1,0:T(8,128)(2,1)S(1)}, bf16[128,1792]{1,0:T(8,128)(2,1)}, u32[]{:S(2)}) copy-start(bf16[128,1792]{1,0:T(8,128)(2,1)} %param.10) | copy-start | bytes 1376260
  7.2 5.5 %copy-start.5 = (f32[1792]{0:T(1024)S(1)}, f32[1792]{0:T(1024)}, u32[]{:S(2)}) copy-start(f32[1792]{0:T(1024)} %param.11) | copy-start | bytes 21508
  7.2 86.9 %all-gather.3.cloned.1.call-start = ((), (), s32[]{:S(2)}) async-start(), calls=%async_computation.6 | async-start | bytes 4257792 | tf_op jit(solution)/shard_map/all_gather | solution.py:80
  9.8 195.2 %all-gather.5.cloned.1.call-start = ((), (), s32[]{:S(2)}) async-start(), calls=%async_computation.7 | async-start | bytes 9934848 | tf_op jit(solution)/shard_map/all_gather | solution.py:80
  14.2 5.6 %copy-start.4 = (bf16[1,2,64,224]{3,2,1,0:T(8,128)(2,1)S(1)}, bf16[1,2,64,224]{3,2,1,0:T(8,128)(2,1)}, u32[]{:S(2)}) copy-start(bf16[1,2,64,224]{3,2,1,0:T(8,128)(2,1)} %param.18) | copy-start | bytes 172036
  14.2 6.8 %copy-start.7 = (f32[3,224]{1,0:T(4,128)S(1)}, f32[3,224]{1,0:T(4,128)}, u32[]{:S(2)}) copy-start(f32[3,224]{1,0:T(4,128)} %param.17) | copy-start | bytes 8068
  14.2 26.6 %all-to-all-start = ((bf16[4,128,1792]{2,1,0:T(8,128)(2,1)}), bf16[4,128,1792]{2,1,0:T(8,128)(2,1)S(1)}, u32[]{:S(2)}, u32[]{:S(2)}) async-start(bf16[4,128,1792]{2,1,0:T(8,128)(2,1)} %tile.4), calls=%async_computation | async-start | bytes 3670016 | tf_op jit(solution)/shard_map/all_to_all | solution.py:92
  125.7 3.7 %copy-start.3 = (bf16[1024,1,224]{0,2,1:T(8,128)(2,1)S(1)}, bf16[1024,1,224]{0,2,1:T(8,128)(2,1)}, u32[]{:S(2)}) copy-start(bf16[1024,1,224]{0,2,1:T(8,128)(2,1)} %get-tuple-element.19) | copy-start | bytes 1376260
  173.0 1.3 copy-start.6
  173.5 0.8 copy-start
  198.8 6.2 %collective-permute-start = (bf16[512,1792]{1,0:T(8,128)(2,1)S(1)}, bf16[512,1792]{1,0:T(8,128)(2,1)}, u32[]{:S(2)}, u32[]{:S(2)}) collective-permute-start(bf16[512,1792]{1,0:T(8,128)(2,1)S(1)} %bitcast.62), channel_id=1, source_target_pairs={{0,1},{1,0},{2,3},{3,2},{4,5},{5,4},{6,7},{7,6},{8,9},{9,8},{10,11... | collective-permute-start | bytes 5505032 | tf_op jit(solution)/shard_map/ppermute | solution.py:110
  205.0 7.0 %copy-start.8 = (bf16[1792,2688]{1,0:T(8,128)(2,1)S(1)}, bf16[1792,2688]{1,0:T(8,128)(2,1)}, u32[]{:S(2)}) copy-start(bf16[1792,2688]{1,0:T(8,128)(2,1)} %all-gather.5.cloned.1.call-done) | copy-start | bytes 28901380
  214.4 4.0 %collective-permute-start.1 = (bf16[512,1792]{1,0:T(8,128)(2,1)S(1)}, bf16[512,1792]{1,0:T(8,128)(2,1)S(1)}, u32[]{:S(2)}, u32[]{:S(2)}) collective-permute-start(bf16[512,1792]{1,0:T(8,128)(2,1)S(1)} %convolution_convert_fusion.1), channel_id=1, source_target_pairs={{0,1},{1,0},{2,3},{3,2},{4,5},{5,4},{6,7},{7,6},{8,9},{9,8},{10,11... | collective-permute-start | bytes 5505032 | tf_op jit(solution)/shard_map/ppermute | solution.py:110
  221.9 27.0 %all-to-all-start.5 = ((bf16[4,128,1792]{2,1,0:T(8,128)(2,1)}), bf16[4,128,1792]{2,1,0:T(8,128)(2,1)S(1)}, u32[]{:S(2)}, u32[]{:S(2)}) async-start(bf16[4,128,1792]{2,1,0:T(8,128)(2,1)} %bitcast.61), calls=%async_computation.5 | async-start | bytes 3670016 | tf_op jit(solution)/shard_map/all_to_all | solution.py:159
  234.6 14.6 %copy-start.1 = (bf16[128,1792]{1,0:T(8,128)(2,1)S(1)}, bf16[128,1792]{1,0:T(8,128)(2,1)}, u32[]{:S(2)}) copy-start(bf16[128,1792]{1,0:T(8,128)(2,1)} %copy-done) | copy-start | bytes 1376260
Sparse Core Ops, SparseCore 0:
  11.2 82.8 all-gather.2
  96.7 104.0 all-gather.4

commit v8 on v7

--- a/solution.py
+++ b/solution.py
@@ -7,6 +7,7 @@
 
 HD = 112
 WIN = 64
+REQ = ("ry", "rz")
 
 
 def normed(row_vals, gain):
@@ -77,7 +78,8 @@
 
 def gather_packed(pieces):
     widths = [p.shape[1] for p in pieces]
-    got = lax.all_gather(jnp.concatenate(pieces, axis=1), "req", axis=0, tiled=True)
+    by_z = lax.all_gather(jnp.concatenate(pieces, axis=1), REQ[1], axis=0, tiled=True)
+    got = lax.all_gather(by_z, REQ[0], axis=0, tiled=True)
     parts = []
     start = 0
     for w in widths:
@@ -164,19 +166,22 @@
 
 def solution(mesh):
     n_req, n_tp = mesh.devices.shape
-    split = jax.sharding.Mesh(mesh.devices.reshape(n_req, n_tp // 2, 2), ("req", "tpx", "tpc"))
+    ny = 4 if n_req % 4 == 0 else 1
+    split = jax.sharding.Mesh(
+        mesh.devices.reshape(ny, n_req // ny, n_tp // 2, 2), REQ + ("tpx", "tpc")
+    )
     tp = ("tpx", "tpc")
     in_specs = (
-        P(("req",) + tp, None),
+        P(REQ + tp, None),
         P(),
         P(),
-        P("req", None, tp),
-        P(tp, "req"),
-        P("req", None, tp),
-        P(tp, "req"),
+        P(REQ, None, tp),
+        P(tp, REQ),
+        P(REQ, None, tp),
+        P(tp, REQ),
         P(None, tp),
-        P("req", None, None, tp),
-        P("req"),
+        P(REQ, None, None, tp),
+        P(REQ),
     )
-    out_specs = (P(("req",) + tp, None), P("req", None, None, tp))
+    out_specs = (P(REQ + tp, None), P(REQ, None, None, tp))
     return jax.shard_map(local, mesh=split, in_specs=in_specs, out_specs=out_specs, check_vma=False)

time: 258 us -> 272 us (1.054)
  blocking collectives: 70.5 us -> 98.7 us
  waiting for transfers between devices: 76.7 us -> 63.9 us
    all_gather x0 -> x1, blocking collectives: none -> 30.7 us  [gather_packed(): lax.all_gather(jnp.concatenate(pieces, axis=1), REQ[1], axis=0, tiled=True)]
    all_gather x2 -> x3, waiting for transfers between devices: 41.9 us -> 29.2 us  [the longest x1 16.1 us: gather_packed(): lax.all_gather(jnp.concatenate(pieces, axis=1), REQ[1], axis=0, tiled=True)]
  transfers between devices with their start and end apart: 6 -> 7, of which waited for: 4 -> 5; matrix products, arithmetic and copies ran while one was open for 25% -> 24% of each run, Pallas kernels for 0% -> 0%
where the time goes in v8:
time: 272 us; the launch traced here: 271 us
  blocking collectives  98.7 us (36%)
  waiting for transfers between devices  63.9 us (23%)
  matrix products  39.4 us (14%)
  local copies, waits for them, and re-layouts  30.1 us (11%)
  between operations  14.7 us (5%)
  other arithmetic  12.7 us (5%)
  starting transfers between devices  11.5 us (4%)
    all_gather x1, blocking collectives, gather_packed(): lax.all_gather(jnp.concatenate(pieces, axis=1), REQ[1], axis=0, tiled=True)  30.7 us
    all_to_all x1, blocking collectives, tp_sum_scatter(): chips = lax.all_to_all(pair, 'tpx', 0, 0, tiled=True)  26.4 us
    all_to_all x1, blocking collectives, local(): lax.all_to_all(jnp.tile(normed(residual, ffn_gain)[None], (nx, 1, 1)), 't...  24.2 us
    all_to_all x1, waiting for transfers between devices, tp_gather(): lax.all_to_all(jnp.tile(x[None], (nx, 1, 1)), 'tpx', 0, 0, tiled=True)  19.5 us
    all_gather x1, waiting for transfers between devices, gather_packed(): lax.all_gather(jnp.concatenate(pieces, axis=1), REQ[1], axis=0, tiled=True)  16.1 us
    all_gather x2, waiting for transfers between devices, gather_packed(): got = lax.all_gather(by_z, REQ[0], axis=0, tiled=True)  13.1 us
    all_to_all x1, waiting for transfers between devices, local(): chips = lax.all_to_all(pair.reshape(mine.shape), 'tpx', 0, 0, tiled=True)  11.7 us
    dot_general x2, matrix products, mlp_rows(): gate_up = jnp.dot(rows, ffn_all, preferred_element_type=jnp.float32)  10.5 us
  transfers between devices with their start and end apart: 7, of which 5 were waited for; matrix products, arithmetic and copies ran while one was open for 24% of the time, Pallas kernels for 0%

profile of v8, /device:TPU:1, one launch (start us, length us, event | category | flops | bytes accessed | tf_op | source)
XLA Modules:
  0.0 271.1 jit_solution(9360561414915895319)
XLA Ops:
  8.2 1.6 pad_maximum_fusion.3
  11.7 30.7 %all_gather.12 = bf16[448,1120]{1,0:T(8,128)(2,1)} all-gather(bf16[56,1120]{1,0:T(8,128)(2,1)S(1)} %pad_maximum_fusion.4), channel_id=1, replica_groups=mesh['ry'=4,'rz'=8,'tpx'=4,'tpc'=2] {'rz'}, dimensions={0}, use_global_device_ids=true | all-gather | bytes 1128960 | tf_op jit(solution)/shard_map/all_gather | solution.py:81
  42.4 16.1 %all-gather.6.cloned.1.call-done = bf16[448,2688]{1,0:T(8,128)(2,1)} async-done(((bf16[56,2688]{1,0:T(8,128)(2,1)}), bf16[448,2688]{1,0:T(8,128)(2,1)}) %all-gather.6.cloned.1.call-update) | async-done | bytes 2408464 | tf_op jit(solution)/shard_map/all_gather | solution.py:81
  60.3 4.3 %all-to-all-start = ((bf16[4,128,1792]{2,1,0:T(8,128)(2,1)}), bf16[4,128,1792]{2,1,0:T(8,128)(2,1)S(1)}, u32[]{:S(2)}, u32[]{:S(2)}) async-start(bf16[4,128,1792]{2,1,0:T(8,128)(2,1)} %tile.4), calls=%async_computation | async-start | bytes 3670016 | tf_op jit(solution)/shard_map/all_to_all | solution.py:94
  66.6 19.5 %all-to-all-done = bf16[4,128,1792]{2,1,0:T(8,128)(2,1)S(1)} async-done(((bf16[4,128,1792]{2,1,0:T(8,128)(2,1)}), bf16[4,128,1792]{2,1,0:T(8,128)(2,1)S(1)}, u32[]{:S(2)}, u32[]{:S(2)}) %all-to-all-start) | async-done | bytes 1835040 | tf_op jit(solution)/shard_map/all_to_all | solution.py:94
  86.4 9.3 %all_to_all.30 = bf16[4,2,128,1792]{3,2,0,1:T(8,128)(2,1)S(1)} all-to-all(bf16[4,2,128,1792]{3,2,0,1:T(8,128)(2,1)S(1)} %broadcast_in_dim.24), channel_id=1, replica_groups=mesh['ry'=4,'rz'=8,'tpx'=4,'tpc'=2] {'tpc'}, dimensions={1} | all-to-all | bytes 7340032 | tf_op jit(solution)/shard_map/all_to_all | solution.py:96
  95.7 2.0 copy.81
  97.7 13.1 %all-gather.4.cloned.1.call-done = bf16[1792,1120]{1,0:T(8,128)(2,1)} async-done(((bf16[448,1120]{1,0:T(8,128)(2,1)}), bf16[1792,1120]{1,0:T(8,128)(2,1)}) %all-gather.4.cloned.1.call-update) | async-done | bytes 4014096 | tf_op jit(solution)/shard_map/all_gather | solution.py:82
  110.8 6.6 %fusion.13 = bf16[1024,896]{0,1:T(8,128)(2,1)S(1)} fusion(bf16[1024,1792]{1,0:T(8,128)(2,1)} %bitcast.60, bf16[1792,1120]{1,0:T(8,128)(2,1)} %all-gather.4.cloned.1.call-done), kind=kOutput, calls=%fused_computation.21 | convolution fusion | flops 3289251840 | bytes 8716288 | tf_op jit(solution)/shard_map/dot_general | solution.py:143
  119.6 1.7 reshape.284
  125.7 2.2 copy.83
  129.1 2.9 %fusion.72 = f32[16,2,64]{2,1,0:T(2,128)S(1)} fusion(bf16[16,64,2,112]{1,3,2,0:T(8,128)(2,1)} %copy.90, bf16[16,64,2,112]{1,3,2,0:T(8,128)(2,1)S(1)} %copy.89, bf16[16,64,2,112]{1,0,3,2:T(8,128)(2,1)} %reshape.282, pred[16,64,128]{2,1,0:T(8,128)(4,1)S(1)} %broadcast_and_fusion), kind=kOutput, calls=%fused_computation.111 | convolution fusion | flops 61603968 | bytes 1515520 | tf_op jit(solution)/shard_map/sub | solution.py:41
  132.0 3.4 %fusion.18 = f32[16,2,64,128]{3,2,1,0:T(8,128)} fusion(bf16[16,64,2,112]{1,3,2,0:T(8,128)(2,1)} %copy.90, bf16[16,64,2,112]{1,3,2,0:T(8,128)(2,1)S(1)} %copy.89, bf16[16,64,2,112]{1,0,3,2:T(8,128)(2,1)} %reshape.282, pred[16,64,128]{2,1,0:T(8,128)(4,1)S(1)} %broadcast_and_fusion), kind=kOutput, calls=%fused_computation.31 | convolution fusion | flops 61079552 | bytes 2555904 | tf_op jit(solution)/shard_map/bqhd,bkhd->bhqk/dot_general | solution.py:33
  135.4 7.3 %convolution_bitcast_fusion = f32[16,64,2,112]{3,1,2,0:T(8,128)} fusion(bf16[16,64,2,112]{1,3,2,0:T(8,128)(2,1)} %copy.84, bf16[16,64,2,112]{1,3,2,0:T(8,128)(2,1)} %copy.83, f32[16,2,64]{2,1,0:T(2,128)S(1)} %fusion.72, f32[16,2,64,128]{3,2,1,0:T(8,128)} %fusion.18), kind=kOutput, calls=%fused_computation.32 | convolution fusion | flops 61343872 | bytes 2891776 | tf_op jit(solution)/shard_map/bhqk,bkhd->bqhd/dot_general | solution.py:43
  142.6 2.1 copy.92
  144.7 1.6 reshape_reshape.3
  146.8 2.9 %convolution_convert_fusion = bf16[1024,1792]{1,0:T(8,128)(2,1)S(1)} fusion(bf16[1792,1120]{1,0:T(8,128)(2,1)} %all-gather.4.cloned.1.call-done, f32[1024,224]{1,0:T(8,128)} %reshape_reshape.3, f32[1088,224]{1,0:T(8,128)S(1)} %convert_select_fusion, bf16[1024,1,224]{2,0,1:T(8,128)(2,1)S(1)} %copy.110, f32[224]{0:T(256)S(1)} %bitcast.76, ...), kind=kOutput, calls=%fused_computation.7 | convolution fusion | flops 825982976 | bytes 9309184 | tf_op jit(solution)/shard_map/dot_general | solution.py:146
  150.0 8.1 %all_to_all.31 = bf16[4,2,128,1792]{3,2,0,1:T(8,128)(2,1)} all-to-all(bf16[4,2,128,1792]{3,2,0,1:T(8,128)(2,1)S(1)} %copy.94), channel_id=1, replica_groups=mesh['ry'=4,'rz'=8,'tpx'=4,'tpc'=2] {'tpc'}, dimensions={1} | all-to-all | bytes 7340032 | tf_op jit(solution)/shard_map/all_to_all | solution.py:105
  158.1 3.0 %reduce_sum.59 = bf16[4,128,1792]{2,1,0:T(8,128)(2,1)S(1)} reduce(bf16[4,2,128,1792]{3,2,0,1:T(8,128)(2,1)} %all_to_all.31, bf16[]{:T(256)} %constant.46.clone.1), dimensions={1}, to_apply=%region_3.4 | reduce | flops 917504 | bytes 5505026 | tf_op jit(solution)/shard_map/reduce_sum | solution.py:106
  161.1 26.4 %all_to_all.32 = bf16[4,128,1792]{2,1,0:T(8,128)(2,1)S(1)} all-to-all(bf16[4,128,1792]{2,1,0:T(8,128)(2,1)S(1)} %reduce_sum.59), channel_id=1, replica_groups=mesh['ry'=4,'rz'=8,'tpx'=4,'tpc'=2] {'tpx'}, dimensions={0} | all-to-all | bytes 3670016 | tf_op jit(solution)/shard_map/all_to_all | solution.py:107
  189.1 24.2 %all_to_all.33 = bf16[4,128,1792]{2,1,0:T(8,128)(2,1)S(1)} all-to-all(bf16[4,128,1792]{2,1,0:T(8,128)(2,1)S(1)} %tile.5), channel_id=1, replica_groups=mesh['ry'=4,'rz'=8,'tpx'=4,'tpc'=2] {'tpx'}, dimensions={0} | all-to-all | bytes 3670016 | tf_op jit(solution)/shard_map/all_to_all | solution.py:152
  213.3 2.7 collective-permute-start
  216.0 3.5 %collective-permute-done = bf16[512,1792]{1,0:T(8,128)(2,1)} collective-permute-done((bf16[512,1792]{1,0:T(8,128)(2,1)S(1)}, bf16[512,1792]{1,0:T(8,128)(2,1)}, u32[]{:S(2)}, u32[]{:S(2)}) %collective-permute-start) | collective-permute-done | bytes 1835040 | tf_op jit(solution)/shard_map/ppermute | solution.py:112
  219.6 7.0 %fusion.1 = f32[512,1792]{1,0:T(8,128)S(1)} fusion(bf16[512,1792]{1,0:T(8,128)(2,1)} %collective-permute-done, bf16[1792,2688]{1,0:T(8,128)(2,1)} %all-gather.8.cloned.1.call-done), kind=kOutput, calls=%fused_computation.3 | convolution fusion | flops 3288334336 | bytes 11927552 | tf_op jit(solution)/shard_map/dot_general | solution.py:116
  226.6 2.3 convolution_convert_fusion.1
  229.4 3.5 %fusion.3 = f32[512,1792]{1,0:T(8,128)S(1)} fusion(bf16[512,1792]{1,0:T(8,128)(2,1)S(1)} %bitcast.63, bf16[1792,2688]{1,0:T(8,128)(2,1)S(1)} %copy-done.8), kind=kOutput, calls=%fused_computation.5 | convolution fusion | flops 3288334336 | bytes 11927552 | tf_op jit(solution)/shard_map/dot_general | solution.py:116
  232.9 3.6 %add_convert_fusion = bf16[512,1792]{1,0:T(8,128)(2,1)} fusion(bf16[512,1792]{1,0:T(8,128)(2,1)S(1)} %collective-permute-done.1, bf16[1792,2688]{1,0:T(8,128)(2,1)S(1)} %copy-done.8, f32[512,1792]{1,0:T(8,128)S(1)} %fusion.3), kind=kOutput, calls=%fused_computation.9 | convolution fusion | flops 1651507200 | bytes 10551296 | tf_op jit(solution)/shard_map/dot_general | solution.py:118
  236.5 3.8 %all-to-all-start.5 = ((bf16[4,128,1792]{2,1,0:T(8,128)(2,1)}), bf16[4,128,1792]{2,1,0:T(8,128)(2,1)S(1)}, u32[]{:S(2)}, u32[]{:S(2)}) async-start(bf16[4,128,1792]{2,1,0:T(8,128)(2,1)} %bitcast.61), calls=%async_computation.5 | async-start | bytes 3670016 | tf_op jit(solution)/shard_map/all_to_all | solution.py:161
  241.2 3.5 %copy.96 = bf16[1,1024,224]{2,0,1:T(2,128)(2,1)} copy(bf16[1,1024,224]{1,2,0:T(8,128)(2,1)} %get-tuple-element.14) | data formatting | bytes 917504 | tf_op jit(solution)/shard_map/stack;squeeze | solution.py:75
  244.7 4.4 %pad_maximum_fusion = bf16[2,1024,224]{2,0,1:T(2,128)(2,1)} fusion(bf16[1,1024,224]{2,0,1:T(2,128)(2,1)S(1)} %copy.97, bf16[1,1024,224]{2,0,1:T(2,128)(2,1)} %copy.96), kind=kLoop, calls=%fused_computation.42 | loop fusion | flops 1835008 | bytes 1835008 | tf_op jit(solution)/shard_map/stack | solution.py:75
  249.1 2.0 gather_fusion.1
  251.8 11.7 %all-to-all-done.5 = bf16[4,128,1792]{2,1,0:T(8,128)(2,1)S(1)} async-done(((bf16[4,128,1792]{2,1,0:T(8,128)(2,1)}), bf16[4,128,1792]{2,1,0:T(8,128)(2,1)S(1)}, u32[]{:S(2)}, u32[]{:S(2)}) %all-to-all-start.5) | async-done | bytes 1835040 | tf_op jit(solution)/shard_map/all_to_all | solution.py:161
  (73 shorter events, 19.3 us)
Async XLA Ops:
  7.2 51.3 %all-gather.6.cloned.1.call-start = ((), (), s32[]{:S(2)}) async-start(), calls=%async_computation.7 | async-start | bytes 2709504 | tf_op jit(solution)/shard_map/all_gather | solution.py:81
  9.8 101.0 %all-gather.4.cloned.1.call-start = ((), (), s32[]{:S(2)}) async-start(), calls=%async_computation.6 | async-start | bytes 5160960 | tf_op jit(solution)/shard_map/all_gather | solution.py:82
  42.3 16.2 %copy-start.2 = (bf16[128,1792]{1,0:T(8,128)(2,1)S(1)}, bf16[128,1792]{1,0:T(8,128)(2,1)}, u32[]{:S(2)}) copy-start(bf16[128,1792]{1,0:T(8,128)(2,1)} %param.10) | copy-start | bytes 1376260
  42.3 16.4 %copy-start.5 = (f32[1792]{0:T(1024)S(1)}, f32[1792]{0:T(1024)}, u32[]{:S(2)}) copy-start(f32[1792]{0:T(1024)} %param.11) | copy-start | bytes 21508
  42.4 177.2 %all-gather.8.cloned.1.call-start = ((), (), s32[]{:S(2)}) async-start(), calls=%async_computation.8 | async-start | bytes 12042240 | tf_op jit(solution)/shard_map/all_gather | solution.py:82
  60.3 5.0 %copy-start.4 = (bf16[1,2,64,224]{3,2,1,0:T(8,128)(2,1)S(1)}, bf16[1,2,64,224]{3,2,1,0:T(8,128)(2,1)}, u32[]{:S(2)}) copy-start(bf16[1,2,64,224]{3,2,1,0:T(8,128)(2,1)} %param.18) | copy-start | bytes 172036
  60.3 6.2 %copy-start.7 = (f32[3,224]{1,0:T(4,128)S(1)}, f32[3,224]{1,0:T(4,128)}, u32[]{:S(2)}) copy-start(f32[3,224]{1,0:T(4,128)} %param.17) | copy-start | bytes 8068
  60.3 25.8 %all-to-all-start = ((bf16[4,128,1792]{2,1,0:T(8,128)(2,1)}), bf16[4,128,1792]{2,1,0:T(8,128)(2,1)S(1)}, u32[]{:S(2)}, u32[]{:S(2)}) async-start(bf16[4,128,1792]{2,1,0:T(8,128)(2,1)} %tile.4), calls=%async_computation | async-start | bytes 3670016 | tf_op jit(solution)/shard_map/all_to_all | solution.py:94
  142.6 3.7 %copy-start.3 = (bf16[1024,1,224]{0,2,1:T(8,128)(2,1)S(1)}, bf16[1024,1,224]{0,2,1:T(8,128)(2,1)}, u32[]{:S(2)}) copy-start(bf16[1024,1,224]{0,2,1:T(8,128)(2,1)} %get-tuple-element.19) | copy-start | bytes 1376260
  187.5 1.3 copy-start.6
  188.0 0.8 copy-start
  213.3 6.2 %collective-permute-start = (bf16[512,1792]{1,0:T(8,128)(2,1)S(1)}, bf16[512,1792]{1,0:T(8,128)(2,1)}, u32[]{:S(2)}, u32[]{:S(2)}) collective-permute-start(bf16[512,1792]{1,0:T(8,128)(2,1)S(1)} %bitcast.62), channel_id=1, source_target_pairs={{0,1},{1,0},{2,3},{3,2},{4,5},{5,4},{6,7},{7,6},{8,9},{9,8},{10,11... | collective-permute-start | bytes 5505032 | tf_op jit(solution)/shard_map/ppermute | solution.py:112
  219.6 7.0 %copy-start.8 = (bf16[1792,2688]{1,0:T(8,128)(2,1)S(1)}, bf16[1792,2688]{1,0:T(8,128)(2,1)}, u32[]{:S(2)}) copy-start(bf16[1792,2688]{1,0:T(8,128)(2,1)} %all-gather.8.cloned.1.call-done) | copy-start | bytes 28901380
  228.9 4.0 %collective-permute-start.1 = (bf16[512,1792]{1,0:T(8,128)(2,1)S(1)}, bf16[512,1792]{1,0:T(8,128)(2,1)S(1)}, u32[]{:S(2)}, u32[]{:S(2)}) collective-permute-start(bf16[512,1792]{1,0:T(8,128)(2,1)S(1)} %convolution_convert_fusion.1), channel_id=1, source_target_pairs={{0,1},{1,0},{2,3},{3,2},{4,5},{5,4},{6,7},{7,6},{8,9},{9,8},{10,11... | collective-permute-start | bytes 5505032 | tf_op jit(solution)/shard_map/ppermute | solution.py:112
  236.5 27.0 %all-to-all-start.5 = ((bf16[4,128,1792]{2,1,0:T(8,128)(2,1)}), bf16[4,128,1792]{2,1,0:T(8,128)(2,1)S(1)}, u32[]{:S(2)}, u32[]{:S(2)}) async-start(bf16[4,128,1792]{2,1,0:T(8,128)(2,1)} %bitcast.61), calls=%async_computation.5 | async-start | bytes 3670016 | tf_op jit(solution)/shard_map/all_to_all | solution.py:161
  249.1 14.6 %copy-start.1 = (bf16[128,1792]{1,0:T(8,128)(2,1)S(1)}, bf16[128,1792]{1,0:T(8,128)(2,1)}, u32[]{:S(2)}) copy-start(bf16[128,1792]{1,0:T(8,128)(2,1)} %copy-done) | copy-start | bytes 1376260
Sparse Core Ops, SparseCore 0:
  10.4 48.0 all-gather.5
  60.3 50.4 all-gather.3
  112.6 96.5 all-gather.7

commit v9 on v7

--- a/solution.py
+++ b/solution.py
@@ -156,8 +156,7 @@
     part_theirs = mlp_rows(theirs, ffn_all, down_t, ffn_width)
     back = core_swap(part_theirs)
     pair = (part_mine.astype(jnp.float32) + back.astype(jnp.float32)).astype(jnp.bfloat16)
-    chips = lax.all_to_all(pair.reshape(mine.shape), "tpx", 0, 0, tiled=True)
-    ffn_part = chips.astype(jnp.float32).sum(axis=0)
+    ffn_part = lax.psum_scatter(pair, "tpx", scatter_dimension=0, tiled=True).astype(jnp.float32)
     layer_out = (residual.astype(jnp.float32) + ffn_part).astype(jnp.bfloat16)
     return (layer_out, renewed[None])
 

time: 258 us -> 256 us (level)
  waiting for transfers between devices: 76.7 us -> 81.2 us
  starting transfers between devices: 12.1 us -> 8.21 us
    reduce_scatter x0 -> x1, waiting for transfers between devices: none -> 16.7 us  [local(): lax.psum_scatter(pair, 'tpx', scatter_dimension=0, tiled=True)]
    all_to_all x1 -> x0, waiting for transfers between devices: 11.7 us -> none  [local(): chips = lax.all_to_all(pair.reshape(mine.shape), 'tpx', 0, 0, tiled=True)]
    all_to_all x1 -> x0, starting transfers between devices: 3.84 us -> none  [local(): chips = lax.all_to_all(pair.reshape(mine.shape), 'tpx', 0, 0, tiled=True)]
where the time goes in v9:
time: 256 us; the launch traced here: 255 us
  waiting for transfers between devices  81.2 us (32%)
  blocking collectives  70.4 us (28%)
  matrix products  37.3 us (15%)
  local copies, waits for them, and re-layouts  28.2 us (11%)
  other arithmetic  15.3 us (6%)
  between operations  14.7 us (6%)
  starting transfers between devices  8.21 us (3%)
    all_gather x2, waiting for transfers between devices, gather_packed(): lax.all_gather(jnp.concatenate(pieces, axis=1), 'req', axis=0, tiled=True)  41.9 us
    all_to_all x1, blocking collectives, tp_sum_scatter(): chips = lax.all_to_all(pair, 'tpx', 0, 0, tiled=True)  26.5 us
    all_to_all x1, blocking collectives, local(): lax.all_to_all(jnp.tile(normed(residual, ffn_gain)[None], (nx, 1, 1)), 't...  24.2 us
    all_to_all x1, waiting for transfers between devices, tp_gather(): lax.all_to_all(jnp.tile(x[None], (nx, 1, 1)), 'tpx', 0, 0, tiled=True)  19 us
    reduce_scatter x1, waiting for transfers between devices, local(): lax.psum_scatter(pair, 'tpx', scatter_dimension=0, tiled=True)  16.7 us
    all_to_all x1, blocking collectives, tp_sum_scatter(): pair = lax.all_to_all(parts, 'tpc', 1, 1, tiled=True)  10.5 us
    dot_general x2, matrix products, mlp_rows(): gate_up = jnp.dot(rows, ffn_all, preferred_element_type=jnp.float32)  10.5 us
    all_to_all x1, blocking collectives, tp_gather(): got = lax.all_to_all(both, 'tpc', 1, 1, tiled=True)  9.19 us
  transfers between devices with their start and end apart: 6, of which 4 were waited for; matrix products, arithmetic and copies ran while one was open for 25% of the time, Pallas kernels for 0%

profile of v9, /device:TPU:1, one launch (start us, length us, event | category | flops | bytes accessed | tf_op | source)
XLA Modules:
  0.0 255.3 jit_solution(15443570003032676183)
XLA Ops:
  8.3 1.4 pad_maximum_fusion.4
  10.8 1.7 pad_maximum_fusion.3
  12.8 1.3 tile.4
  14.2 5.0 %all-to-all-start = ((bf16[4,128,1792]{2,1,0:T(8,128)(2,1)}), bf16[4,128,1792]{2,1,0:T(8,128)(2,1)S(1)}, u32[]{:S(2)}, u32[]{:S(2)}) async-start(bf16[4,128,1792]{2,1,0:T(8,128)(2,1)} %tile.4), calls=%async_computation | async-start | bytes 3670016 | tf_op jit(solution)/shard_map/all_to_all | solution.py:92
  21.8 19.0 %all-to-all-done = bf16[4,128,1792]{2,1,0:T(8,128)(2,1)S(1)} async-done(((bf16[4,128,1792]{2,1,0:T(8,128)(2,1)}), bf16[4,128,1792]{2,1,0:T(8,128)(2,1)S(1)}, u32[]{:S(2)}, u32[]{:S(2)}) %all-to-all-start) | async-done | bytes 1835040 | tf_op jit(solution)/shard_map/all_to_all | solution.py:92
  41.0 9.2 %all_to_all.25 = bf16[4,2,128,1792]{3,2,0,1:T(8,128)(2,1)S(1)} all-to-all(bf16[4,2,128,1792]{3,2,0,1:T(8,128)(2,1)S(1)} %broadcast_in_dim.24), channel_id=1, replica_groups=mesh['req'=32,'tpx'=4,'tpc'=2] {'tpc'}, dimensions={1} | all-to-all | bytes 7340032 | tf_op jit(solution)/shard_map/all_to_all | solution.py:94
  50.2 2.0 copy.81
  52.2 41.9 %all-gather.3.cloned.1.call-done = bf16[1792,1120]{1,0:T(8,128)(2,1)} async-done(((bf16[56,1120]{1,0:T(8,128)(2,1)}), bf16[1792,1120]{1,0:T(8,128)(2,1)}) %all-gather.3.cloned.1.call-update) | async-done | bytes 4014096 | tf_op jit(solution)/shard_map/all_gather | solution.py:80
  94.1 6.6 %fusion.13 = bf16[1024,896]{0,1:T(8,128)(2,1)S(1)} fusion(bf16[1024,1792]{1,0:T(8,128)(2,1)} %bitcast.59, bf16[1792,1120]{1,0:T(8,128)(2,1)} %all-gather.3.cloned.1.call-done), kind=kOutput, calls=%fused_computation.20 | convolution fusion | flops 3289251840 | bytes 8716288 | tf_op jit(solution)/shard_map/dot_general | solution.py:141
  100.7 1.4 slice_bitcast_fusion
  103.9 2.5 reshape.278
  109.5 2.2 reshape.254
  111.7 2.2 copy.83
  113.9 2.1 copy.84
  116.0 2.4 fusion.72
  118.4 3.0 %fusion.18 = f32[16,2,64,128]{3,2,1,0:T(8,128)} fusion(bf16[16,64,2,112]{1,3,2,0:T(8,128)(2,1)S(1)} %copy.90, bf16[16,64,2,112]{1,3,2,0:T(8,128)(2,1)S(1)} %copy.89, bf16[16,64,2,112]{1,0,3,2:T(8,128)(2,1)} %reshape.278, pred[16,64,128]{2,1,0:T(8,128)(4,1)S(1)} %broadcast_and_fusion), kind=kOutput, calls=%fused_computation.30 | convolution fusion | flops 61079552 | bytes 2555904 | tf_op jit(solution)/shard_map/bqhd,bkhd->bhqk/dot_general | solution.py:32
  121.5 6.3 %convolution_bitcast_fusion = f32[16,64,2,112]{3,1,2,0:T(8,128)S(1)} fusion(bf16[16,64,2,112]{1,3,2,0:T(8,128)(2,1)} %copy.84, bf16[16,64,2,112]{1,3,2,0:T(8,128)(2,1)} %copy.83, f32[16,2,64]{2,1,0:T(2,128)S(1)} %fusion.72, f32[16,2,64,128]{3,2,1,0:T(8,128)} %fusion.18), kind=kOutput, calls=%fused_computation.31 | convolution fusion | flops 61343872 | bytes 2891776 | tf_op jit(solution)/shard_map/bhqk,bkhd->bqhd/dot_general | solution.py:42
  130.4 2.6 %convolution_convert_fusion = bf16[1024,1792]{1,0:T(8,128)(2,1)S(1)} fusion(bf16[1792,1120]{1,0:T(8,128)(2,1)} %all-gather.3.cloned.1.call-done, f32[1024,224]{1,0:T(8,128)S(1)} %reshape_reshape.3, f32[1088,224]{1,0:T(8,128)S(1)} %convert_select_fusion, bf16[1024,1,224]{2,0,1:T(8,128)(2,1)S(1)} %copy.110, f32[224]{0:T(256)S(1)} %bitcast.74, ...), kind=kOutput, calls=%fused_computation.7 | convolution fusion | flops 825982976 | bytes 9309184 | tf_op jit(solution)/shard_map/dot_general | solution.py:144
  133.3 10.5 %all_to_all.26 = bf16[4,2,128,1792]{3,2,0,1:T(8,128)(2,1)} all-to-all(bf16[4,2,128,1792]{3,2,0,1:T(8,128)(2,1)S(1)} %copy.94), channel_id=1, replica_groups=mesh['req'=32,'tpx'=4,'tpc'=2] {'tpc'}, dimensions={1} | all-to-all | bytes 7340032 | tf_op jit(solution)/shard_map/all_to_all | solution.py:103
  143.8 2.9 %reduce_sum.50 = bf16[4,128,1792]{2,1,0:T(8,128)(2,1)S(1)} reduce(bf16[4,2,128,1792]{3,2,0,1:T(8,128)(2,1)} %all_to_all.26, bf16[]{:T(256)} %constant.46.clone.1), dimensions={1}, to_apply=%region_3.4 | reduce | flops 917504 | bytes 5505026 | tf_op jit(solution)/shard_map/reduce_sum | solution.py:104
  146.7 26.5 %all_to_all.27 = bf16[4,128,1792]{2,1,0:T(8,128)(2,1)S(1)} all-to-all(bf16[4,128,1792]{2,1,0:T(8,128)(2,1)S(1)} %reduce_sum.50), channel_id=1, replica_groups=mesh['req'=32,'tpx'=4,'tpc'=2] {'tpx'}, dimensions={0} | all-to-all | bytes 3670016 | tf_op jit(solution)/shard_map/all_to_all | solution.py:105
  174.2 24.2 %all_to_all.28 = bf16[4,128,1792]{2,1,0:T(8,128)(2,1)S(1)} all-to-all(bf16[4,128,1792]{2,1,0:T(8,128)(2,1)S(1)} %tile.5), channel_id=1, replica_groups=mesh['req'=32,'tpx'=4,'tpc'=2] {'tpx'}, dimensions={0} | all-to-all | bytes 3670016 | tf_op jit(solution)/shard_map/all_to_all | solution.py:150
  198.4 2.7 %collective-permute-start = (bf16[512,1792]{1,0:T(8,128)(2,1)S(1)}, bf16[512,1792]{1,0:T(8,128)(2,1)}, u32[]{:S(2)}, u32[]{:S(2)}) collective-permute-start(bf16[512,1792]{1,0:T(8,128)(2,1)S(1)} %bitcast.60), channel_id=1, source_target_pairs={{0,1},{1,0},{2,3},{3,2},{4,5},{5,4},{6,7},{7,6},{8,9},{9,8},{10,11... | collective-permute-start | bytes 5505032 | tf_op jit(solution)/shard_map/ppermute | solution.py:110
  201.1 3.5 %collective-permute-done = bf16[512,1792]{1,0:T(8,128)(2,1)} collective-permute-done((bf16[512,1792]{1,0:T(8,128)(2,1)S(1)}, bf16[512,1792]{1,0:T(8,128)(2,1)}, u32[]{:S(2)}, u32[]{:S(2)}) %collective-permute-start) | collective-permute-done | bytes 1835040 | tf_op jit(solution)/shard_map/ppermute | solution.py:110
  204.7 7.0 %fusion.1 = f32[512,1792]{1,0:T(8,128)S(1)} fusion(bf16[512,1792]{1,0:T(8,128)(2,1)} %collective-permute-done, bf16[1792,2688]{1,0:T(8,128)(2,1)} %all-gather.5.cloned.1.call-done), kind=kOutput, calls=%fused_computation.3 | convolution fusion | flops 3288334336 | bytes 11927552 | tf_op jit(solution)/shard_map/dot_general | solution.py:114
  211.7 2.3 convolution_convert_fusion.1
  214.5 3.5 %fusion.3 = f32[512,1792]{1,0:T(8,128)S(1)} fusion(bf16[512,1792]{1,0:T(8,128)(2,1)S(1)} %bitcast.61, bf16[1792,2688]{1,0:T(8,128)(2,1)S(1)} %copy-done.9), kind=kOutput, calls=%fused_computation.5 | convolution fusion | flops 3288334336 | bytes 11927552 | tf_op jit(solution)/shard_map/dot_general | solution.py:114
  218.0 3.6 %add_convert_fusion = bf16[512,1792]{1,0:T(8,128)(2,1)} fusion(bf16[512,1792]{1,0:T(8,128)(2,1)S(1)} %collective-permute-done.1, bf16[1792,2688]{1,0:T(8,128)(2,1)S(1)} %copy-done.9, f32[512,1792]{1,0:T(8,128)S(1)} %fusion.3), kind=kOutput, calls=%fused_computation.8 | convolution fusion | flops 1651507200 | bytes 10551296 | tf_op jit(solution)/shard_map/dot_general | solution.py:116
  224.0 3.4 %pad_maximum_fusion = bf16[2,1024,224]{2,0,1:T(2,128)(2,1)} fusion(bf16[1,1024,224]{2,0,1:T(2,128)(2,1)S(1)} %copy.97, bf16[1,1024,224]{2,0,1:T(2,128)(2,1)S(1)} %copy.96), kind=kLoop, calls=%fused_computation.41 | loop fusion | flops 1835008 | bytes 1835008 | tf_op jit(solution)/shard_map/stack | solution.py:74
  227.4 2.1 gather_fusion.1
  230.2 16.7 %reduce-scatter.2.cloned.1.call-done = bf16[128,1792]{1,0:T(8,128)(2,1)} async-done(((bf16[512,1792]{1,0:T(8,128)(2,1)}), bf16[128,1792]{1,0:T(8,128)(2,1)}) %reduce-scatter.2.cloned.1.call-update) | async-done | bytes 458768 | tf_op jit(solution)/shard_map/reduce_scatter | solution.py:159
  246.9 1.9 fusion.31
  (71 shorter events, 16.9 us)
Async XLA Ops:
  7.2 5.3 %copy-start = (bf16[128,1792]{1,0:T(8,128)(2,1)S(1)}, bf16[128,1792]{1,0:T(8,128)(2,1)}, u32[]{:S(2)}) copy-start(bf16[128,1792]{1,0:T(8,128)(2,1)} %param.10) | copy-start | bytes 1376260
  7.2 5.5 %copy-start.5 = (f32[1792]{0:T(1024)S(1)}, f32[1792]{0:T(1024)}, u32[]{:S(2)}) copy-start(f32[1792]{0:T(1024)} %param.11) | copy-start | bytes 21508
  7.2 86.9 %all-gather.3.cloned.1.call-start = ((), (), s32[]{:S(2)}) async-start(), calls=%async_computation.6 | async-start | bytes 4257792 | tf_op jit(solution)/shard_map/all_gather | solution.py:80
  9.8 194.9 %all-gather.5.cloned.1.call-start = ((), (), s32[]{:S(2)}) async-start(), calls=%async_computation.7 | async-start | bytes 9934848 | tf_op jit(solution)/shard_map/all_gather | solution.py:80
  14.2 5.6 %copy-start.4 = (bf16[1,2,64,224]{3,2,1,0:T(8,128)(2,1)S(1)}, bf16[1,2,64,224]{3,2,1,0:T(8,128)(2,1)}, u32[]{:S(2)}) copy-start(bf16[1,2,64,224]{3,2,1,0:T(8,128)(2,1)} %param.18) | copy-start | bytes 172036
  14.2 7.4 %copy-start.7 = (f32[3,224]{1,0:T(4,128)S(1)}, f32[3,224]{1,0:T(4,128)}, u32[]{:S(2)}) copy-start(f32[3,224]{1,0:T(4,128)} %param.17) | copy-start | bytes 8068
  14.2 26.6 %all-to-all-start = ((bf16[4,128,1792]{2,1,0:T(8,128)(2,1)}), bf16[4,128,1792]{2,1,0:T(8,128)(2,1)S(1)}, u32[]{:S(2)}, u32[]{:S(2)}) async-start(bf16[4,128,1792]{2,1,0:T(8,128)(2,1)} %tile.4), calls=%async_computation | async-start | bytes 3670016 | tf_op jit(solution)/shard_map/all_to_all | solution.py:92
  19.2 227.8 %reduce-scatter.2.cloned.1.call-start = ((), (), s32[]{:S(2)}) async-start(), calls=%async_computation.8 | async-start | bytes 2293760 | tf_op jit(solution)/shard_map/reduce_scatter | solution.py:159
  21.5 87.2 %copy-start.3 = (bf16[1,64,224]{2,1,0:T(8,128)(2,1)}, bf16[1,64,224]{2,1,0:T(8,128)(2,1)S(1)}, u32[]{:S(2)}) copy-start(bf16[1,64,224]{2,1,0:T(8,128)(2,1)S(1)} %copy.121) | copy-start | bytes 86020
  127.8 1.4 copy-start.2
  173.2 0.7 copy-start.6
  198.4 6.2 %collective-permute-start = (bf16[512,1792]{1,0:T(8,128)(2,1)S(1)}, bf16[512,1792]{1,0:T(8,128)(2,1)}, u32[]{:S(2)}, u32[]{:S(2)}) collective-permute-start(bf16[512,1792]{1,0:T(8,128)(2,1)S(1)} %bitcast.60), channel_id=1, source_target_pairs={{0,1},{1,0},{2,3},{3,2},{4,5},{5,4},{6,7},{7,6},{8,9},{9,8},{10,11... | collective-permute-start | bytes 5505032 | tf_op jit(solution)/shard_map/ppermute | solution.py:110
  204.7 7.0 %copy-start.9 = (bf16[1792,2688]{1,0:T(8,128)(2,1)S(1)}, bf16[1792,2688]{1,0:T(8,128)(2,1)}, u32[]{:S(2)}) copy-start(bf16[1792,2688]{1,0:T(8,128)(2,1)} %all-gather.5.cloned.1.call-done) | copy-start | bytes 28901380
  214.0 4.0 %collective-permute-start.1 = (bf16[512,1792]{1,0:T(8,128)(2,1)S(1)}, bf16[512,1792]{1,0:T(8,128)(2,1)S(1)}, u32[]{:S(2)}, u32[]{:S(2)}) collective-permute-start(bf16[512,1792]{1,0:T(8,128)(2,1)S(1)} %convolution_convert_fusion.1), channel_id=1, source_target_pairs={{0,1},{1,0},{2,3},{3,2},{4,5},{5,4},{6,7},{7,6},{8,9},{9,8},{10,11... | collective-permute-start | bytes 5505032 | tf_op jit(solution)/shard_map/ppermute | solution.py:110
  221.6 0.7 copy-start.8
  221.6 1.5 copy-start.1
Sparse Core Ops, SparseCore 0:
  11.2 82.8 all-gather.2
  96.7 103.9 all-gather.4
  221.8 25.0 reduce-scatter.1

commit v10 on v9

--- a/solution.py
+++ b/solution.py
@@ -141,10 +141,23 @@
     projected = jnp.dot(normed_all, mix_all, preferred_element_type=jnp.float32)
     projected = projected.astype(jnp.bfloat16).reshape(row_total, 4, feat_width)
     mixed_heads, renewed = mix_request(projected, past_cache[0], cached_len[0], conv_taps, WIN, HD)
-    attn_full = lax.dot_general(
-        mixed_heads, out_t, (((1,), (1,)), ((), ())), preferred_element_type=jnp.float32
-    )
-    attn_part = tp_sum_scatter(attn_full.astype(jnp.bfloat16))
+    nx = lax.axis_size("tpx")
+    nc = lax.axis_size("tpc")
+    me_c = lax.axis_index("tpc")
+    by_core = mixed_heads.reshape(nx, nc, -1, feat_width)
+    mine_rows = lax.dynamic_index_in_dim(by_core, me_c, axis=1, keepdims=False)
+    their_rows = lax.dynamic_index_in_dim(by_core, 1 - me_c, axis=1, keepdims=False)
+
+    def out_rows(r):
+        return lax.dot_general(
+            r.reshape(-1, feat_width), out_t, (((1,), (1,)), ((), ())),
+            preferred_element_type=jnp.float32,
+        ).astype(jnp.bfloat16)
+
+    back = core_swap(out_rows(their_rows))
+    pair = (out_rows(mine_rows).astype(jnp.float32) + back.astype(jnp.float32)).astype(jnp.bfloat16)
+    chips = lax.all_to_all(pair.reshape((nx, -1) + pair.shape[1:]), "tpx", 0, 0, tiled=True)
+    attn_part = chips.astype(jnp.float32).sum(axis=0)
     residual = (tokens.astype(jnp.float32) + attn_part).astype(jnp.bfloat16)
     nx = lax.axis_size("tpx")
     mine = lax.all_to_all(

time: 256 us -> 255 us (level)
  blocking collectives: 70.4 us -> 59.9 us
  waiting for transfers between devices: 81.2 us -> 88 us
  starting transfers between devices: 8.21 us -> 12.2 us
  other arithmetic: 15.3 us -> 12.7 us
    all_to_all x2 -> x1, blocking collectives: 37 us -> 26.5 us  [local(): lax.all_to_all(pair.reshape((nx, -1) + pair.shape[1:]), 'tpx', 0, 0, tile...]
    ppermute x2 -> x3, starting transfers between devices: 3.16 us -> 7.18 us  [core_swap(): return lax.ppermute(x, 'tpc', [(0, 1), (1, 0)])]
    ppermute x2 -> x3, waiting for transfers between devices: 3.55 us -> 6.96 us  [core_swap(): return lax.ppermute(x, 'tpc', [(0, 1), (1, 0)])]
    reduce_sum x2 -> x1, other arithmetic: 3.18 us -> 0.26 us  [local(): attn_part = chips.astype(jnp.float32).sum(axis=0)]
  transfers between devices with their start and end apart: 6 -> 7, of which waited for: 4 -> 6; matrix products, arithmetic and copies ran while one was open for 25% -> 24% of each run, Pallas kernels for 0% -> 0%
where the time goes in v10:
time: 255 us; the launch traced here: 254 us
  waiting for transfers between devices  88 us (35%)
  blocking collectives  59.9 us (23%)
  matrix products  38.5 us (15%)
  local copies, waits for them, and re-layouts  27.7 us (11%)
  between operations  14.7 us (6%)
  other arithmetic  12.7 us (5%)
  starting transfers between devices  12.2 us (5%)
    all_gather x2, waiting for transfers between devices, gather_packed(): lax.all_gather(jnp.concatenate(pieces, axis=1), 'req', axis=0, tiled=True)  43.3 us
    all_to_all x1, blocking collectives, local(): lax.all_to_all(pair.reshape((nx, -1) + pair.shape[1:]), 'tpx', 0, 0, tile...  26.5 us
    all_to_all x1, blocking collectives, local(): lax.all_to_all(jnp.tile(normed(residual, ffn_gain)[None], (nx, 1, 1)), 't...  24.2 us
    all_to_all x1, waiting for transfers between devices, tp_gather(): lax.all_to_all(jnp.tile(x[None], (nx, 1, 1)), 'tpx', 0, 0, tiled=True)  19 us
    reduce_scatter x1, waiting for transfers between devices, local(): lax.psum_scatter(pair, 'tpx', scatter_dimension=0, tiled=True)  18.6 us
    dot_general x2, matrix products, mlp_rows(): gate_up = jnp.dot(rows, ffn_all, preferred_element_type=jnp.float32)  10.5 us
    all_to_all x1, blocking collectives, tp_gather(): got = lax.all_to_all(both, 'tpc', 1, 1, tiled=True)  9.19 us
    ppermute x3, starting transfers between devices, core_swap(): return lax.ppermute(x, 'tpc', [(0, 1), (1, 0)])  7.18 us
  transfers between devices with their start and end apart: 7, of which 6 were waited for; matrix products, arithmetic and copies ran while one was open for 24% of the time, Pallas kernels for 0%

profile of v10, /device:TPU:1, one launch (start us, length us, event | category | flops | bytes accessed | tf_op | source)
XLA Modules:
  0.0 253.7 jit_solution(9108953400346048274)
XLA Ops:
  8.3 1.4 pad_maximum_fusion.4
  10.8 1.6 pad_maximum_fusion.3
  14.2 5.0 %all-to-all-start = ((bf16[4,128,1792]{2,1,0:T(8,128)(2,1)}), bf16[4,128,1792]{2,1,0:T(8,128)(2,1)S(1)}, u32[]{:S(2)}, u32[]{:S(2)}) async-start(bf16[4,128,1792]{2,1,0:T(8,128)(2,1)} %tile.4), calls=%async_computation | async-start | bytes 3670016 | tf_op jit(solution)/shard_map/all_to_all | solution.py:92
  21.7 19.0 %all-to-all-done = bf16[4,128,1792]{2,1,0:T(8,128)(2,1)S(1)} async-done(((bf16[4,128,1792]{2,1,0:T(8,128)(2,1)}), bf16[4,128,1792]{2,1,0:T(8,128)(2,1)S(1)}, u32[]{:S(2)}, u32[]{:S(2)}) %all-to-all-start) | async-done | bytes 1835040 | tf_op jit(solution)/shard_map/all_to_all | solution.py:92
  41.0 9.2 %all_to_all.20 = bf16[4,2,128,1792]{3,2,0,1:T(8,128)(2,1)S(1)} all-to-all(bf16[4,2,128,1792]{3,2,0,1:T(8,128)(2,1)S(1)} %broadcast_in_dim.24), channel_id=1, replica_groups=mesh['req'=32,'tpx'=4,'tpc'=2] {'tpc'}, dimensions={1} | all-to-all | bytes 7340032 | tf_op jit(solution)/shard_map/all_to_all | solution.py:94
  50.2 2.0 copy.67
  52.2 41.9 %all-gather.3.cloned.1.call-done = bf16[1792,1120]{1,0:T(8,128)(2,1)} async-done(((bf16[56,1120]{1,0:T(8,128)(2,1)}), bf16[1792,1120]{1,0:T(8,128)(2,1)}) %all-gather.3.cloned.1.call-update) | async-done | bytes 4014096 | tf_op jit(solution)/shard_map/all_gather | solution.py:80
  94.1 6.6 %fusion.13 = bf16[1024,896]{0,1:T(8,128)(2,1)S(1)} fusion(bf16[1024,1792]{1,0:T(8,128)(2,1)} %bitcast.61, bf16[1792,1120]{1,0:T(8,128)(2,1)} %all-gather.3.cloned.1.call-done), kind=kOutput, calls=%fused_computation.22 | convolution fusion | flops 3289251840 | bytes 8716288 | tf_op jit(solution)/shard_map/dot_general | solution.py:141
  100.7 1.4 slice_bitcast_fusion
  103.9 2.4 reshape.292
  109.6 2.2 reshape.265
  111.7 2.1 copy.69
  113.9 2.1 copy.70
  116.0 2.4 fusion.68
  118.5 3.0 %fusion.18 = f32[16,2,64,128]{3,2,1,0:T(8,128)} fusion(bf16[16,64,2,112]{1,3,2,0:T(8,128)(2,1)S(1)} %copy.76, bf16[16,64,2,112]{1,3,2,0:T(8,128)(2,1)S(1)} %copy.75, bf16[16,64,2,112]{1,0,3,2:T(8,128)(2,1)} %reshape.292, pred[16,64,128]{2,1,0:T(8,128)(4,1)S(1)} %broadcast_and_fusion), kind=kOutput, calls=%fused_computation.32 | convolution fusion | flops 61079552 | bytes 2555904 | tf_op jit(solution)/shard_map/bqhd,bkhd->bhqk/dot_general | solution.py:32
  121.5 6.3 %convolution_bitcast_fusion = f32[16,64,2,112]{3,1,2,0:T(8,128)S(1)} fusion(bf16[16,64,2,112]{1,3,2,0:T(8,128)(2,1)} %copy.70, bf16[16,64,2,112]{1,3,2,0:T(8,128)(2,1)} %copy.69, f32[16,2,64]{2,1,0:T(2,128)S(1)} %fusion.68, f32[16,2,64,128]{3,2,1,0:T(8,128)} %fusion.18), kind=kOutput, calls=%fused_computation.33 | convolution fusion | flops 61343872 | bytes 2891776 | tf_op jit(solution)/shard_map/bhqk,bkhd->bqhd/dot_general | solution.py:42
  131.0 1.9 convolution_convert_fusion
  132.8 3.3 %collective-permute-start = (bf16[512,1792]{1,0:T(8,128)(2,1)S(1)}, bf16[512,1792]{1,0:T(8,128)(2,1)S(1)}, u32[]{:S(2)}, u32[]{:S(2)}) collective-permute-start(bf16[512,1792]{1,0:T(8,128)(2,1)S(1)} %convolution_convert_fusion), channel_id=1, source_target_pairs={{0,1},{1,0},{2,3},{3,2},{4,5},{5,4},{6,7},{7,6},{8,9},{9,8},{10,11... | collective-permute-start | bytes 5505032 | tf_op jit(solution)/shard_map/ppermute | solution.py:110
  136.1 3.4 %collective-permute-done = bf16[512,1792]{1,0:T(8,128)(2,1)S(1)} collective-permute-done((bf16[512,1792]{1,0:T(8,128)(2,1)S(1)}, bf16[512,1792]{1,0:T(8,128)(2,1)S(1)}, u32[]{:S(2)}, u32[]{:S(2)}) %collective-permute-start) | collective-permute-done | bytes 1835040 | tf_op jit(solution)/shard_map/ppermute | solution.py:110
  139.5 1.9 add_convert_fusion.1
  141.4 26.5 %all_to_all.21 = bf16[4,128,1792]{2,1,0:T(8,128)(2,1)S(1)} all-to-all(bf16[4,128,1792]{2,1,0:T(8,128)(2,1)S(1)} %bitcast.60), channel_id=1, replica_groups=mesh['req'=32,'tpx'=4,'tpc'=2] {'tpx'}, dimensions={0} | all-to-all | bytes 3670016 | tf_op jit(solution)/shard_map/all_to_all | solution.py:159
  168.9 24.2 %all_to_all.22 = bf16[4,128,1792]{2,1,0:T(8,128)(2,1)S(1)} all-to-all(bf16[4,128,1792]{2,1,0:T(8,128)(2,1)S(1)} %tile.5), channel_id=1, replica_groups=mesh['req'=32,'tpx'=4,'tpc'=2] {'tpx'}, dimensions={0} | all-to-all | bytes 3670016 | tf_op jit(solution)/shard_map/all_to_all | solution.py:163
  193.1 2.7 %collective-permute-start.1 = (bf16[512,1792]{1,0:T(8,128)(2,1)S(1)}, bf16[512,1792]{1,0:T(8,128)(2,1)}, u32[]{:S(2)}, u32[]{:S(2)}) collective-permute-start(bf16[512,1792]{1,0:T(8,128)(2,1)S(1)} %bitcast.63), channel_id=1, source_target_pairs={{0,1},{1,0},{2,3},{3,2},{4,5},{5,4},{6,7},{7,6},{8,9},{9,8},{10,11... | collective-permute-start | bytes 5505032 | tf_op jit(solution)/shard_map/ppermute | solution.py:110
  195.8 3.5 %collective-permute-done.1 = bf16[512,1792]{1,0:T(8,128)(2,1)} collective-permute-done((bf16[512,1792]{1,0:T(8,128)(2,1)S(1)}, bf16[512,1792]{1,0:T(8,128)(2,1)}, u32[]{:S(2)}, u32[]{:S(2)}) %collective-permute-start.1) | collective-permute-done | bytes 1835040 | tf_op jit(solution)/shard_map/ppermute | solution.py:110
  200.7 7.0 %fusion.1 = f32[512,1792]{1,0:T(8,128)S(1)} fusion(bf16[512,1792]{1,0:T(8,128)(2,1)} %collective-permute-done.1, bf16[1792,2688]{1,0:T(8,128)(2,1)} %all-gather.5.cloned.1.call-done), kind=kOutput, calls=%fused_computation.3 | convolution fusion | flops 3288334336 | bytes 11927552 | tf_op jit(solution)/shard_map/dot_general | solution.py:114
  207.8 2.3 convolution_convert_fusion.2
  211.3 3.5 %fusion.3 = f32[512,1792]{1,0:T(8,128)S(1)} fusion(bf16[512,1792]{1,0:T(8,128)(2,1)S(1)} %bitcast.64, bf16[1792,2688]{1,0:T(8,128)(2,1)S(1)} %copy-done.9), kind=kOutput, calls=%fused_computation.5 | convolution fusion | flops 3288334336 | bytes 11927552 | tf_op jit(solution)/shard_map/dot_general | solution.py:114
  214.8 3.6 %add_convert_fusion = bf16[512,1792]{1,0:T(8,128)(2,1)} fusion(bf16[512,1792]{1,0:T(8,128)(2,1)S(1)} %collective-permute-done.2, bf16[1792,2688]{1,0:T(8,128)(2,1)S(1)} %copy-done.9, f32[512,1792]{1,0:T(8,128)S(1)} %fusion.3), kind=kOutput, calls=%fused_computation.7 | convolution fusion | flops 1651507200 | bytes 10551296 | tf_op jit(solution)/shard_map/dot_general | solution.py:116
  220.7 3.4 %pad_maximum_fusion = bf16[2,1024,224]{2,0,1:T(2,128)(2,1)} fusion(bf16[1,1024,224]{2,0,1:T(2,128)(2,1)S(1)} %copy.84, bf16[1,1024,224]{2,0,1:T(2,128)(2,1)S(1)} %copy.83), kind=kLoop, calls=%fused_computation.43 | loop fusion | flops 1835008 | bytes 1835008 | tf_op jit(solution)/shard_map/stack | solution.py:74
  224.1 1.9 gather_fusion.1
  226.7 18.6 %reduce-scatter.2.cloned.1.call-done = bf16[128,1792]{1,0:T(8,128)(2,1)} async-done(((bf16[512,1792]{1,0:T(8,128)(2,1)}), bf16[128,1792]{1,0:T(8,128)(2,1)}) %reduce-scatter.2.cloned.1.call-update) | async-done | bytes 458768 | tf_op jit(solution)/shard_map/reduce_scatter | solution.py:172
  245.3 1.9 fusion.31
  (73 shorter events, 20.6 us)
Async XLA Ops:
  7.2 5.3 %copy-start = (bf16[128,1792]{1,0:T(8,128)(2,1)S(1)}, bf16[128,1792]{1,0:T(8,128)(2,1)}, u32[]{:S(2)}) copy-start(bf16[128,1792]{1,0:T(8,128)(2,1)} %param.10) | copy-start | bytes 1376260
  7.2 5.4 %copy-start.5 = (f32[1792]{0:T(1024)S(1)}, f32[1792]{0:T(1024)}, u32[]{:S(2)}) copy-start(f32[1792]{0:T(1024)} %param.11) | copy-start | bytes 21508
  7.2 86.9 %all-gather.3.cloned.1.call-start = ((), (), s32[]{:S(2)}) async-start(), calls=%async_computation.5 | async-start | bytes 4257792 | tf_op jit(solution)/shard_map/all_gather | solution.py:80
  9.8 191.0 %all-gather.5.cloned.1.call-start = ((), (), s32[]{:S(2)}) async-start(), calls=%async_computation.6 | async-start | bytes 9934848 | tf_op jit(solution)/shard_map/all_gather | solution.py:80
  14.2 5.6 %copy-start.4 = (bf16[1,2,64,224]{3,2,1,0:T(8,128)(2,1)S(1)}, bf16[1,2,64,224]{3,2,1,0:T(8,128)(2,1)}, u32[]{:S(2)}) copy-start(bf16[1,2,64,224]{3,2,1,0:T(8,128)(2,1)} %param.18) | copy-start | bytes 172036
  14.2 7.4 %copy-start.7 = (f32[3,224]{1,0:T(4,128)S(1)}, f32[3,224]{1,0:T(4,128)}, u32[]{:S(2)}) copy-start(f32[3,224]{1,0:T(4,128)} %param.17) | copy-start | bytes 8068
  14.2 26.6 %all-to-all-start = ((bf16[4,128,1792]{2,1,0:T(8,128)(2,1)}), bf16[4,128,1792]{2,1,0:T(8,128)(2,1)S(1)}, u32[]{:S(2)}, u32[]{:S(2)}) async-start(bf16[4,128,1792]{2,1,0:T(8,128)(2,1)} %tile.4), calls=%async_computation | async-start | bytes 3670016 | tf_op jit(solution)/shard_map/all_to_all | solution.py:92
  19.1 226.2 %reduce-scatter.2.cloned.1.call-start = ((), (), s32[]{:S(2)}) async-start(), calls=%async_computation.7 | async-start | bytes 2293760 | tf_op jit(solution)/shard_map/reduce_scatter | solution.py:172
  21.4 87.3 %copy-start.3 = (bf16[1,64,224]{2,1,0:T(8,128)(2,1)}, bf16[1,64,224]{2,1,0:T(8,128)(2,1)S(1)}, u32[]{:S(2)}) copy-start(bf16[1,64,224]{2,1,0:T(8,128)(2,1)S(1)} %copy.112) | copy-start | bytes 86020
  127.8 1.4 copy-start.2
  132.8 6.7 %collective-permute-start = (bf16[512,1792]{1,0:T(8,128)(2,1)S(1)}, bf16[512,1792]{1,0:T(8,128)(2,1)S(1)}, u32[]{:S(2)}, u32[]{:S(2)}) collective-permute-start(bf16[512,1792]{1,0:T(8,128)(2,1)S(1)} %convolution_convert_fusion), channel_id=1, source_target_pairs={{0,1},{1,0},{2,3},{3,2},{4,5},{5,4},{6,7},{7,6},{8,9},{9,8},{10,11... | collective-permute-start | bytes 5505032 | tf_op jit(solution)/shard_map/ppermute | solution.py:110
  167.9 0.7 copy-start.6
  193.1 6.2 %collective-permute-start.1 = (bf16[512,1792]{1,0:T(8,128)(2,1)S(1)}, bf16[512,1792]{1,0:T(8,128)(2,1)}, u32[]{:S(2)}, u32[]{:S(2)}) collective-permute-start(bf16[512,1792]{1,0:T(8,128)(2,1)S(1)} %bitcast.63), channel_id=1, source_target_pairs={{0,1},{1,0},{2,3},{3,2},{4,5},{5,4},{6,7},{7,6},{8,9},{9,8},{10,11... | collective-permute-start | bytes 5505032 | tf_op jit(solution)/shard_map/ppermute | solution.py:110
  200.7 7.0 %copy-start.9 = (bf16[1792,2688]{1,0:T(8,128)(2,1)S(1)}, bf16[1792,2688]{1,0:T(8,128)(2,1)}, u32[]{:S(2)}) copy-start(bf16[1792,2688]{1,0:T(8,128)(2,1)} %all-gather.5.cloned.1.call-done) | copy-start | bytes 28901380
  210.1 4.7 %collective-permute-start.2 = (bf16[512,1792]{1,0:T(8,128)(2,1)S(1)}, bf16[512,1792]{1,0:T(8,128)(2,1)S(1)}, u32[]{:S(2)}, u32[]{:S(2)}) collective-permute-start(bf16[512,1792]{1,0:T(8,128)(2,1)S(1)} %convolution_convert_fusion.2), channel_id=1, source_target_pairs={{0,1},{1,0},{2,3},{3,2},{4,5},{5,4},{6,7},{7,6},{8,9},{9,8},{10,11... | collective-permute-start | bytes 5505032 | tf_op jit(solution)/shard_map/ppermute | solution.py:110
  218.4 0.6 copy-start.8
  218.4 1.5 copy-start.1
Sparse Core Ops, SparseCore 0:
  11.2 82.8 all-gather.2
  96.7 103.9 all-gather.4
  218.5 26.7 reduce-scatter.1

commit v11 on v10

--- a/solution.py
+++ b/solution.py
@@ -86,26 +86,6 @@
     return parts
 
 
-def tp_gather(x):
-    nx = lax.axis_size("tpx")
-    nc = lax.axis_size("tpc")
-    by_chip = lax.all_to_all(jnp.tile(x[None], (nx, 1, 1)), "tpx", 0, 0, tiled=True)
-    both = jnp.broadcast_to(by_chip[:, None], (nx, nc) + x.shape)
-    got = lax.all_to_all(both, "tpc", 1, 1, tiled=True)
-    return got.reshape((nx * nc * x.shape[0],) + x.shape[1:])
-
-
-def tp_sum_scatter(x):
-    nx = lax.axis_size("tpx")
-    nc = lax.axis_size("tpc")
-    rows = x.shape[0] // (nx * nc)
-    parts = x.reshape((nx, nc, rows) + x.shape[1:])
-    pair = lax.all_to_all(parts, "tpc", 1, 1, tiled=True)
-    pair = pair.astype(jnp.float32).sum(axis=1).astype(jnp.bfloat16)
-    chips = lax.all_to_all(pair, "tpx", 0, 0, tiled=True)
-    return chips.astype(jnp.float32).sum(axis=0)
-
-
 def core_swap(x):
     return lax.ppermute(x, "tpc", [(0, 1), (1, 0)])
 
@@ -136,7 +116,16 @@
     rows = mix_weight.shape[0]
     mix_all, out_t = gather_packed([mix_weight.reshape(rows, -1), out_weight.T])
     ffn_all, down_t = gather_packed([ffn_weight.reshape(rows, -1), down_weight.T])
-    normed_all = tp_gather(normed(tokens, norm_gain))
+    nxt = lax.axis_size("tpx")
+    tok_mine = lax.all_to_all(
+        jnp.tile(normed(tokens, norm_gain)[None], (nxt, 1, 1)), "tpx", 0, 0, tiled=True
+    )
+    tok_theirs = core_swap(tok_mine)
+    first = lax.axis_index("tpc") == 0
+    pairs = jnp.stack(
+        [jnp.where(first, tok_mine, tok_theirs), jnp.where(first, tok_theirs, tok_mine)], axis=1
+    )
+    normed_all = pairs.reshape((-1,) + tok_mine.shape[2:])
     row_total = normed_all.shape[0]
     projected = jnp.dot(normed_all, mix_all, preferred_element_type=jnp.float32)
     projected = projected.astype(jnp.bfloat16).reshape(row_total, 4, feat_width)

time: 255 us -> 255 us (level)
  blocking collectives: 59.9 us -> 78 us
  waiting for transfers between devices: 88 us -> 72.3 us
  other arithmetic: 12.7 us -> 16.6 us
  local copies, waits for them, and re-layouts: 27.7 us -> 24.4 us
  starting transfers between devices: 12.2 us -> 9.25 us
    all_to_all x1 -> x0, waiting for transfers between devices: 19 us -> none  [tp_gather(): lax.all_to_all(jnp.tile(x[None], (nx, 1, 1)), 'tpx', 0, 0, tiled=True)]
    all_to_all x1, blocking collectives: 9.19 us -> 27.3 us  [local(): lax.all_to_all(jnp.tile(normed(tokens, norm_gain)[None], (nxt, 1, 1)), 't...]
    all_to_all x1 -> x0, starting transfers between devices: 4.97 us -> none  [tp_gather(): lax.all_to_all(jnp.tile(x[None], (nx, 1, 1)), 'tpx', 0, 0, tiled=True)]
    another operation x0 -> x2, other arithmetic: none -> 3.82 us  [local(): jnp.stack([jnp.where(first, tok_mine, tok_theirs), jnp.where(first, tok_t...]
    ppermute x3 -> x4, starting transfers between devices: 7.18 us -> 9.13 us  [core_swap(): return lax.ppermute(x, 'tpc', [(0, 1), (1, 0)])]
    ppermute x3 -> x4, waiting for transfers between devices: 6.96 us -> 7.95 us  [core_swap(): return lax.ppermute(x, 'tpc', [(0, 1), (1, 0)])]
where the time goes in v11:
time: 255 us; the launch traced here: 254 us
  blocking collectives  78 us (31%)
  waiting for transfers between devices  72.3 us (28%)
  matrix products  38.5 us (15%)
  local copies, waits for them, and re-layouts  24.4 us (10%)
  other arithmetic  16.6 us (7%)
  between operations  14.8 us (6%)
  starting transfers between devices  9.25 us (4%)
    all_gather x2, waiting for transfers between devices, gather_packed(): lax.all_gather(jnp.concatenate(pieces, axis=1), 'req', axis=0, tiled=True)  45.7 us
    all_to_all x1, blocking collectives, local(): lax.all_to_all(jnp.tile(normed(tokens, norm_gain)[None], (nxt, 1, 1)), 't...  27.3 us
    all_to_all x1, blocking collectives, local(): lax.all_to_all(pair.reshape((nx, -1) + pair.shape[1:]), 'tpx', 0, 0, tile...  26.5 us
    all_to_all x1, blocking collectives, local(): lax.all_to_all(jnp.tile(normed(residual, ffn_gain)[None], (nx, 1, 1)), 't...  24.2 us
    reduce_scatter x1, waiting for transfers between devices, local(): lax.psum_scatter(pair, 'tpx', scatter_dimension=0, tiled=True)  18.6 us
    dot_general x2, matrix products, mlp_rows(): gate_up = jnp.dot(rows, ffn_all, preferred_element_type=jnp.float32)  10.5 us
    ppermute x4, starting transfers between devices, core_swap(): return lax.ppermute(x, 'tpc', [(0, 1), (1, 0)])  9.13 us
    ppermute x4, waiting for transfers between devices, core_swap(): return lax.ppermute(x, 'tpc', [(0, 1), (1, 0)])  7.95 us
  transfers between devices with their start and end apart: 7, of which 6 were waited for; matrix products, arithmetic and copies ran while one was open for 24% of the time, Pallas kernels for 0%

profile of v11, /device:TPU:1, one launch (start us, length us, event | category | flops | bytes accessed | tf_op | source)
XLA Modules:
  0.0 253.7 jit_solution(14736242709046291994)
XLA Ops:
  8.3 1.4 pad_maximum_fusion.5
  10.8 1.6 pad_maximum_fusion.4
  13.0 27.3 %all_to_all.15 = bf16[4,128,1792]{2,1,0:T(8,128)(2,1)S(1)} all-to-all(bf16[4,128,1792]{2,1,0:T(8,128)(2,1)S(1)} %tile.4), channel_id=1, replica_groups=mesh['req'=32,'tpx'=4,'tpc'=2] {'tpx'}, dimensions={0} | all-to-all | bytes 3670016 | tf_op jit(solution)/shard_map/all_to_all | solution.py:120
  40.3 2.0 collective-permute-start
  45.8 1.7 select_bitcast_fusion.1
  47.6 2.1 pad_maximum_fusion
  49.6 44.5 %all-gather.3.cloned.1.call-done = bf16[1792,1120]{1,0:T(8,128)(2,1)} async-done(((bf16[56,1120]{1,0:T(8,128)(2,1)}), bf16[1792,1120]{1,0:T(8,128)(2,1)}) %all-gather.3.cloned.1.call-update) | async-done | bytes 4014096 | tf_op jit(solution)/shard_map/all_gather | solution.py:80
  94.1 6.6 %fusion.13 = bf16[1024,896]{0,1:T(8,128)(2,1)S(1)} fusion(bf16[1024,1792]{1,0:T(8,128)(2,1)} %bitcast.67, bf16[1792,1120]{1,0:T(8,128)(2,1)} %all-gather.3.cloned.1.call-done), kind=kOutput, calls=%fused_computation.25 | convolution fusion | flops 3289251840 | bytes 8716288 | tf_op jit(solution)/shard_map/dot_general | solution.py:130
  100.7 1.4 slice_bitcast_fusion
  103.9 2.6 %reshape.291 = bf16[16,64,2,112]{1,0,3,2:T(8,128)(2,1)} reshape(bf16[1024,1,224]{0,2,1:T(8,128)(2,1)} %get-tuple-element.14) | data formatting | bytes 917504 | tf_op jit(solution)/shard_map/reshape;reshape;squeeze | solution.py:22
  109.7 2.2 reshape.264
  111.9 2.1 copy.32
  114.0 2.1 copy.33
  116.2 2.4 fusion.68
  118.6 3.0 %fusion.18 = f32[16,2,64,128]{3,2,1,0:T(8,128)} fusion(bf16[16,64,2,112]{1,3,2,0:T(8,128)(2,1)S(1)} %copy.39, bf16[16,64,2,112]{1,3,2,0:T(8,128)(2,1)S(1)} %copy.38, bf16[16,64,2,112]{1,0,3,2:T(8,128)(2,1)} %reshape.291, pred[16,64,128]{2,1,0:T(8,128)(4,1)S(1)} %broadcast_and_fusion), kind=kOutput, calls=%fused_computation.35 | convolution fusion | flops 61079552 | bytes 2555904 | tf_op jit(solution)/shard_map/bqhd,bkhd->bhqk/dot_general | solution.py:32
  121.6 6.3 %convolution_bitcast_fusion = f32[16,64,2,112]{3,1,2,0:T(8,128)S(1)} fusion(bf16[16,64,2,112]{1,3,2,0:T(8,128)(2,1)} %copy.33, bf16[16,64,2,112]{1,3,2,0:T(8,128)(2,1)} %copy.32, f32[16,2,64]{2,1,0:T(2,128)S(1)} %fusion.68, f32[16,2,64,128]{3,2,1,0:T(8,128)} %fusion.18), kind=kOutput, calls=%fused_computation.36 | convolution fusion | flops 61343872 | bytes 2891776 | tf_op jit(solution)/shard_map/bhqk,bkhd->bqhd/dot_general | solution.py:42
  131.1 1.9 convolution_convert_fusion
  133.0 3.3 %collective-permute-start.1 = (bf16[512,1792]{1,0:T(8,128)(2,1)S(1)}, bf16[512,1792]{1,0:T(8,128)(2,1)S(1)}, u32[]{:S(2)}, u32[]{:S(2)}) collective-permute-start(bf16[512,1792]{1,0:T(8,128)(2,1)S(1)} %convolution_convert_fusion), channel_id=1, source_target_pairs={{0,1},{1,0},{2,3},{3,2},{4,5},{5,4},{6,7},{7,6},{8,9},{9,8},{10,11... | collective-permute-start | bytes 5505032 | tf_op jit(solution)/shard_map/ppermute | solution.py:90
  136.3 3.4 %collective-permute-done.1 = bf16[512,1792]{1,0:T(8,128)(2,1)S(1)} collective-permute-done((bf16[512,1792]{1,0:T(8,128)(2,1)S(1)}, bf16[512,1792]{1,0:T(8,128)(2,1)S(1)}, u32[]{:S(2)}, u32[]{:S(2)}) %collective-permute-start.1) | collective-permute-done | bytes 1835040 | tf_op jit(solution)/shard_map/ppermute | solution.py:90
  139.7 1.9 add_convert_fusion.1
  141.6 26.5 %all_to_all.16 = bf16[4,128,1792]{2,1,0:T(8,128)(2,1)S(1)} all-to-all(bf16[4,128,1792]{2,1,0:T(8,128)(2,1)S(1)} %bitcast.66), channel_id=1, replica_groups=mesh['req'=32,'tpx'=4,'tpc'=2] {'tpx'}, dimensions={0} | all-to-all | bytes 3670016 | tf_op jit(solution)/shard_map/all_to_all | solution.py:148
  169.0 24.2 %all_to_all.17 = bf16[4,128,1792]{2,1,0:T(8,128)(2,1)S(1)} all-to-all(bf16[4,128,1792]{2,1,0:T(8,128)(2,1)S(1)} %tile.5), channel_id=1, replica_groups=mesh['req'=32,'tpx'=4,'tpc'=2] {'tpx'}, dimensions={0} | all-to-all | bytes 3670016 | tf_op jit(solution)/shard_map/all_to_all | solution.py:152
  193.3 2.7 %collective-permute-start.2 = (bf16[512,1792]{1,0:T(8,128)(2,1)S(1)}, bf16[512,1792]{1,0:T(8,128)(2,1)}, u32[]{:S(2)}, u32[]{:S(2)}) collective-permute-start(bf16[512,1792]{1,0:T(8,128)(2,1)S(1)} %bitcast.69), channel_id=1, source_target_pairs={{0,1},{1,0},{2,3},{3,2},{4,5},{5,4},{6,7},{7,6},{8,9},{9,8},{10,11... | collective-permute-start | bytes 5505032 | tf_op jit(solution)/shard_map/ppermute | solution.py:90
  196.0 3.5 %collective-permute-done.2 = bf16[512,1792]{1,0:T(8,128)(2,1)} collective-permute-done((bf16[512,1792]{1,0:T(8,128)(2,1)S(1)}, bf16[512,1792]{1,0:T(8,128)(2,1)}, u32[]{:S(2)}, u32[]{:S(2)}) %collective-permute-start.2) | collective-permute-done | bytes 1835040 | tf_op jit(solution)/shard_map/ppermute | solution.py:90
  200.7 7.0 %fusion.1 = f32[512,1792]{1,0:T(8,128)S(1)} fusion(bf16[512,1792]{1,0:T(8,128)(2,1)} %collective-permute-done.2, bf16[1792,2688]{1,0:T(8,128)(2,1)} %all-gather.5.cloned.1.call-done), kind=kOutput, calls=%fused_computation.3 | convolution fusion | flops 3288334336 | bytes 11927552 | tf_op jit(solution)/shard_map/dot_general | solution.py:94
  207.8 2.3 convolution_convert_fusion.2
  211.3 3.5 %fusion.3 = f32[512,1792]{1,0:T(8,128)S(1)} fusion(bf16[512,1792]{1,0:T(8,128)(2,1)S(1)} %bitcast.70, bf16[1792,2688]{1,0:T(8,128)(2,1)S(1)} %copy-done.9), kind=kOutput, calls=%fused_computation.5 | convolution fusion | flops 3288334336 | bytes 11927552 | tf_op jit(solution)/shard_map/dot_general | solution.py:94
  214.8 3.6 %add_convert_fusion = bf16[512,1792]{1,0:T(8,128)(2,1)} fusion(bf16[512,1792]{1,0:T(8,128)(2,1)S(1)} %collective-permute-done.3, bf16[1792,2688]{1,0:T(8,128)(2,1)S(1)} %copy-done.9, f32[512,1792]{1,0:T(8,128)S(1)} %fusion.3), kind=kOutput, calls=%fused_computation.8 | convolution fusion | flops 1651507200 | bytes 10551296 | tf_op jit(solution)/shard_map/dot_general | solution.py:96
  220.7 3.4 %pad_maximum_fusion.1 = bf16[2,1024,224]{2,0,1:T(2,128)(2,1)} fusion(bf16[1,1024,224]{2,0,1:T(2,128)(2,1)S(1)} %copy.47, bf16[1,1024,224]{2,0,1:T(2,128)(2,1)S(1)} %copy.46), kind=kLoop, calls=%fused_computation.46 | loop fusion | flops 1835008 | bytes 1835008 | tf_op jit(solution)/shard_map/stack | solution.py:74
  224.1 1.9 gather_fusion.1
  226.7 18.6 %reduce-scatter.2.cloned.1.call-done = bf16[128,1792]{1,0:T(8,128)(2,1)} async-done(((bf16[512,1792]{1,0:T(8,128)(2,1)}), bf16[128,1792]{1,0:T(8,128)(2,1)}) %reduce-scatter.2.cloned.1.call-update) | async-done | bytes 458768 | tf_op jit(solution)/shard_map/reduce_scatter | solution.py:161
  245.3 1.9 fusion.31
  (73 shorter events, 20.0 us)
Async XLA Ops:
  7.2 5.3 %copy-start = (bf16[128,1792]{1,0:T(8,128)(2,1)S(1)}, bf16[128,1792]{1,0:T(8,128)(2,1)}, u32[]{:S(2)}) copy-start(bf16[128,1792]{1,0:T(8,128)(2,1)} %param.10) | copy-start | bytes 1376260
  7.2 5.5 %copy-start.5 = (f32[1792]{0:T(1024)S(1)}, f32[1792]{0:T(1024)}, u32[]{:S(2)}) copy-start(f32[1792]{0:T(1024)} %param.11) | copy-start | bytes 21508
  7.2 86.9 %all-gather.3.cloned.1.call-start = ((), (), s32[]{:S(2)}) async-start(), calls=%async_computation.4 | async-start | bytes 4257792 | tf_op jit(solution)/shard_map/all_gather | solution.py:80
  9.8 191.0 %all-gather.5.cloned.1.call-start = ((), (), s32[]{:S(2)}) async-start(), calls=%async_computation.5 | async-start | bytes 9934848 | tf_op jit(solution)/shard_map/all_gather | solution.py:80
  12.4 232.9 %reduce-scatter.2.cloned.1.call-start = ((), (), s32[]{:S(2)}) async-start(), calls=%async_computation.6 | async-start | bytes 2293760 | tf_op jit(solution)/shard_map/reduce_scatter | solution.py:161
  13.0 29.9 %copy-start.4 = (bf16[1,2,64,224]{3,2,1,0:T(8,128)(2,1)S(1)}, bf16[1,2,64,224]{3,2,1,0:T(8,128)(2,1)}, u32[]{:S(2)}) copy-start(bf16[1,2,64,224]{3,2,1,0:T(8,128)(2,1)} %param.18) | copy-start | bytes 172036
  13.0 31.7 %copy-start.7 = (f32[3,224]{1,0:T(4,128)S(1)}, f32[3,224]{1,0:T(4,128)}, u32[]{:S(2)}) copy-start(f32[3,224]{1,0:T(4,128)} %param.17) | copy-start | bytes 8068
  40.3 5.5 %collective-permute-start = (bf16[4,128,1792]{2,1,0:T(8,128)(2,1)S(1)}, bf16[4,128,1792]{2,1,0:T(8,128)(2,1)}, u32[]{:S(2)}, u32[]{:S(2)}) collective-permute-start(bf16[4,128,1792]{2,1,0:T(8,128)(2,1)S(1)} %all_to_all.15), channel_id=1, source_target_pairs={{0,1},{1,0},{2,3},{3,2},{4,5},{5,4},{6,7},{7,6},{8,9},{9,8},{10,11... | collective-permute-start | bytes 5505032 | tf_op jit(solution)/shard_map/ppermute | solution.py:90
  44.5 64.3 %copy-start.3 = (bf16[1,64,224]{2,1,0:T(8,128)(2,1)}, bf16[1,64,224]{2,1,0:T(8,128)(2,1)S(1)}, u32[]{:S(2)}) copy-start(bf16[1,64,224]{2,1,0:T(8,128)(2,1)S(1)} %copy.75) | copy-start | bytes 86020
  127.9 1.4 copy-start.2
  133.0 6.7 %collective-permute-start.1 = (bf16[512,1792]{1,0:T(8,128)(2,1)S(1)}, bf16[512,1792]{1,0:T(8,128)(2,1)S(1)}, u32[]{:S(2)}, u32[]{:S(2)}) collective-permute-start(bf16[512,1792]{1,0:T(8,128)(2,1)S(1)} %convolution_convert_fusion), channel_id=1, source_target_pairs={{0,1},{1,0},{2,3},{3,2},{4,5},{5,4},{6,7},{7,6},{8,9},{9,8},{10,11... | collective-permute-start | bytes 5505032 | tf_op jit(solution)/shard_map/ppermute | solution.py:90
  168.0 0.7 copy-start.6
  193.3 6.2 %collective-permute-start.2 = (bf16[512,1792]{1,0:T(8,128)(2,1)S(1)}, bf16[512,1792]{1,0:T(8,128)(2,1)}, u32[]{:S(2)}, u32[]{:S(2)}) collective-permute-start(bf16[512,1792]{1,0:T(8,128)(2,1)S(1)} %bitcast.69), channel_id=1, source_target_pairs={{0,1},{1,0},{2,3},{3,2},{4,5},{5,4},{6,7},{7,6},{8,9},{9,8},{10,11... | collective-permute-start | bytes 5505032 | tf_op jit(solution)/shard_map/ppermute | solution.py:90
  200.7 7.0 %copy-start.9 = (bf16[1792,2688]{1,0:T(8,128)(2,1)S(1)}, bf16[1792,2688]{1,0:T(8,128)(2,1)}, u32[]{:S(2)}) copy-start(bf16[1792,2688]{1,0:T(8,128)(2,1)} %all-gather.5.cloned.1.call-done) | copy-start | bytes 28901380
  210.1 4.7 %collective-permute-start.3 = (bf16[512,1792]{1,0:T(8,128)(2,1)S(1)}, bf16[512,1792]{1,0:T(8,128)(2,1)S(1)}, u32[]{:S(2)}, u32[]{:S(2)}) collective-permute-start(bf16[512,1792]{1,0:T(8,128)(2,1)S(1)} %convolution_convert_fusion.2), channel_id=1, source_target_pairs={{0,1},{1,0},{2,3},{3,2},{4,5},{5,4},{6,7},{7,6},{8,9},{9,8},{10,11... | collective-permute-start | bytes 5505032 | tf_op jit(solution)/shard_map/ppermute | solution.py:90
  218.4 0.6 copy-start.8
  218.4 1.5 copy-start.1
Sparse Core Ops, SparseCore 0:
  11.2 82.8 all-gather.2
  96.7 104.0 all-gather.4
  218.5 26.7 reduce-scatter.1

commit v12 on v11

--- a/solution.py
+++ b/solution.py
@@ -154,9 +154,18 @@
     )
     flat = mine.reshape((-1,) + mine.shape[2:])
     theirs = core_swap(flat)
-    part_mine = mlp_rows(flat, ffn_all, down_t, ffn_width)
-    part_theirs = mlp_rows(theirs, ffn_all, down_t, ffn_width)
-    back = core_swap(part_theirs)
+    both = jnp.concatenate([theirs, flat], axis=0)
+    gate_up = jnp.dot(both, ffn_all, preferred_element_type=jnp.float32)
+    activated = (jax.nn.silu(gate_up[:, :ffn_width]) * gate_up[:, ffn_width:]).astype(jnp.bfloat16)
+    n_rows = flat.shape[0]
+
+    def down_rows(a):
+        return lax.dot_general(
+            a, down_t, (((1,), (1,)), ((), ())), preferred_element_type=jnp.float32
+        ).astype(jnp.bfloat16)
+
+    back = core_swap(down_rows(activated[:n_rows]))
+    part_mine = down_rows(activated[n_rows:])
     pair = (part_mine.astype(jnp.float32) + back.astype(jnp.float32)).astype(jnp.bfloat16)
     ffn_part = lax.psum_scatter(pair, "tpx", scatter_dimension=0, tiled=True).astype(jnp.float32)
     layer_out = (residual.astype(jnp.float32) + ffn_part).astype(jnp.bfloat16)

time: 255 us -> 258 us (1.012)
  waiting for transfers between devices: 72.3 us -> 81.2 us
  local copies, waits for them, and re-layouts: 24.4 us -> 19.8 us
    all_gather x2, waiting for transfers between devices: 45.7 us -> 49.5 us  [gather_packed(): lax.all_gather(jnp.concatenate(pieces, axis=1), 'req', axis=0, tiled=True)]
    ppermute x4, waiting for transfers between devices: 7.95 us -> 11.3 us  [core_swap(): return lax.ppermute(x, 'tpc', [(0, 1), (1, 0)])]
    reshape x4, local copies, waits for them, and re-layouts: 5.13 us -> 2.54 us  [blocks(): lo = rows[:row_count].reshape(nb, window, head_count, head_size)]
    dot_general x4 -> x3, matrix products: 16.4 us -> 15.8 us  [the longest x1 10.3 us: local(): gate_up = jnp.dot(both, ffn_all, preferred_element_type=jnp.float32)]
  transfers between devices with their start and end apart: 7 -> 7, of which waited for: 6 -> 7; matrix products, arithmetic and copies ran while one was open for 24% -> 20% of each run, Pallas kernels for 0% -> 0%
where the time goes in v12:
time: 258 us
  waiting for transfers between devices  81.2 us (31%)
  blocking collectives  78 us (30%)
  matrix products  38.2 us (15%)
  local copies, waits for them, and re-layouts  19.8 us (8%)
  other arithmetic  16.4 us (6%)
  between operations  14.8 us (6%)
  starting transfers between devices  9.34 us (4%)
    all_gather x2, waiting for transfers between devices, gather_packed(): lax.all_gather(jnp.concatenate(pieces, axis=1), 'req', axis=0, tiled=True)  49.5 us
    all_to_all x1, blocking collectives, local(): lax.all_to_all(jnp.tile(normed(tokens, norm_gain)[None], (nxt, 1, 1)), 't...  27.3 us
    all_to_all x1, blocking collectives, local(): lax.all_to_all(pair.reshape((nx, -1) + pair.shape[1:]), 'tpx', 0, 0, tile...  26.5 us
    all_to_all x1, blocking collectives, local(): lax.all_to_all(jnp.tile(normed(residual, ffn_gain)[None], (nx, 1, 1)), 't...  24.2 us
    reduce_scatter x1, waiting for transfers between devices, local(): lax.psum_scatter(pair, 'tpx', scatter_dimension=0, tiled=True)  20.4 us
    ppermute x4, waiting for transfers between devices, core_swap(): return lax.ppermute(x, 'tpc', [(0, 1), (1, 0)])  11.3 us
    dot_general x1, matrix products, local(): gate_up = jnp.dot(both, ffn_all, preferred_element_type=jnp.float32)  10.3 us
    ppermute x4, starting transfers between devices, core_swap(): return lax.ppermute(x, 'tpc', [(0, 1), (1, 0)])  9.22 us
  transfers between devices with their start and end apart: 7, of which 7 were waited for; matrix products, arithmetic and copies ran while one was open for 20% of the time, Pallas kernels for 0%

profile of v12, /device:TPU:1, one launch (start us, length us, event | category | flops | bytes accessed | tf_op | source)
XLA Modules:
  0.0 257.7 jit_solution(6405352428845010643)
XLA Ops:
  8.3 1.4 pad_maximum_fusion.5
  10.8 1.7 pad_maximum_fusion.4
  13.0 27.3 %all_to_all.15 = bf16[4,128,1792]{2,1,0:T(8,128)(2,1)S(1)} all-to-all(bf16[4,128,1792]{2,1,0:T(8,128)(2,1)S(1)} %tile.4), channel_id=1, replica_groups=mesh['req'=32,'tpx'=4,'tpc'=2] {'tpx'}, dimensions={0} | all-to-all | bytes 3670016 | tf_op jit(solution)/shard_map/all_to_all | solution.py:120
  40.3 2.0 collective-permute-start
  45.8 1.7 select_bitcast_fusion.1
  47.6 2.1 pad_maximum_fusion
  49.7 44.5 %all-gather.3.cloned.1.call-done = bf16[1792,1120]{1,0:T(8,128)(2,1)} async-done(((bf16[56,1120]{1,0:T(8,128)(2,1)}), bf16[1792,1120]{1,0:T(8,128)(2,1)}) %all-gather.3.cloned.1.call-update) | async-done | bytes 4014096 | tf_op jit(solution)/shard_map/all_gather | solution.py:80
  94.1 6.6 %fusion.13 = bf16[1024,896]{0,1:T(8,128)(2,1)S(1)} fusion(bf16[1024,1792]{1,0:T(8,128)(2,1)} %bitcast.65, bf16[1792,1120]{1,0:T(8,128)(2,1)} %all-gather.3.cloned.1.call-done), kind=kOutput, calls=%fused_computation.24 | convolution fusion | flops 3289251840 | bytes 8716288 | tf_op jit(solution)/shard_map/dot_general | solution.py:130
  100.7 1.4 slice_bitcast_fusion
  104.0 1.5 copy.32
  105.4 1.2 copy.33
  107.7 2.5 reshape.291
  111.9 2.8 %fusion.65 = f32[16,2,64]{2,1,0:T(2,128)S(1)} fusion(bf16[16,64,2,112]{1,3,2,0:T(8,128)(2,1)} %copy.39, bf16[16,64,2,112]{1,3,2,0:T(8,128)(2,1)S(1)} %copy.38, bf16[16,64,2,112]{1,0,3,2:T(8,128)(2,1)} %reshape.291, pred[16,64,128]{2,1,0:T(8,128)(4,1)S(1)} %copy-done.5), kind=kOutput, calls=%fused_computation.112 | convolution fusion | flops 61603968 | bytes 1515520 | tf_op jit(solution)/shard_map/sub | solution.py:40
  114.7 3.0 %fusion.18 = f32[16,2,64,128]{3,2,1,0:T(8,128)} fusion(bf16[16,64,2,112]{1,3,2,0:T(8,128)(2,1)S(1)} %copy-done.1, bf16[16,64,2,112]{1,3,2,0:T(8,128)(2,1)S(1)} %copy.38, bf16[16,64,2,112]{1,0,3,2:T(8,128)(2,1)} %reshape.291, pred[16,64,128]{2,1,0:T(8,128)(4,1)S(1)} %copy-done.5), kind=kOutput, calls=%fused_computation.34 | convolution fusion | flops 61079552 | bytes 2555904 | tf_op jit(solution)/shard_map/bqhd,bkhd->bhqk/dot_general | solution.py:32
  117.8 6.3 %convolution_bitcast_fusion = f32[16,64,2,112]{3,1,2,0:T(8,128)S(1)} fusion(bf16[16,64,2,112]{1,3,2,0:T(8,128)(2,1)} %copy.33, bf16[16,64,2,112]{1,3,2,0:T(8,128)(2,1)} %copy.32, f32[16,2,64]{2,1,0:T(2,128)S(1)} %fusion.65, f32[16,2,64,128]{3,2,1,0:T(8,128)} %fusion.18), kind=kOutput, calls=%fused_computation.35 | convolution fusion | flops 61343872 | bytes 2891776 | tf_op jit(solution)/shard_map/bhqk,bkhd->bqhd/dot_general | solution.py:42
  125.7 1.5 fusion.22
  127.3 1.9 convolution_convert_fusion
  129.1 3.4 %collective-permute-start.1 = (bf16[512,1792]{1,0:T(8,128)(2,1)S(1)}, bf16[512,1792]{1,0:T(8,128)(2,1)S(1)}, u32[]{:S(2)}, u32[]{:S(2)}) collective-permute-start(bf16[512,1792]{1,0:T(8,128)(2,1)S(1)} %convolution_convert_fusion), channel_id=1, source_target_pairs={{0,1},{1,0},{2,3},{3,2},{4,5},{5,4},{6,7},{7,6},{8,9},{9,8},{10,11... | collective-permute-start | bytes 5505032 | tf_op jit(solution)/shard_map/ppermute | solution.py:90
  132.5 3.4 %collective-permute-done.1 = bf16[512,1792]{1,0:T(8,128)(2,1)S(1)} collective-permute-done((bf16[512,1792]{1,0:T(8,128)(2,1)S(1)}, bf16[512,1792]{1,0:T(8,128)(2,1)S(1)}, u32[]{:S(2)}, u32[]{:S(2)}) %collective-permute-start.1) | collective-permute-done | bytes 1835040 | tf_op jit(solution)/shard_map/ppermute | solution.py:90
  135.9 1.9 add_convert_fusion.1
  137.8 26.5 %all_to_all.16 = bf16[4,128,1792]{2,1,0:T(8,128)(2,1)S(1)} all-to-all(bf16[4,128,1792]{2,1,0:T(8,128)(2,1)S(1)} %bitcast.64), channel_id=1, replica_groups=mesh['req'=32,'tpx'=4,'tpc'=2] {'tpx'}, dimensions={0} | all-to-all | bytes 3670016 | tf_op jit(solution)/shard_map/all_to_all | solution.py:148
  165.3 24.2 %all_to_all.17 = bf16[4,128,1792]{2,1,0:T(8,128)(2,1)S(1)} all-to-all(bf16[4,128,1792]{2,1,0:T(8,128)(2,1)S(1)} %tile.5), channel_id=1, replica_groups=mesh['req'=32,'tpx'=4,'tpc'=2] {'tpx'}, dimensions={0} | all-to-all | bytes 3670016 | tf_op jit(solution)/shard_map/all_to_all | solution.py:152
  189.5 2.7 %collective-permute-start.2 = (bf16[512,1792]{1,0:T(8,128)(2,1)S(1)}, bf16[512,1792]{1,0:T(8,128)(2,1)}, u32[]{:S(2)}, u32[]{:S(2)}) collective-permute-start(bf16[512,1792]{1,0:T(8,128)(2,1)S(1)} %bitcast.67), channel_id=1, source_target_pairs={{0,1},{1,0},{2,3},{3,2},{4,5},{5,4},{6,7},{7,6},{8,9},{9,8},{10,11... | collective-permute-start | bytes 5505032 | tf_op jit(solution)/shard_map/ppermute | solution.py:90
  192.2 3.5 %collective-permute-done.2 = bf16[512,1792]{1,0:T(8,128)(2,1)} collective-permute-done((bf16[512,1792]{1,0:T(8,128)(2,1)S(1)}, bf16[512,1792]{1,0:T(8,128)(2,1)}, u32[]{:S(2)}, u32[]{:S(2)}) %collective-permute-start.2) | collective-permute-done | bytes 1835040 | tf_op jit(solution)/shard_map/ppermute | solution.py:90
  195.7 5.0 %all-gather.5.cloned.1.call-done = bf16[1792,2688]{1,0:T(8,128)(2,1)} async-done(((bf16[56,2688]{1,0:T(8,128)(2,1)}), bf16[1792,2688]{1,0:T(8,128)(2,1)}) %all-gather.5.cloned.1.call-update) | async-done | bytes 9633808 | tf_op jit(solution)/shard_map/all_gather | solution.py:80
  200.8 10.3 %fusion.1 = f32[1024,1792]{1,0:T(8,128)S(1)} fusion(bf16[1792,2688]{1,0:T(8,128)(2,1)} %all-gather.5.cloned.1.call-done, bf16[512,1792]{1,0:T(8,128)(2,1)S(1)} %bitcast.68, bf16[512,1792]{1,0:T(8,128)(2,1)} %collective-permute-done.2), kind=kOutput, calls=%fused_computation.3 | convolution fusion | flops 6584008704 | bytes 17432576 | tf_op jit(solution)/shard_map/dot_general | solution.py:158
  212.1 2.1 convolution_convert_fusion.2
  215.4 3.4 %collective-permute-done.3 = bf16[512,1792]{1,0:T(8,128)(2,1)S(1)} collective-permute-done((bf16[512,1792]{1,0:T(8,128)(2,1)S(1)}, bf16[512,1792]{1,0:T(8,128)(2,1)S(1)}, u32[]{:S(2)}, u32[]{:S(2)}) %collective-permute-start.3) | collective-permute-done | bytes 1835040 | tf_op jit(solution)/shard_map/ppermute | solution.py:90
  218.8 3.4 %add_convert_fusion = bf16[512,1792]{1,0:T(8,128)(2,1)} fusion(bf16[512,1792]{1,0:T(8,128)(2,1)S(1)} %collective-permute-done.3, bf16[1792,2688]{1,0:T(8,128)(2,1)S(1)} %copy-done.10, bf16[1024,896]{1,0:T(8,128)(2,1)S(1)} %fusion.3), kind=kOutput, calls=%fused_computation.11 | convolution fusion | flops 1648754688 | bytes 7798784 | tf_op jit(solution)/shard_map/dot_general | solution.py:163
  224.9 2.6 %pad_maximum_fusion.1 = bf16[2,1024,224]{2,0,1:T(2,128)(2,1)S(1)} fusion(bf16[1,1024,224]{2,0,1:T(2,128)(2,1)S(1)} %copy.47, bf16[1,1024,224]{2,0,1:T(2,128)(2,1)S(1)} %copy.46), kind=kLoop, calls=%fused_computation.45 | loop fusion | flops 1835008 | bytes 1835008 | tf_op jit(solution)/shard_map/stack | solution.py:74
  228.9 20.4 %reduce-scatter.2.cloned.1.call-done = bf16[128,1792]{1,0:T(8,128)(2,1)} async-done(((bf16[512,1792]{1,0:T(8,128)(2,1)}), bf16[128,1792]{1,0:T(8,128)(2,1)}) %reduce-scatter.2.cloned.1.call-update) | async-done | bytes 458768 | tf_op jit(solution)/shard_map/reduce_scatter | solution.py:170
  249.3 1.9 fusion.31
  (75 shorter events, 19.0 us)
Async XLA Ops:
  7.2 5.3 %copy-start = (bf16[128,1792]{1,0:T(8,128)(2,1)S(1)}, bf16[128,1792]{1,0:T(8,128)(2,1)}, u32[]{:S(2)}) copy-start(bf16[128,1792]{1,0:T(8,128)(2,1)} %param.10) | copy-start | bytes 1376260
  7.2 5.5 %copy-start.7 = (f32[1792]{0:T(1024)S(1)}, f32[1792]{0:T(1024)}, u32[]{:S(2)}) copy-start(f32[1792]{0:T(1024)} %param.11) | copy-start | bytes 21508
  7.2 86.9 %all-gather.3.cloned.1.call-start = ((), (), s32[]{:S(2)}) async-start(), calls=%async_computation.4 | async-start | bytes 4257792 | tf_op jit(solution)/shard_map/all_gather | solution.py:80
  9.8 191.0 %all-gather.5.cloned.1.call-start = ((), (), s32[]{:S(2)}) async-start(), calls=%async_computation.5 | async-start | bytes 9934848 | tf_op jit(solution)/shard_map/all_gather | solution.py:80
  12.4 236.8 %reduce-scatter.2.cloned.1.call-start = ((), (), s32[]{:S(2)}) async-start(), calls=%async_computation.6 | async-start | bytes 2293760 | tf_op jit(solution)/shard_map/reduce_scatter | solution.py:170
  13.0 29.9 %copy-start.6 = (bf16[1,2,64,224]{3,2,1,0:T(8,128)(2,1)S(1)}, bf16[1,2,64,224]{3,2,1,0:T(8,128)(2,1)}, u32[]{:S(2)}) copy-start(bf16[1,2,64,224]{3,2,1,0:T(8,128)(2,1)} %param.18) | copy-start | bytes 172036
  13.0 31.1 %copy-start.9 = (f32[3,224]{1,0:T(4,128)S(1)}, f32[3,224]{1,0:T(4,128)}, u32[]{:S(2)}) copy-start(f32[3,224]{1,0:T(4,128)} %param.17) | copy-start | bytes 8068
  40.3 5.5 %collective-permute-start = (bf16[4,128,1792]{2,1,0:T(8,128)(2,1)S(1)}, bf16[4,128,1792]{2,1,0:T(8,128)(2,1)}, u32[]{:S(2)}, u32[]{:S(2)}) collective-permute-start(bf16[4,128,1792]{2,1,0:T(8,128)(2,1)S(1)} %all_to_all.15), channel_id=1, source_target_pairs={{0,1},{1,0},{2,3},{3,2},{4,5},{5,4},{6,7},{7,6},{8,9},{9,8},{10,11... | collective-permute-start | bytes 5505032 | tf_op jit(solution)/shard_map/ppermute | solution.py:90
  104.0 2.7 %copy-start.3 = (bf16[1024,1,224]{0,2,1:T(8,128)(2,1)S(1)}, bf16[1024,1,224]{0,2,1:T(8,128)(2,1)}, u32[]{:S(2)}) copy-start(bf16[1024,1,224]{0,2,1:T(8,128)(2,1)} %get-tuple-element.15) | copy-start | bytes 1376260
  105.4 4.7 %copy-start.4 = (bf16[1024,1,224]{0,2,1:T(8,128)(2,1)S(1)}, bf16[1024,1,224]{0,2,1:T(8,128)(2,1)}, u32[]{:S(2)}) copy-start(bf16[1024,1,224]{0,2,1:T(8,128)(2,1)} %get-tuple-element.13) | copy-start | bytes 1376260
  107.7 4.2 %copy-start.5 = (pred[16,64,128]{2,1,0:T(8,128)(4,1)S(1)}, pred[16,64,128]{2,1,0:T(8,128)(4,1)}, u32[]{:S(2)}) copy-start(pred[16,64,128]{2,1,0:T(8,128)(4,1)} %broadcast_and_fusion) | copy-start | bytes 393220
  111.9 2.8 %copy-start.1 = (bf16[16,64,2,112]{1,3,2,0:T(8,128)(2,1)S(1)}, bf16[16,64,2,112]{1,3,2,0:T(8,128)(2,1)}, u32[]{:S(2)}) copy-start(bf16[16,64,2,112]{1,3,2,0:T(8,128)(2,1)} %copy.39) | copy-start | bytes 1376260
  129.1 6.8 %collective-permute-start.1 = (bf16[512,1792]{1,0:T(8,128)(2,1)S(1)}, bf16[512,1792]{1,0:T(8,128)(2,1)S(1)}, u32[]{:S(2)}, u32[]{:S(2)}) collective-permute-start(bf16[512,1792]{1,0:T(8,128)(2,1)S(1)} %convolution_convert_fusion), channel_id=1, source_target_pairs={{0,1},{1,0},{2,3},{3,2},{4,5},{5,4},{6,7},{7,6},{8,9},{9,8},{10,11... | collective-permute-start | bytes 5505032 | tf_op jit(solution)/shard_map/ppermute | solution.py:90
  164.3 0.7 copy-start.8
  189.5 6.2 %collective-permute-start.2 = (bf16[512,1792]{1,0:T(8,128)(2,1)S(1)}, bf16[512,1792]{1,0:T(8,128)(2,1)}, u32[]{:S(2)}, u32[]{:S(2)}) collective-permute-start(bf16[512,1792]{1,0:T(8,128)(2,1)S(1)} %bitcast.67), channel_id=1, source_target_pairs={{0,1},{1,0},{2,3},{3,2},{4,5},{5,4},{6,7},{7,6},{8,9},{9,8},{10,11... | collective-permute-start | bytes 5505032 | tf_op jit(solution)/shard_map/ppermute | solution.py:90
  200.8 11.3 %copy-start.10 = (bf16[1792,2688]{1,0:T(8,128)(2,1)S(1)}, bf16[1792,2688]{1,0:T(8,128)(2,1)}, u32[]{:S(2)}) copy-start(bf16[1792,2688]{1,0:T(8,128)(2,1)} %all-gather.5.cloned.1.call-done) | copy-start | bytes 28901380
  214.2 4.6 %collective-permute-start.3 = (bf16[512,1792]{1,0:T(8,128)(2,1)S(1)}, bf16[512,1792]{1,0:T(8,128)(2,1)S(1)}, u32[]{:S(2)}, u32[]{:S(2)}) collective-permute-start(bf16[512,1792]{1,0:T(8,128)(2,1)S(1)} %convolution_convert_fusion.2), channel_id=1, source_target_pairs={{0,1},{1,0},{2,3},{3,2},{4,5},{5,4},{6,7},{7,6},{8,9},{9,8},{10,11... | collective-permute-start | bytes 5505032 | tf_op jit(solution)/shard_map/ppermute | solution.py:90
  222.2 1.0 copy-start.2
Sparse Core Ops, SparseCore 0:
  11.2 82.8 all-gather.2
  96.7 104.0 all-gather.4
  222.4 26.8 reduce-scatter.1

commit v13 on v11

--- a/solution.py
+++ b/solution.py
@@ -158,7 +158,12 @@
     part_theirs = mlp_rows(theirs, ffn_all, down_t, ffn_width)
     back = core_swap(part_theirs)
     pair = (part_mine.astype(jnp.float32) + back.astype(jnp.float32)).astype(jnp.bfloat16)
-    ffn_part = lax.psum_scatter(pair, "tpx", scatter_dimension=0, tiled=True).astype(jnp.float32)
+    cols = pair.shape[1] // 2
+    on_sc = lax.psum_scatter(pair[:, :cols], "tpx", scatter_dimension=0, tiled=True)
+    by_a2a = lax.all_to_all(pair[:, cols:].reshape((nx, -1, cols)), "tpx", 0, 0, tiled=True)
+    ffn_part = jnp.concatenate(
+        [on_sc.astype(jnp.float32), by_a2a.astype(jnp.float32).sum(axis=0)], axis=1
+    )
     layer_out = (residual.astype(jnp.float32) + ffn_part).astype(jnp.bfloat16)
     return (layer_out, renewed[None])
 

time: 255 us -> 254 us (level)
  waiting for transfers between devices: 72.3 us -> 66.3 us
  starting transfers between devices: 9.25 us -> 13.9 us
    reduce_scatter x1, waiting for transfers between devices: 18.6 us -> 0.95 us  [local(): lax.psum_scatter(pair[:, :cols], 'tpx', scatter_dimension=0, tiled=True)]
    all_to_all x0 -> x1, waiting for transfers between devices: none -> 11.7 us  [local(): lax.all_to_all(pair[:, cols:].reshape((nx, -1, cols)), 'tpx', 0, 0, tiled...]
    all_to_all x0 -> x1, starting transfers between devices: none -> 4.63 us  [local(): lax.all_to_all(pair[:, cols:].reshape((nx, -1, cols)), 'tpx', 0, 0, tiled...]
  transfers between devices with their start and end apart: 7 -> 8, of which waited for: 6 -> 7; matrix products, arithmetic and copies ran while one was open for 24% -> 25% of each run, Pallas kernels for 0% -> 0%
where the time goes in v13:
time: 254 us; the launch traced here: 253 us
  blocking collectives  78 us (31%)
  waiting for transfers between devices  66.3 us (26%)
  matrix products  37.2 us (15%)
  local copies, waits for them, and re-layouts  25.3 us (10%)
  other arithmetic  17.8 us (7%)
  between operations  14.8 us (6%)
  starting transfers between devices  13.9 us (5%)
    all_gather x2, waiting for transfers between devices, gather_packed(): lax.all_gather(jnp.concatenate(pieces, axis=1), 'req', axis=0, tiled=True)  45.7 us
    all_to_all x1, blocking collectives, local(): lax.all_to_all(jnp.tile(normed(tokens, norm_gain)[None], (nxt, 1, 1)), 't...  27.3 us
    all_to_all x1, blocking collectives, local(): lax.all_to_all(pair.reshape((nx, -1) + pair.shape[1:]), 'tpx', 0, 0, tile...  26.5 us
    all_to_all x1, blocking collectives, local(): lax.all_to_all(jnp.tile(normed(residual, ffn_gain)[None], (nx, 1, 1)), 't...  24.2 us
    all_to_all x1, waiting for transfers between devices, local(): lax.all_to_all(pair[:, cols:].reshape((nx, -1, cols)), 'tpx', 0, 0, tiled...  11.7 us
    dot_general x2, matrix products, mlp_rows(): gate_up = jnp.dot(rows, ffn_all, preferred_element_type=jnp.float32)  10.5 us
    ppermute x4, starting transfers between devices, core_swap(): return lax.ppermute(x, 'tpc', [(0, 1), (1, 0)])  9.13 us
    ppermute x4, waiting for transfers between devices, core_swap(): return lax.ppermute(x, 'tpc', [(0, 1), (1, 0)])  7.95 us
  transfers between devices with their start and end apart: 8, of which 7 were waited for; matrix products, arithmetic and copies ran while one was open for 25% of the time, Pallas kernels for 0%

profile of v13, /device:TPU:1, one launch (start us, length us, event | category | flops | bytes accessed | tf_op | source)
XLA Modules:
  0.0 253.3 jit_solution(17294180878208792725)
XLA Ops:
  8.3 1.4 pad_maximum_fusion.5
  10.8 1.6 pad_maximum_fusion.4
  13.0 27.3 %all_to_all.20 = bf16[4,128,1792]{2,1,0:T(8,128)(2,1)S(1)} all-to-all(bf16[4,128,1792]{2,1,0:T(8,128)(2,1)S(1)} %tile.4), channel_id=1, replica_groups=mesh['req'=32,'tpx'=4,'tpc'=2] {'tpx'}, dimensions={0} | all-to-all | bytes 3670016 | tf_op jit(solution)/shard_map/all_to_all | solution.py:120
  40.3 2.0 collective-permute-start
  45.8 1.7 select_bitcast_fusion.1
  47.6 2.1 pad_maximum_fusion
  49.6 44.5 %all-gather.3.cloned.1.call-done = bf16[1792,1120]{1,0:T(8,128)(2,1)} async-done(((bf16[56,1120]{1,0:T(8,128)(2,1)}), bf16[1792,1120]{1,0:T(8,128)(2,1)}) %all-gather.3.cloned.1.call-update) | async-done | bytes 4014096 | tf_op jit(solution)/shard_map/all_gather | solution.py:80
  94.1 6.6 %fusion.13 = bf16[1024,896]{0,1:T(8,128)(2,1)S(1)} fusion(bf16[1024,1792]{1,0:T(8,128)(2,1)} %bitcast.68, bf16[1792,1120]{1,0:T(8,128)(2,1)} %all-gather.3.cloned.1.call-done), kind=kOutput, calls=%fused_computation.26 | convolution fusion | flops 3289251840 | bytes 8716288 | tf_op jit(solution)/shard_map/dot_general | solution.py:130
  103.9 2.6 %reshape.295 = bf16[16,64,2,112]{1,0,3,2:T(8,128)(2,1)} reshape(bf16[1024,1,224]{0,2,1:T(8,128)(2,1)} %get-tuple-element.14) | data formatting | bytes 917504 | tf_op jit(solution)/shard_map/reshape;reshape;squeeze | solution.py:22
  109.7 2.2 reshape.267
  111.9 2.1 copy.32
  114.1 2.1 copy.33
  116.2 2.4 fusion.69
  118.7 3.0 %fusion.18 = f32[16,2,64,128]{3,2,1,0:T(8,128)} fusion(bf16[16,64,2,112]{1,3,2,0:T(8,128)(2,1)S(1)} %copy.39, bf16[16,64,2,112]{1,3,2,0:T(8,128)(2,1)S(1)} %copy.38, bf16[16,64,2,112]{1,0,3,2:T(8,128)(2,1)} %reshape.295, pred[16,64,128]{2,1,0:T(8,128)(4,1)S(1)} %broadcast_and_fusion), kind=kOutput, calls=%fused_computation.36 | convolution fusion | flops 61079552 | bytes 2555904 | tf_op jit(solution)/shard_map/bqhd,bkhd->bhqk/dot_general | solution.py:32
  121.7 6.3 %convolution_bitcast_fusion = f32[16,64,2,112]{3,1,2,0:T(8,128)S(1)} fusion(bf16[16,64,2,112]{1,3,2,0:T(8,128)(2,1)} %copy.33, bf16[16,64,2,112]{1,3,2,0:T(8,128)(2,1)} %copy.32, f32[16,2,64]{2,1,0:T(2,128)S(1)} %fusion.69, f32[16,2,64,128]{3,2,1,0:T(8,128)} %fusion.18), kind=kOutput, calls=%fused_computation.37 | convolution fusion | flops 61343872 | bytes 2891776 | tf_op jit(solution)/shard_map/bhqk,bkhd->bqhd/dot_general | solution.py:42
  131.1 1.9 convolution_convert_fusion
  133.0 3.3 %collective-permute-start.1 = (bf16[512,1792]{1,0:T(8,128)(2,1)S(1)}, bf16[512,1792]{1,0:T(8,128)(2,1)S(1)}, u32[]{:S(2)}, u32[]{:S(2)}) collective-permute-start(bf16[512,1792]{1,0:T(8,128)(2,1)S(1)} %convolution_convert_fusion), channel_id=1, source_target_pairs={{0,1},{1,0},{2,3},{3,2},{4,5},{5,4},{6,7},{7,6},{8,9},{9,8},{10,11... | collective-permute-start | bytes 5505032 | tf_op jit(solution)/shard_map/ppermute | solution.py:90
  136.3 3.4 %collective-permute-done.1 = bf16[512,1792]{1,0:T(8,128)(2,1)S(1)} collective-permute-done((bf16[512,1792]{1,0:T(8,128)(2,1)S(1)}, bf16[512,1792]{1,0:T(8,128)(2,1)S(1)}, u32[]{:S(2)}, u32[]{:S(2)}) %collective-permute-start.1) | collective-permute-done | bytes 1835040 | tf_op jit(solution)/shard_map/ppermute | solution.py:90
  139.7 1.9 add_convert_fusion.1
  141.6 26.5 %all_to_all.21 = bf16[4,128,1792]{2,1,0:T(8,128)(2,1)S(1)} all-to-all(bf16[4,128,1792]{2,1,0:T(8,128)(2,1)S(1)} %bitcast.67), channel_id=1, replica_groups=mesh['req'=32,'tpx'=4,'tpc'=2] {'tpx'}, dimensions={0} | all-to-all | bytes 3670016 | tf_op jit(solution)/shard_map/all_to_all | solution.py:148
  169.1 24.2 %all_to_all.22 = bf16[4,128,1792]{2,1,0:T(8,128)(2,1)S(1)} all-to-all(bf16[4,128,1792]{2,1,0:T(8,128)(2,1)S(1)} %tile.5), channel_id=1, replica_groups=mesh['req'=32,'tpx'=4,'tpc'=2] {'tpx'}, dimensions={0} | all-to-all | bytes 3670016 | tf_op jit(solution)/shard_map/all_to_all | solution.py:152
  193.3 2.7 %collective-permute-start.2 = (bf16[512,1792]{1,0:T(8,128)(2,1)S(1)}, bf16[512,1792]{1,0:T(8,128)(2,1)}, u32[]{:S(2)}, u32[]{:S(2)}) collective-permute-start(bf16[512,1792]{1,0:T(8,128)(2,1)S(1)} %bitcast.70), channel_id=1, source_target_pairs={{0,1},{1,0},{2,3},{3,2},{4,5},{5,4},{6,7},{7,6},{8,9},{9,8},{10,11... | collective-permute-start | bytes 5505032 | tf_op jit(solution)/shard_map/ppermute | solution.py:90
  196.0 3.5 %collective-permute-done.2 = bf16[512,1792]{1,0:T(8,128)(2,1)} collective-permute-done((bf16[512,1792]{1,0:T(8,128)(2,1)S(1)}, bf16[512,1792]{1,0:T(8,128)(2,1)}, u32[]{:S(2)}, u32[]{:S(2)}) %collective-permute-start.2) | collective-permute-done | bytes 1835040 | tf_op jit(solution)/shard_map/ppermute | solution.py:90
  200.7 7.0 %fusion.1 = f32[512,1792]{1,0:T(8,128)S(1)} fusion(bf16[512,1792]{1,0:T(8,128)(2,1)} %collective-permute-done.2, bf16[1792,2688]{1,0:T(8,128)(2,1)} %all-gather.5.cloned.1.call-done), kind=kOutput, calls=%fused_computation.3 | convolution fusion | flops 3288334336 | bytes 11927552 | tf_op jit(solution)/shard_map/dot_general | solution.py:94
  207.8 2.3 convolution_convert_fusion.2
  211.3 3.5 %fusion.3 = f32[512,1792]{1,0:T(8,128)S(1)} fusion(bf16[512,1792]{1,0:T(8,128)(2,1)S(1)} %bitcast.71, bf16[1792,2688]{1,0:T(8,128)(2,1)S(1)} %copy-done.9), kind=kOutput, calls=%fused_computation.5 | convolution fusion | flops 3288334336 | bytes 11927552 | tf_op jit(solution)/shard_map/dot_general | solution.py:94
  214.8 2.3 add_convert_fusion
  217.1 1.4 fusion.66
  218.6 4.6 %all-to-all-start.3 = ((bf16[4,128,896]{2,1,0:T(8,128)(2,1)}), bf16[4,128,896]{2,1,0:T(8,128)(2,1)}, u32[]{:S(2)}, u32[]{:S(2)}) async-start(bf16[4,128,896]{2,1,0:T(8,128)(2,1)} %bitcast.22), calls=%async_computation.4 | async-start | bytes 1835008 | tf_op jit(solution)/shard_map/all_to_all | solution.py:163
  224.9 3.4 %pad_maximum_fusion.1 = bf16[2,1024,224]{2,0,1:T(2,128)(2,1)} fusion(bf16[1,1024,224]{2,0,1:T(2,128)(2,1)S(1)} %copy.47, bf16[1,1024,224]{2,0,1:T(2,128)(2,1)S(1)} %copy.46), kind=kLoop, calls=%fused_computation.47 | loop fusion | flops 1835008 | bytes 1835008 | tf_op jit(solution)/shard_map/stack | solution.py:74
  228.3 1.9 gather_fusion.1
  230.9 11.7 %all-to-all-done.3 = bf16[4,128,896]{2,1,0:T(8,128)(2,1)} async-done(((bf16[4,128,896]{2,1,0:T(8,128)(2,1)}), bf16[4,128,896]{2,1,0:T(8,128)(2,1)}, u32[]{:S(2)}, u32[]{:S(2)}) %all-to-all-start.3) | async-done | bytes 917536 | tf_op jit(solution)/shard_map/all_to_all | solution.py:163
  (78 shorter events, 24.9 us)
Async XLA Ops:
  7.2 5.3 %copy-start = (bf16[128,1792]{1,0:T(8,128)(2,1)S(1)}, bf16[128,1792]{1,0:T(8,128)(2,1)}, u32[]{:S(2)}) copy-start(bf16[128,1792]{1,0:T(8,128)(2,1)} %param.10) | copy-start | bytes 1376260
  7.2 5.5 %copy-start.5 = (f32[1792]{0:T(1024)S(1)}, f32[1792]{0:T(1024)}, u32[]{:S(2)}) copy-start(f32[1792]{0:T(1024)} %param.11) | copy-start | bytes 21508
  7.2 86.9 %all-gather.3.cloned.1.call-start = ((), (), s32[]{:S(2)}) async-start(), calls=%async_computation.5 | async-start | bytes 4257792 | tf_op jit(solution)/shard_map/all_gather | solution.py:80
  9.8 191.0 %all-gather.5.cloned.1.call-start = ((), (), s32[]{:S(2)}) async-start(), calls=%async_computation.6 | async-start | bytes 9934848 | tf_op jit(solution)/shard_map/all_gather | solution.py:80
  12.4 232.5 %reduce-scatter.2.cloned.1.call-start = ((), (), s32[]{:S(2)}) async-start(), calls=%async_computation.7 | async-start | bytes 1146880 | tf_op jit(solution)/shard_map/reduce_scatter | solution.py:162
  13.0 29.9 %copy-start.4 = (bf16[1,2,64,224]{3,2,1,0:T(8,128)(2,1)S(1)}, bf16[1,2,64,224]{3,2,1,0:T(8,128)(2,1)}, u32[]{:S(2)}) copy-start(bf16[1,2,64,224]{3,2,1,0:T(8,128)(2,1)} %param.18) | copy-start | bytes 172036
  13.0 31.7 %copy-start.7 = (f32[3,224]{1,0:T(4,128)S(1)}, f32[3,224]{1,0:T(4,128)}, u32[]{:S(2)}) copy-start(f32[3,224]{1,0:T(4,128)} %param.17) | copy-start | bytes 8068
  40.3 5.5 %collective-permute-start = (bf16[4,128,1792]{2,1,0:T(8,128)(2,1)S(1)}, bf16[4,128,1792]{2,1,0:T(8,128)(2,1)}, u32[]{:S(2)}, u32[]{:S(2)}) collective-permute-start(bf16[4,128,1792]{2,1,0:T(8,128)(2,1)S(1)} %all_to_all.20), channel_id=1, source_target_pairs={{0,1},{1,0},{2,3},{3,2},{4,5},{5,4},{6,7},{7,6},{8,9},{9,8},{10,11... | collective-permute-start | bytes 5505032 | tf_op jit(solution)/shard_map/ppermute | solution.py:90
  44.5 64.3 %copy-start.3 = (bf16[1,64,224]{2,1,0:T(8,128)(2,1)}, bf16[1,64,224]{2,1,0:T(8,128)(2,1)S(1)}, u32[]{:S(2)}) copy-start(bf16[1,64,224]{2,1,0:T(8,128)(2,1)S(1)} %copy.75) | copy-start | bytes 86020
  128.0 1.4 copy-start.2
  133.0 6.7 %collective-permute-start.1 = (bf16[512,1792]{1,0:T(8,128)(2,1)S(1)}, bf16[512,1792]{1,0:T(8,128)(2,1)S(1)}, u32[]{:S(2)}, u32[]{:S(2)}) collective-permute-start(bf16[512,1792]{1,0:T(8,128)(2,1)S(1)} %convolution_convert_fusion), channel_id=1, source_target_pairs={{0,1},{1,0},{2,3},{3,2},{4,5},{5,4},{6,7},{7,6},{8,9},{9,8},{10,11... | collective-permute-start | bytes 5505032 | tf_op jit(solution)/shard_map/ppermute | solution.py:90
  168.1 0.7 copy-start.6
  193.3 6.2 %collective-permute-start.2 = (bf16[512,1792]{1,0:T(8,128)(2,1)S(1)}, bf16[512,1792]{1,0:T(8,128)(2,1)}, u32[]{:S(2)}, u32[]{:S(2)}) collective-permute-start(bf16[512,1792]{1,0:T(8,128)(2,1)S(1)} %bitcast.70), channel_id=1, source_target_pairs={{0,1},{1,0},{2,3},{3,2},{4,5},{5,4},{6,7},{7,6},{8,9},{9,8},{10,11... | collective-permute-start | bytes 5505032 | tf_op jit(solution)/shard_map/ppermute | solution.py:90
  200.7 7.0 %copy-start.9 = (bf16[1792,2688]{1,0:T(8,128)(2,1)S(1)}, bf16[1792,2688]{1,0:T(8,128)(2,1)}, u32[]{:S(2)}) copy-start(bf16[1792,2688]{1,0:T(8,128)(2,1)} %all-gather.5.cloned.1.call-done) | copy-start | bytes 28901380
  210.1 4.7 %collective-permute-start.3 = (bf16[512,1792]{1,0:T(8,128)(2,1)S(1)}, bf16[512,1792]{1,0:T(8,128)(2,1)S(1)}, u32[]{:S(2)}, u32[]{:S(2)}) collective-permute-start(bf16[512,1792]{1,0:T(8,128)(2,1)S(1)} %convolution_convert_fusion.2), channel_id=1, source_target_pairs={{0,1},{1,0},{2,3},{3,2},{4,5},{5,4},{6,7},{7,6},{8,9},{9,8},{10,11... | collective-permute-start | bytes 5505032 | tf_op jit(solution)/shard_map/ppermute | solution.py:90
  218.5 4.7 %copy-start.8 = (s32[64]{0:T(128)S(1)}, s32[64]{0:T(128)}, u32[]{:S(2)}) copy-start(s32[64]{0:T(128)} %get-tuple-element.26) | copy-start | bytes 772
  218.6 5.5 %copy-start.1 = (bf16[1,1024,224]{1,2,0:T(8,128)(2,1)S(1)}, bf16[1,1024,224]{1,2,0:T(8,128)(2,1)}, u32[]{:S(2)}) copy-start(bf16[1,1024,224]{1,2,0:T(8,128)(2,1)} %get-tuple-element.10) | copy-start | bytes 1376260
  218.6 24.0 %all-to-all-start.3 = ((bf16[4,128,896]{2,1,0:T(8,128)(2,1)}), bf16[4,128,896]{2,1,0:T(8,128)(2,1)}, u32[]{:S(2)}, u32[]{:S(2)}) async-start(bf16[4,128,896]{2,1,0:T(8,128)(2,1)} %bitcast.22), calls=%async_computation.4 | async-start | bytes 1835008 | tf_op jit(solution)/shard_map/all_to_all | solution.py:163
Sparse Core Ops, SparseCore 0:
  11.2 82.8 all-gather.2
  96.7 103.9 all-gather.4
  218.7 26.1 reduce-scatter.1
